TPU v7x, 128 devices: a whole 4x4x4 slice. The times are simulated.
128 devices in a mesh: row: 4 (over x_lo, core), col: 32 (over y, z, x_hi).
Axes of the slice: x: 4 (x_hi: 2, x_lo: 2; x = x_hi * 2 + x_lo), y: 4, z: 4, core: 2. Of those that a mesh axis runs over, the one named last changes fastest.
Arguments:
- prompt_tokens: bfloat16 [32768, 2048], P('col', 'row'), may hold values from -6 to 6
- decode_tokens: bfloat16 [32, 2048], P('col', 'row'), may hold values from -6 to 6
- norm_gain: float32 [2048], replicated, may hold values from 0.25 to 1.75
- norm_bias: float32 [2048], replicated, may hold values from -3 to 3
- project_weight: float32 [2048, 6144], P(('row', 'col')), may hold values from -0.25 to 0.25
- dense_weight: float32 [2048, 2048], P(('row', 'col')), may hold values from -0.125 to 0.125
- expand_weight: float32 [2048, 8192], P(('row', 'col')), may hold values from -0.125 to 0.125
- reduce_weight: float32 [2048, 8192], P(('row', 'col')), may hold values from -0.0625 to 0.0625
- key_cache: bfloat16 [32, 32, 262144], P('col', 'row'), may hold values from -15 to 15
- value_cache: bfloat16 [32, 32, 262144], P('col', 'row'), may hold values from -12 to 12
- prompt_lengths: int32 [64], P('col'), may hold values from 128 to 512, as said below
- cache_ages: int32 [32], replicated, may hold values from 1 to 4096, as said below
- slot_request: int32 [32], replicated, may hold values from 0 to 31, each once
Outputs:
- prompt_out: bfloat16 [32768, 2048], P('col', 'row')
- decoded: bfloat16 [32, 2048], P('col', 'row')
Inputs may be any that keep to these rules, and one draw needn't show every extreme that they name: `prompt_lengths`: tokens of a prompt at or beyond its length are padding; some prompt is full in every draw. `cache_ages`: cached positions 0 to age - 1 of a request are valid and its new token stands at position age; some request has exactly 4096. `slot_request`: a permutation of the requests.
All inputs are finite; a program needn't handle non-finite values.
Results may differ from a plain program's by a relative error of at most 0.012.
The roundings to bfloat16 on the way count: a program that leaves them out, or rounds other values in their place, can miss the bound.
Values may be sent and summed in bfloat16 or wider, within the bound.
No kernel may reach another device: no remote copies, remote signals or barrier semaphores. Data moves between devices by JAX's collectives and lax.ppermute only.
A program may use at most 192 MiB of HBM per device.

v0:
```python
import jax
import jax.numpy as jnp
from jax import lax
from jax.sharding import PartitionSpec as P

HD = 64
ROT = 32
PLEN = 512
CTX = 4096
KEY_BLOCK = 512


NEG = -1e30


def layer_norm(rows, gain, bias):
    values = rows.astype(jnp.float32)
    centre = jnp.mean(values, axis=-1, keepdims=True)
    centred = values - centre
    deviation = jnp.mean(centred * centred, axis=-1, keepdims=True)
    return (centred * lax.rsqrt(deviation + 1e-05) * gain + bias).astype(jnp.bfloat16)


def rotary(vectors, position):
    half_width = ROT // 2
    frequency = 10000.0 ** (-2.0 * jnp.arange(half_width).astype(jnp.float32) / ROT)
    angle = position.astype(jnp.float32)[..., None, None] * frequency
    cosine = jnp.cos(angle)
    sine_value = jnp.sin(angle)
    lower_part = vectors[..., :half_width]
    upper_part = vectors[..., half_width:ROT]
    return jnp.concatenate(
        [
            lower_part * cosine - upper_part * sine_value,
            upper_part * cosine + lower_part * sine_value,
            vectors[..., ROT:],
        ],
        axis=-1,
    )


def restore_rows(block, row_count, col_count):
    width = block.shape[1]
    shard_rows = block.shape[0] // (row_count * col_count)
    return (
        block.reshape(col_count, row_count, shard_rows, width)
        .transpose(1, 0, 2, 3)
        .reshape(row_count * col_count * shard_rows, width)
    )


def on_device(
    prompt_tokens,
    decode_tokens,
    norm_gain,
    norm_bias,
    project_weight,
    dense_weight,
    expand_weight,
    reduce_weight,
    key_cache,
    value_cache,
    prompt_lengths,
    cache_ages,
    slot_request,
):
    half_float = jnp.bfloat16
    row_count = lax.axis_size("row")
    col_count = lax.axis_size("col")
    regrouped = (
        lax.all_to_all(
            project_weight.astype(half_float), "row", split_axis=1, concat_axis=0, tiled=True
        ),
        lax.all_to_all(
            dense_weight.astype(half_float), "row", split_axis=1, concat_axis=0, tiled=True
        ),
        lax.all_to_all(
            expand_weight.astype(half_float), "row", split_axis=1, concat_axis=0, tiled=True
        ),
        lax.all_to_all(
            reduce_weight.astype(half_float), "row", split_axis=1, concat_axis=0, tiled=True
        ),
    )
    gathered = (
        lax.all_gather(regrouped[0], "col", axis=0, tiled=True),
        lax.all_gather(regrouped[1], "col", axis=0, tiled=True),
        lax.all_gather(regrouped[2], "col", axis=0, tiled=True),
        lax.all_gather(regrouped[3], "col", axis=0, tiled=True),
    )
    w_project, w_dense, w_expand, w_reduce = [
        restore_rows(piece, row_count, col_count) for piece in gathered
    ]
    prompt_full, decode_full = (
        lax.all_gather(prompt_tokens, "row", axis=1, tiled=True),
        lax.all_gather(decode_tokens, "row", axis=1, tiled=True),
    )
    rows_prompt = prompt_full.shape[0]
    slot_local = decode_full.shape[0]
    prompt_count = rows_prompt // PLEN
    heads_local = w_dense.shape[1] // HD
    total_slots = slot_request.shape[0]
    scale = HD ** (-0.5)
    joined = jnp.concatenate([prompt_full, decode_full], axis=0)
    normed = layer_norm(joined, norm_gain, norm_bias)
    merged = jnp.dot(normed, w_project, preferred_element_type=jnp.float32)
    hidden = jax.nn.gelu(
        jnp.dot(normed, w_expand, preferred_element_type=jnp.float32), approximate=True
    ).astype(half_float)
    mlp_part = lax.dot_general(
        hidden, w_reduce, (((1,), (1,)), ((), ())), preferred_element_type=jnp.float32
    )
    places = jnp.arange(PLEN, dtype=jnp.int32)

    def prompt_block(items):
        block, length = items
        queries = rotary(block[:, :, 0], places).astype(half_float)
        keys_rot = rotary(block[:, :, 1], places).astype(half_float)
        values = block[:, :, 2].astype(half_float)
        scores = (
            jnp.einsum("qhd,khd->hqk", queries, keys_rot, preferred_element_type=jnp.float32)
            * scale
        )
        allowed = (places[None, :] <= places[:, None]) & (places[None, :] < length)
        scores = jnp.where(allowed[None], scores, NEG)
        top = jnp.max(scores, axis=-1, keepdims=True)
        raised = jnp.exp(scores - top)
        probs = (raised / jnp.sum(raised, axis=-1, keepdims=True)).astype(half_float)
        mixed = jnp.einsum("hqk,khd->qhd", probs, values, preferred_element_type=jnp.float32)
        return mixed.astype(half_float).reshape(PLEN, heads_local * HD)

    prompt_blocks = merged[:rows_prompt].reshape(prompt_count, PLEN, heads_local, 3, HD)
    prompt_mixed = lax.map(prompt_block, (prompt_blocks, prompt_lengths)).reshape(
        rows_prompt, heads_local * HD
    )
    col_index = lax.axis_index("col")
    first_slot = col_index * slot_local
    local_ids = first_slot + jnp.arange(slot_local, dtype=jnp.int32)
    own_request = lax.dynamic_slice_in_dim(slot_request, first_slot, slot_local)
    all_ids = jnp.arange(total_slots, dtype=jnp.int32)
    slot_match = own_request[:, None] == all_ids[None, :]
    slot_age = jnp.sum(jnp.where(slot_match, cache_ages[None, :], 0), axis=1)
    decode_pieces = merged[rows_prompt:].reshape(slot_local, heads_local, 3, HD)
    query_new = rotary(decode_pieces[:, :, 0], slot_age).astype(half_float)
    key_new = rotary(decode_pieces[:, :, 1], slot_age).astype(half_float)
    value_new = decode_pieces[:, :, 2].astype(half_float)
    packed = jnp.stack([query_new, key_new, value_new], axis=2).reshape(
        slot_local, heads_local * 3 * HD
    )
    handed = lax.all_gather(packed, "col", axis=0, tiled=True)
    chooser = (slot_request[None, :] == local_ids[:, None]).astype(half_float)
    mine = jnp.dot(chooser, handed, preferred_element_type=jnp.float32).astype(half_float)
    mine = mine.reshape(slot_local, heads_local, 3, HD)
    query = mine[:, :, 0]
    own_key = mine[:, :, 1]
    own_value = mine[:, :, 2]
    local_ages = lax.dynamic_slice_in_dim(cache_ages, first_slot, slot_local)
    keys_local = key_cache.reshape(slot_local, heads_local, CTX, HD)
    values_local = value_cache.reshape(slot_local, heads_local, CTX, HD)
    block_count = CTX // KEY_BLOCK

    def score_block(step, held):
        start = step * KEY_BLOCK
        keys_block = lax.dynamic_slice_in_dim(keys_local, start, KEY_BLOCK, 2)
        block_scores = (
            jnp.einsum("shd,shtd->sht", query, keys_block, preferred_element_type=jnp.float32)
            * scale
        )
        key_places = start + jnp.arange(KEY_BLOCK, dtype=jnp.int32)
        block_scores = jnp.where(
            key_places[None, None, :] < local_ages[:, None, None], block_scores, NEG
        )
        return lax.dynamic_update_slice_in_dim(held, block_scores, start, 2)

    cache_scores = lax.fori_loop(
        0, block_count, score_block, jnp.full((slot_local, heads_local, CTX), NEG, jnp.float32)
    )
    own_score = jnp.sum(query.astype(jnp.float32) * own_key.astype(jnp.float32), axis=-1) * scale
    decode_top = jnp.maximum(jnp.max(cache_scores, axis=-1), own_score)
    cache_raised = jnp.exp(cache_scores - decode_top[:, :, None])
    own_raised = jnp.exp(own_score - decode_top)
    decode_total = jnp.sum(cache_raised, axis=-1) + own_raised
    cache_probs = (cache_raised / decode_total[:, :, None]).astype(half_float)
    own_prob = (own_raised / decode_total).astype(half_float)

    def value_block(step, running):
        start = step * KEY_BLOCK
        probs_block = lax.dynamic_slice_in_dim(cache_probs, start, KEY_BLOCK, 2)
        values_block = lax.dynamic_slice_in_dim(values_local, start, KEY_BLOCK, 2)
        return running + jnp.einsum(
            "sht,shtd->shd", probs_block, values_block, preferred_element_type=jnp.float32
        )

    start_value = own_prob.astype(jnp.float32)[:, :, None] * own_value.astype(jnp.float32)
    decode_sum = lax.fori_loop(0, block_count, value_block, start_value)
    decode_mixed = decode_sum.astype(half_float).reshape(slot_local, heads_local * HD)
    returned = lax.all_gather(decode_mixed, "col", axis=0, tiled=True)
    picker = slot_match.astype(half_float)
    decode_heads = jnp.dot(picker, returned, preferred_element_type=jnp.float32).astype(half_float)
    mixed_all = jnp.concatenate([prompt_mixed, decode_heads], axis=0)
    attn_part = lax.dot_general(
        mixed_all, w_dense, (((1,), (1,)), ((), ())), preferred_element_type=jnp.float32
    )
    attn_prompt, attn_decode = (
        lax.psum_scatter(attn_part[:rows_prompt], "row", scatter_dimension=1, tiled=True),
        lax.psum_scatter(attn_part[rows_prompt:], "row", scatter_dimension=1, tiled=True),
    )
    mlp_prompt, mlp_decode = (
        lax.psum_scatter(
            mlp_part[:rows_prompt].astype(jnp.bfloat16), "row", scatter_dimension=1, tiled=True
        ).astype(jnp.float32),
        lax.psum_scatter(
            mlp_part[rows_prompt:].astype(jnp.bfloat16), "row", scatter_dimension=1, tiled=True
        ).astype(jnp.float32),
    )
    summed_prompt = attn_prompt + mlp_prompt
    summed_decode = attn_decode + mlp_decode
    prompt_result = prompt_tokens.astype(jnp.float32) + summed_prompt
    decode_result = decode_tokens.astype(jnp.float32) + summed_decode
    return (prompt_result.astype(half_float), decode_result.astype(half_float))


def solution(mesh):
    in_specs = (
        P("col", "row"),
        P("col", "row"),
        P(),
        P(),
        P(("row", "col"), None),
        P(("row", "col"), None),
        P(("row", "col"), None),
        P(("row", "col"), None),
        P("col", "row", None),
        P("col", "row", None),
        P("col"),
        P(),
        P(),
    )
    out_specs = (P("col", "row"), P("col", "row"))
    return jax.shard_map(
        on_device, mesh=mesh, in_specs=in_specs, out_specs=out_specs, check_vma=False
    )
```

profile of v0, /device:TPU:1, one launch (start us, length us, event | category | flops | bytes accessed | tf_op | source)
XLA Modules:
  0.0 743.6 jit_solution(17155492854786503554)
XLA Ops:
  8.1 7.7 %all_to_all.76 = bf16[16,4,512]{2,0,1:T(8,128)(2,1)} all-to-all(bf16[16,4,512]{2,0,1:T(8,128)(2,1)S(1)} %bitcast.183), channel_id=1, replica_groups=mesh['row'=4,'col'=32] {'row'}, dimensions={1} | all-to-all | bytes 131072 | tf_op jit(solution)/shard_map/all_to_all | solution.py:74
  17.7 8.5 %all_to_all.77 = bf16[16,4,1536]{2,0,1:T(8,128)(2,1)} all-to-all(bf16[16,4,1536]{2,0,1:T(8,128)(2,1)S(1)} %bitcast.177), channel_id=1, replica_groups=mesh['row'=4,'col'=32] {'row'}, dimensions={1} | all-to-all | bytes 393216 | tf_op jit(solution)/shard_map/all_to_all | solution.py:71
  27.4 8.8 %all_to_all.78 = bf16[16,4,2048]{2,0,1:T(8,128)(2,1)} all-to-all(bf16[16,4,2048]{2,0,1:T(8,128)(2,1)S(1)} %bitcast.175), channel_id=1, replica_groups=mesh['row'=4,'col'=32] {'row'}, dimensions={1} | all-to-all | bytes 524288 | tf_op jit(solution)/shard_map/all_to_all | solution.py:77
  38.0 4.4 all-to-all-start.3
  42.5 1.2 dynamic_slice.41
  43.7 1.3 dynamic_slice.42
  45.0 1.9 fusion.72
  47.6 6.1 reshape.576
  53.6 11.1 %reshape.545 = bf16[1,8,4096,64]{3,2,1,0:T(8,128)(2,1)} reshape(bf16[2097152]{0:T(1024)(128)(2,1)} %reshape.576) | data formatting | bytes 8388608 | tf_op jit(solution)/shard_map/reshape | solution.py:157
  64.7 6.0 reshape.578
  70.7 11.0 %reshape.546 = bf16[1,8,4096,64]{3,2,1,0:T(8,128)(2,1)} reshape(bf16[2097152]{0:T(1024)(128)(2,1)} %reshape.578) | data formatting | bytes 8388608 | tf_op jit(solution)/shard_map/reshape | solution.py:158
  81.8 5.1 all_gather.25
  88.2 3.2 copy.89
  91.4 44.8 %all-gather.8.cloned.1.call-done = bf16[1024,2048]{1,0:T(8,128)(2,1)} async-done(((bf16[1024,512]{1,0:T(8,128)(2,1)}), bf16[1024,2048]{1,0:T(8,128)(2,1)}) %all-gather.8.cloned.1.call-update) | async-done | bytes 4194320 | tf_op jit(solution)/shard_map/all_gather | solution.py:94
  136.2 2.8 convert_reduce_fusion
  139.1 3.0 fusion.36
  142.2 89.1 %all-gather.10.cloned.1.call-done = bf16[2048,1536]{1,0:T(8,128)(2,1)} async-done(((bf16[64,1536]{1,0:T(8,128)(2,1)}), bf16[2048,1536]{1,0:T(8,128)(2,1)}) %all-gather.10.cloned.1.call-update) | async-done | bytes 6291472 | tf_op jit(solution)/shard_map/all_gather | solution.py:85
  231.2 3.5 copy.76
  235.2 7.0 fusion.85
  242.2 3.1 slice.161
  245.4 6.6 copy.77
  252.0 9.2 %reshape.540 = f32[2,512,8,3,64]{1,0,4,3,2:T(2,128)} reshape(f32[1024,1536]{0,1:T(8,128)} %copy.77) | data formatting | bytes 12582912 | tf_op jit(solution)/shard_map/reshape | solution.py:131
  261.7 79.5 %all-gather = bf16[32,1,1536]{2,1,0:T(2,128)(2,1)S(1)} all-gather(bf16[1,1,1536]{2,1,0:T(2,128)(2,1)S(1)} %reshape.556), channel_id=1, replica_groups=mesh['row'=4,'col'=32] {'col'}, dimensions={0}, use_global_device_ids=true | all-gather | bytes 101376 | tf_op jit(solution)/shard_map/all_gather | solution.py:149
  341.6 18.2 %while.40 = (s32[]{:T(128)}, f32[1,8,4096]{2,1,0:T(8,128)S(1)}, s32[1]{0:T(128)}, bf16[1,8,4096,64]{3,2,1,0:T(8,128)(2,1)}, bf16[1,8,64]{2,1,0:T(8,128)(2,1)S(1)...) while((s32[]{:T(128)}, f32[1,8,4096]{2,1,0:T(8,128)S(1)}, s32[1]{0:T(128)}, ...), condition=%wide.region_9.10_spmd, body=%wide.region_8.9_spmd.sunk | while | flops 533510 | bytes 1099931 | solution.py:174
  342.3 1.6 fusion.110
  344.5 1.6 fusion.110
  346.8 1.6 fusion.110
  349.1 1.6 fusion.110
  351.4 1.6 fusion.110
  353.7 1.6 fusion.110
  355.9 1.6 fusion.110
  358.2 1.6 fusion.110
  360.4 12.2 %while.41 = (s32[]{:T(128)}, f32[1,8,64]{2,1,0:T(8,128)S(1)}, bf16[1,8,4096]{2,1,0:T(8,128)(2,1)S(1)}, bf16[1,8,4096,64]{3,2,1,0:T(8,128)(2,1)}, s32[]{:T(128)}, /*index=5*/s32[]{:T(128)}, s32[]{:T(128)}, s32[]{:T(128)}) while((s32[]{:T(128)}, f32[1,8,64]{2,1,0:T(8,128)S(1)}, bf16[1,8,4096]{2,1,0:T(8,128)(2,1)S(1)}, ...), condition=%wide.region_13.14_spmd, body=%wide.region_12.13_spmd.sunk | while | flops 524806 | bytes 1081483 | solution.py:194
  360.5 1.5 fusion.113
  362.0 1.5 fusion.113
  363.5 1.5 fusion.113
  365.0 1.5 fusion.113
  366.6 1.5 fusion.113
  368.1 1.5 fusion.113
  369.6 1.5 fusion.113
  371.1 1.5 fusion.113
  372.8 75.5 %all-gather.1 = bf16[32,1,512]{2,1,0:T(2,128)(2,1)S(1)} all-gather(bf16[1,1,512]{2,1,0:T(2,128)(2,1)S(1)} %reshape.558), channel_id=1, replica_groups=mesh['row'=4,'col'=32] {'col'}, dimensions={0}, use_global_device_ids=true | all-gather | bytes 33792 | tf_op jit(solution)/shard_map/all_gather | solution.py:196
  449.5 53.5 %while.42 = (s32[]{:T(128)}, bf16[2,512,512]{2,1,0:T(8,128)(2,1)}, f32[2,512,8,3,64]{1,0,4,3,2:T(2,128)}, s32[2]{0:T(128)}, s32[]{:T(128)}) while((s32[]{:T(128)}, bf16[2,512,512]{2,1,0:T(8,128)(2,1)}, f32[2,512,8,3,64]{1,0,4,3,2:T(2,128)}, s32[2]{0:T(128)}, s32[]{:T(128)}) %tuple.118), condition=%wide.region_5.6_spmd.clone.clone, body=%wide.region_2.5_spmd.clone.clone.sunk | while | flops 554444288 | bytes 41063644 | solution.py:132
  449.5 1.2 dynamic_slice.66
  451.7 6.1 constant_dynamic-slice_fusion.2
  460.8 8.3 %fusion.116 = (f32[8,512]{1,0:T(8,128)}, f32[8,512,512]{1,2,0:T(8,128)}) fusion(pred[512,512]{0,1:T(8,128)(4,1)S(1)} %fusion.115, bf16[512,8,32]{0,2,1:T(8,128)(2,1)} %slice.235, bf16[512,8,16]{0,2,1:T(8,128)(2,1)} %get-tuple-element.479, bf16[512,8,16]{0,2,1:T(8,128)(2,1)} %get-tuple-element.480, bf16[512,8,32]{0,2,1:T(8,128)(2,1)} %slice.236, ...), kind=kOutput, calls=%fused_computation.141.clone.1 | convolution fusion | flops 279970304 | bytes 9715712 | tf_op jit(solution)/shard_map/while/body/eval_jaxpr/sub | solution.py:126
  469.1 5.1 fusion.117
  474.2 1.3 copy.148
  478.4 6.1 constant_dynamic-slice_fusion.2
  487.6 8.3 %fusion.116 = (f32[8,512]{1,0:T(8,128)}, f32[8,512,512]{1,2,0:T(8,128)}) fusion(pred[512,512]{0,1:T(8,128)(4,1)S(1)} %fusion.115, bf16[512,8,32]{0,2,1:T(8,128)(2,1)} %slice.235, bf16[512,8,16]{0,2,1:T(8,128)(2,1)} %get-tuple-element.479, bf16[512,8,16]{0,2,1:T(8,128)(2,1)} %get-tuple-element.480, bf16[512,8,32]{0,2,1:T(8,128)(2,1)} %slice.236, ...), kind=kOutput, calls=%fused_computation.141.clone.1 | convolution fusion | flops 279970304 | bytes 9715712 | tf_op jit(solution)/shard_map/while/body/eval_jaxpr/sub | solution.py:126
  495.8 5.1 fusion.117
  500.9 1.3 copy.148
  503.0 4.3 fusion.53
  507.3 3.3 copy-done.1
  510.7 1.3 copy.99
  512.3 8.4 %copy.91 = bf16[32,4,16,2048]{3,2,0,1:T(8,128)(2,1)} copy(bf16[32,4,16,2048]{3,2,1,0:T(8,128)(2,1)} %bitcast.161) | data formatting | bytes 16777216 | tf_op jit(solution)/shard_map/reshape | solution.py:46
  520.8 8.4 %copy.93 = bf16[32,4,16,2048]{3,2,0,1:T(8,128)(2,1)} copy(bf16[32,4,16,2048]{3,2,1,0:T(8,128)(2,1)} %bitcast.162) | data formatting | bytes 16777216 | tf_op jit(solution)/shard_map/reshape | solution.py:46
  529.2 27.6 %convolution_convert_fusion = bf16[1025,2048]{1,0:T(8,128)(2,1)} fusion(bf16[2048,2048]{1,0:T(8,128)(2,1)} %bitcast.164, bf16[2048,2048]{1,0:T(8,128)(2,1)} %bitcast.163, f32[2048]{0:T(1024)S(1)} %copy-done.9, f32[2048]{0:T(1024)S(1)} %copy-done.11, f32[1025]{0:T(1024)S(1)} %copy-done.5, f32[1025]{0:T(1024)S(1)} %broadcast_multiply_fusion, ...), kind=kOutput, calls=%fused_computation.73 | convolution fusion | flops 17236531200 | bytes 25198600 | tf_op jit(solution)/shard_map/dot_general | solution.py:109
  558.7 4.7 slice.170
  563.5 7.8 %slice.169 = f32[1024,2048]{1,0:T(8,128)} slice(f32[1025,2048]{1,0:T(8,128)} %copy-done.1), slice={[0:1024], [0:2048]} | slice | bytes 16777216 | tf_op jit(solution)/shard_map/slice | solution.py:204
  572.5 30.1 %reduce-scatter.15.cloned.1.call-done = bf16[512,1]{1,0:T(8,128)(2,1)} async-done(((bf16[2048,1]{1,0:T(8,128)(2,1)}), bf16[512,1]{1,0:T(8,128)(2,1)}) %reduce-scatter.15.cloned.1.call-update) | async-done | bytes 1040
  604.2 46.9 %reduce-scatter.11.cloned.1.call-done = bf16[1024,512]{1,0:T(8,128)(2,1)} async-done(((bf16[1024,2048]{1,0:T(8,128)(2,1)}), bf16[1024,512]{1,0:T(8,128)(2,1)}) %reduce-scatter.11.cloned.1.call-update) | async-done | bytes 1048592 | tf_op jit(solution)/shard_map/reduce_scatter | solution.py:208
  651.1 82.5 %reduce-scatter.9.cloned.1.call-done = f32[1024,512]{1,0:T(8,128)} async-done(((f32[1024,2048]{1,0:T(8,128)}), f32[1024,512]{1,0:T(8,128)}) %reduce-scatter.9.cloned.1.call-update) | async-done | bytes 2097168 | tf_op jit(solution)/shard_map/reduce_scatter | solution.py:204
  733.6 3.3 add_convert_fusion.2
  (154 shorter events, 31.8 us)
Async XLA Ops:
  7.2 81.1 %all-gather.12.cloned.1.call-start = ((), (), s32[]{:S(2)}) async-start(), calls=%async_computation.10 | async-start | bytes 2162688 | tf_op jit(solution)/shard_map/all_gather | solution.py:86
  15.9 120.4 %all-gather.8.cloned.1.call-start = ((), (), s32[]{:S(2)}) async-start(), calls=%async_computation.8 | async-start | bytes 5242880 | tf_op jit(solution)/shard_map/all_gather | solution.py:94
  16.6 214.6 %all-gather.10.cloned.1.call-start = ((), (), s32[]{:S(2)}) async-start(), calls=%async_computation.9 | async-start | bytes 6488064 | tf_op jit(solution)/shard_map/all_gather | solution.py:85
  26.3 486.1 %all-gather.14.cloned.1.call-start = ((), (), s32[]{:S(2)}) async-start(), calls=%async_computation.12 | async-start | bytes 8650752 | tf_op jit(solution)/shard_map/all_gather | solution.py:87
  38.0 48.9 %all-to-all-start.3 = ((bf16[16,4,2048]{2,0,1:T(8,128)(2,1)}), bf16[16,4,2048]{2,0,1:T(8,128)(2,1)S(1)}, u32[]{:S(2)}, u32[]{:S(2)}) async-start(bf16[16,4,2048]{2,0,1:T(8,128)(2,1)} %bitcast.126), calls=%async_computation.4 | async-start | bytes 524288 | tf_op jit(solution)/shard_map/all_to_all | solution.py:80
  42.5 478.3 %all-gather.16.cloned.1.call-start = ((), (), s32[]{:S(2)}) async-start(), calls=%async_computation.13 | async-start | bytes 8650752 | tf_op jit(solution)/shard_map/all_gather | solution.py:88
  64.7 17.1 %copy-start.6 = (bf16[1,512]{1,0:T(2,128)(2,1)S(1)}, bf16[1,512]{1,0:T(2,128)(2,1)}, u32[]{:S(2)}) copy-start(bf16[1,512]{1,0:T(2,128)(2,1)} %param.20) | copy-start | bytes 3076
  87.0 0.7 copy-start.3
  87.7 483.7 %reduce-scatter.13.cloned.1.call-start = ((), (), s32[]{:S(2)}) async-start(), calls=%async_computation.15 | async-start | bytes 1310720
  139.1 95.6 %copy-start.8 = (f32[2048]{0:T(1024)S(1)}, f32[2048]{0:T(1024)}, u32[]{:S(2)}) copy-start(f32[2048]{0:T(1024)} %param.22) | copy-start | bytes 24580
  139.1 95.6 %copy-start.10 = (f32[2048]{0:T(1024)S(1)}, f32[2048]{0:T(1024)}, u32[]{:S(2)}) copy-start(f32[2048]{0:T(1024)} %param.21) | copy-start | bytes 24580
  142.2 92.5 %copy-start.4 = (f32[1025]{0:T(1024)}, f32[1025]{0:T(1024)S(1)}, u32[]{:S(2)}) copy-start(f32[1025]{0:T(1024)S(1)} %add_rsqrt_fusion) | copy-start | bytes 12304
  231.2 4.0 copy-start
  252.0 89.2 %copy-start.12 = (s32[32]{0:T(128)S(1)}, s32[32]{0:T(128)}, u32[]{:S(2)}) copy-start(s32[32]{0:T(128)} %param.31) | copy-start | bytes 388
  507.3 3.3 copy-start.1
  512.1 90.5 %reduce-scatter.15.cloned.1.call-start = ((), (), s32[]{:S(2)}) async-start(), calls=%async_computation.16 | async-start | bytes 655360
  520.8 8.4 %copy-start.5 = (f32[1025]{0:T(1024)S(1)}, f32[1025]{0:T(1024)}, u32[]{:S(2)}) copy-start(f32[1025]{0:T(1024)} %copy-done.4) | copy-start | bytes 12304
  520.8 8.4 %copy-start.9 = (f32[2048]{0:T(1024)S(1)}, f32[2048]{0:T(1024)}, u32[]{:S(2)}) copy-start(f32[2048]{0:T(1024)} %param.22) | copy-start | bytes 24580
  520.8 8.4 %copy-start.11 = (f32[2048]{0:T(1024)S(1)}, f32[2048]{0:T(1024)}, u32[]{:S(2)}) copy-start(f32[2048]{0:T(1024)} %param.21) | copy-start | bytes 24580
  558.6 92.5 %reduce-scatter.11.cloned.1.call-start = ((), (), s32[]{:S(2)}) async-start(), calls=%async_computation.14 | async-start | bytes 5242880 | tf_op jit(solution)/shard_map/reduce_scatter | solution.py:208
  563.4 170.2 %reduce-scatter.9.cloned.1.call-start = ((), (), s32[]{:S(2)}) async-start(), calls=%async_computation.11 | async-start | bytes 10485760 | tf_op jit(solution)/shard_map/reduce_scatter | solution.py:204
  571.3 32.3 %copy-start.7 = (bf16[1,512]{1,0:T(2,128)(2,1)S(1)}, bf16[1,512]{1,0:T(2,128)(2,1)}, u32[]{:S(2)}) copy-start(bf16[1,512]{1,0:T(2,128)(2,1)} %param.20) | copy-start | bytes 3076
  571.3 162.3 %copy-start.2 = (bf16[1024,512]{1,0:T(8,128)(2,1)S(1)}, bf16[1024,512]{1,0:T(8,128)(2,1)}, u32[]{:S(2)}) copy-start(bf16[1024,512]{1,0:T(8,128)(2,1)} %param.19) | copy-start | bytes 3145732
Sparse Core Ops, SparseCore 0:
  16.0 71.9 all-gather.11
  89.6 46.5 all-gather.7
  139.2 91.9 all-gather.9
  234.2 104.1 all-gather.13
  341.4 102.0 all-gather.15
  512.2 45.2 reduce-scatter.12
  560.0 42.5 reduce-scatter.14
  605.1 45.9 reduce-scatter.10
  653.6 79.9 reduce-scatter.8
where the time goes:
time: 751 us; the launch traced here: 744 us
  waiting for transfers between devices  294 us (39%)
  blocking collectives  185 us (25%)
  local copies, waits for them, and re-layouts  127 us (17%)
  matrix products  91.1 us (12%)
  other arithmetic  25.6 us (3%)
  between operations  15 us (2%)
    all_gather x1, waiting for transfers between devices, on_device(): lax.all_gather(regrouped[0], 'col', axis=0, tiled=True)  89.1 us
    reduce_scatter x1, waiting for transfers between devices, on_device(): lax.psum_scatter(attn_part[:rows_prompt], 'row', scatter_dimension=1, til...  82.5 us
    all_gather x1, blocking collectives, on_device(): handed = lax.all_gather(packed, 'col', axis=0, tiled=True)  79.5 us
    all_gather x1, blocking collectives, on_device(): returned = lax.all_gather(decode_mixed, 'col', axis=0, tiled=True)  75.5 us
    reduce_scatter x1, waiting for transfers between devices, on_device(): lax.psum_scatter(mlp_part[:rows_prompt].astype(jnp.bfloat16), 'row', scat...  46.9 us
    all_gather x1, waiting for transfers between devices, on_device(): lax.all_gather(prompt_tokens, 'row', axis=1, tiled=True)  44.8 us
    unnamed x11, waiting for transfers between devices  30.9 us
    dot_general x1, matrix products, on_device(): lax.dot_general(hidden, w_reduce, (((1,), (1,)), ((), ())), preferred_ele...  27.6 us
  transfers between devices with their start and end apart: 10, of which 5 were waited for; matrix products, arithmetic and copies ran while one was open for 32% of the time, Pallas kernels for 0%

commit v1 on v0

--- a/solution.py
+++ b/solution.py
@@ -67,40 +67,39 @@
     half_float = jnp.bfloat16
     row_count = lax.axis_size("row")
     col_count = lax.axis_size("col")
-    regrouped = (
-        lax.all_to_all(
-            project_weight.astype(half_float), "row", split_axis=1, concat_axis=0, tiled=True
-        ),
-        lax.all_to_all(
-            dense_weight.astype(half_float), "row", split_axis=1, concat_axis=0, tiled=True
-        ),
-        lax.all_to_all(
-            expand_weight.astype(half_float), "row", split_axis=1, concat_axis=0, tiled=True
-        ),
-        lax.all_to_all(
-            reduce_weight.astype(half_float), "row", split_axis=1, concat_axis=0, tiled=True
-        ),
-    )
-    gathered = (
-        lax.all_gather(regrouped[0], "col", axis=0, tiled=True),
-        lax.all_gather(regrouped[1], "col", axis=0, tiled=True),
-        lax.all_gather(regrouped[2], "col", axis=0, tiled=True),
-        lax.all_gather(regrouped[3], "col", axis=0, tiled=True),
-    )
-    w_project, w_dense, w_expand, w_reduce = [
-        restore_rows(piece, row_count, col_count) for piece in gathered
-    ]
-    prompt_full, decode_full = (
-        lax.all_gather(prompt_tokens, "row", axis=1, tiled=True),
-        lax.all_gather(decode_tokens, "row", axis=1, tiled=True),
-    )
+
+    def by_row_group(weight):
+        local_rows, width = weight.shape
+        return weight.astype(half_float).reshape(local_rows, row_count, width // row_count)
+
+    def regroup(weights):
+        joined = jnp.concatenate([by_row_group(w) for w in weights], axis=2)
+        swapped = lax.all_to_all(joined, "row", split_axis=1, concat_axis=0, tiled=True)
+        flat = swapped.reshape(swapped.shape[0], swapped.shape[2])
+        gathered = lax.all_gather(flat, "col", axis=0, tiled=True)
+        restored = restore_rows(gathered, row_count, col_count)
+        pieces = []
+        offset = 0
+        for w in weights:
+            width = w.shape[1] // row_count
+            pieces.append(restored[:, offset:offset + width])
+            offset += width
+        return pieces
+
+    w_project, w_dense = regroup((project_weight, dense_weight))
+    w_expand, w_reduce = regroup((expand_weight, reduce_weight))
+    local_joined = jnp.concatenate([prompt_tokens, decode_tokens], axis=0)
+    spread = jnp.broadcast_to(local_joined[None], (row_count,) + local_joined.shape)
+    swapped_rows = lax.all_to_all(spread, "row", split_axis=0, concat_axis=0, tiled=True)
+    joined = swapped_rows.transpose(1, 0, 2).reshape(local_joined.shape[0], -1)
+    prompt_full = joined[: prompt_tokens.shape[0]]
+    decode_full = joined[prompt_tokens.shape[0]:]
     rows_prompt = prompt_full.shape[0]
     slot_local = decode_full.shape[0]
     prompt_count = rows_prompt // PLEN
     heads_local = w_dense.shape[1] // HD
     total_slots = slot_request.shape[0]
     scale = HD ** (-0.5)
-    joined = jnp.concatenate([prompt_full, decode_full], axis=0)
     normed = layer_norm(joined, norm_gain, norm_bias)
     merged = jnp.dot(normed, w_project, preferred_element_type=jnp.float32)
     hidden = jax.nn.gelu(
@@ -146,7 +145,10 @@
     packed = jnp.stack([query_new, key_new, value_new], axis=2).reshape(
         slot_local, heads_local * 3 * HD
     )
-    handed = lax.all_gather(packed, "col", axis=0, tiled=True)
+    handed = lax.all_to_all(
+        jnp.broadcast_to(packed, (col_count,) + packed.shape[1:]),
+        "col", split_axis=0, concat_axis=0, tiled=True,
+    )
     chooser = (slot_request[None, :] == local_ids[:, None]).astype(half_float)
     mine = jnp.dot(chooser, handed, preferred_element_type=jnp.float32).astype(half_float)
     mine = mine.reshape(slot_local, heads_local, 3, HD)
@@ -193,29 +195,21 @@
     start_value = own_prob.astype(jnp.float32)[:, :, None] * own_value.astype(jnp.float32)
     decode_sum = lax.fori_loop(0, block_count, value_block, start_value)
     decode_mixed = decode_sum.astype(half_float).reshape(slot_local, heads_local * HD)
-    returned = lax.all_gather(decode_mixed, "col", axis=0, tiled=True)
+    returned = lax.all_to_all(
+        jnp.broadcast_to(decode_mixed, (col_count,) + decode_mixed.shape[1:]),
+        "col", split_axis=0, concat_axis=0, tiled=True,
+    )
     picker = slot_match.astype(half_float)
     decode_heads = jnp.dot(picker, returned, preferred_element_type=jnp.float32).astype(half_float)
     mixed_all = jnp.concatenate([prompt_mixed, decode_heads], axis=0)
     attn_part = lax.dot_general(
         mixed_all, w_dense, (((1,), (1,)), ((), ())), preferred_element_type=jnp.float32
     )
-    attn_prompt, attn_decode = (
-        lax.psum_scatter(attn_part[:rows_prompt], "row", scatter_dimension=1, tiled=True),
-        lax.psum_scatter(attn_part[rows_prompt:], "row", scatter_dimension=1, tiled=True),
-    )
-    mlp_prompt, mlp_decode = (
-        lax.psum_scatter(
-            mlp_part[:rows_prompt].astype(jnp.bfloat16), "row", scatter_dimension=1, tiled=True
-        ).astype(jnp.float32),
-        lax.psum_scatter(
-            mlp_part[rows_prompt:].astype(jnp.bfloat16), "row", scatter_dimension=1, tiled=True
-        ).astype(jnp.float32),
-    )
-    summed_prompt = attn_prompt + mlp_prompt
-    summed_decode = attn_decode + mlp_decode
-    prompt_result = prompt_tokens.astype(jnp.float32) + summed_prompt
-    decode_result = decode_tokens.astype(jnp.float32) + summed_decode
+    summed = lax.psum_scatter(
+        (attn_part + mlp_part).astype(half_float), "row", scatter_dimension=1, tiled=True
+    ).astype(jnp.float32)
+    prompt_result = prompt_tokens.astype(jnp.float32) + summed[:rows_prompt]
+    decode_result = decode_tokens.astype(jnp.float32) + summed[rows_prompt:]
     return (prompt_result.astype(half_float), decode_result.astype(half_float))
 
 

time: 751 us -> 457 us (0.61)
  waiting for transfers between devices: 294 us -> 110 us
  blocking collectives: 185 us -> 21.4 us
  starting transfers between devices: 5.42 us -> 30.8 us
  local copies, waits for them, and re-layouts: 127 us -> 141 us
  matrix products: 91.1 us -> 101 us
    all_gather x3 -> x0, blocking collectives: 160 us -> none  [the longest x1 79.5 us: on_device(): handed = lax.all_gather(packed, 'col', axis=0, tiled=True)]
    all_gather x5 -> x2, waiting for transfers between devices: 134 us -> 0.03 us  [regroup(): gathered = lax.all_gather(flat, 'col', axis=0, tiled=True)]
    reduce_scatter x2 -> x1, waiting for transfers between devices: 129 us -> 49 us  [on_device(): lax.psum_scatter((attn_part + mlp_part).astype(half_float), 'row', scatte...]
    all_to_all x1 -> x3, waiting for transfers between devices: 0.01 us -> 61 us  [the longest x1 61 us: on_device(): lax.all_to_all(spread, 'row', split_axis=0, concat_axis=0, tiled=True)]
    unnamed x11 -> x3, waiting for transfers between devices: 30.9 us -> 0.05 us
    all_to_all x1 -> x3, starting transfers between devices: 4.41 us -> 30.7 us  [the longest x1 14.9 us: on_device(): lax.all_to_all(jnp.broadcast_to(packed, (col_count,) + packed.shape[1:]),...]
    convert_element_type x0 -> x1, local copies, waits for them, and re-layouts: none -> 19.4 us  [layer_norm(): values = rows.astype(jnp.float32)]
    slice x4 -> x0, local copies, waits for them, and re-layouts: 13.3 us -> none  [the longest x1 7.82 us: on_device(): attn_part[:rows_prompt]]
  transfers between devices with their start and end apart: 10 -> 6, of which waited for: 5 -> 2; matrix products, arithmetic and copies ran while one was open for 32% -> 47% of each run, Pallas kernels for 0% -> 0%
where the time goes in v1:
time: 457 us; the launch traced here: 452 us
  local copies, waits for them, and re-layouts  141 us (31%)
  waiting for transfers between devices  110 us (24%)
  matrix products  101 us (22%)
  other arithmetic  31.3 us (7%)
  starting transfers between devices  30.8 us (7%)
  blocking collectives  21.4 us (5%)
  between operations  15 us (3%)
    all_to_all x1, waiting for transfers between devices, on_device(): lax.all_to_all(spread, 'row', split_axis=0, concat_axis=0, tiled=True)  61 us
    reduce_scatter x1, waiting for transfers between devices, on_device(): lax.psum_scatter((attn_part + mlp_part).astype(half_float), 'row', scatte...  49 us
    dot_general x1, matrix products, on_device(): lax.dot_general(hidden, w_reduce, (((1,), (1,)), ((), ())), preferred_ele...  28.5 us
    unnamed x32, local copies, waits for them, and re-layouts  26.1 us
    reshape x2, local copies, waits for them, and re-layouts, restore_rows(): block.reshape(col_count, row_count, shard_rows, width).transpose(1, 0, 2, 3)  22.4 us
    all_to_all x2, blocking collectives, regroup(): lax.all_to_all(joined, 'row', split_axis=1, concat_axis=0, tiled=True)  21.4 us
    convert_element_type x1, local copies, waits for them, and re-layouts, layer_norm(): values = rows.astype(jnp.float32)  19.4 us
    sub x2, matrix products, prompt_block(): raised = jnp.exp(scores - top)  16.5 us
  transfers between devices with their start and end apart: 6, of which 2 were waited for; matrix products, arithmetic and copies ran while one was open for 47% of the time, Pallas kernels for 0%

profile of v1, /device:TPU:1, one launch (start us, length us, event | category | flops | bytes accessed | tf_op | source)
XLA Modules:
  0.0 451.6 jit_solution(13209618191397862010)
XLA Ops:
  7.2 1.0 convert_element_type.254
  8.3 1.0 convert_element_type.253
  9.7 9.5 %all_to_all.53 = bf16[16,4,2048]{2,0,1:T(8,128)(2,1)} all-to-all(bf16[16,4,2048]{2,0,1:T(8,128)(2,1)S(1)} %copy.66), channel_id=1, replica_groups=mesh['row'=4,'col'=32] {'row'}, dimensions={1} | all-to-all | bytes 524288 | tf_op jit(solution)/shard_map/all_to_all | solution.py:77
  19.3 1.1 convert_element_type.271
  20.5 1.1 convert_element_type.270
  22.4 11.9 %all_to_all.54 = bf16[16,4,4096]{2,0,1:T(8,128)(2,1)} all-to-all(bf16[16,4,4096]{2,0,1:T(8,128)(2,1)S(1)} %copy.79), channel_id=1, replica_groups=mesh['row'=4,'col'=32] {'row'}, dimensions={1} | all-to-all | bytes 1048576 | tf_op jit(solution)/shard_map/all_to_all | solution.py:77
  34.5 2.2 broadcast_in_dim.108
  36.7 6.4 %all-to-all-start = ((bf16[4,1025,512]{2,1,0:T(8,128)(2,1)}), bf16[4,1025,512]{2,1,0:T(8,128)(2,1)}, u32[]{:S(2)}, u32[]{:S(2)}) async-start(bf16[4,1025,512]{2,1,0:T(8,128)(2,1)} %broadcast_in_dim.108), calls=%async_computation | async-start | bytes 8454144 | tf_op jit(solution)/shard_map/all_to_all | solution.py:93
  43.8 1.3 fusion.79
  45.8 61.0 %all-to-all-done = bf16[4,1025,512]{2,1,0:T(8,128)(2,1)} async-done(((bf16[4,1025,512]{2,1,0:T(8,128)(2,1)}), bf16[4,1025,512]{2,1,0:T(8,128)(2,1)}, u32[]{:S(2)}, u32[]{:S(2)}) %all-to-all-start) | async-done | bytes 4198432 | tf_op jit(solution)/shard_map/all_to_all | solution.py:93
  106.9 3.5 convert_bitcast_fusion
  110.4 19.4 %copy.65 = f32[1025,4,512]{2,1,0:T(4,128)S(1)} copy(f32[1025,4,512]{2,0,1:T(8,128)S(1)} %convert_bitcast_fusion) | data formatting | bytes 16793600 | tf_op jit(solution)/shard_map/convert_element_type | solution.py:17
  129.8 1.5 pad.21
  131.4 7.4 %copy.93 = f32[129,8,4,512]{3,1,2,0:T(8,128)} copy(f32[129,8,4,512]{3,2,1,0:T(4,128)S(1)} %bitcast.132) | data formatting | bytes 16908288
  138.8 2.8 convert_reduce_fusion
  141.7 3.5 fusion.43
  145.2 8.3 %copy.67 = bf16[32,4,16,2048]{3,2,0,1:T(8,128)(2,1)} copy(bf16[32,4,16,2048]{3,2,1,0:T(8,128)(2,1)} %bitcast.140) | data formatting | bytes 16777216 | tf_op jit(solution)/shard_map/reshape | solution.py:46
  153.5 11.7 %fusion.51 = f32[1025,1536]{1,0:T(8,128)S(1)} fusion(bf16[2048,2048]{1,0:T(8,128)(2,1)} %bitcast.138, f32[1025,2048]{1,0:T(8,128)} %bitcast.136, f32[2048]{0:T(1024)S(1)} %copy-done.6, f32[2048]{0:T(1024)S(1)} %copy-done.8, f32[1025]{0:T(1024)S(1)} %add_rsqrt_fusion, f32[1025]{0:T(1024)S(1)} %broadcast_multiply_fusion), kind=kOutput, calls=%fused_computation.77 | convolution fusion | flops 6459238400 | bytes 21067784 | tf_op jit(solution)/shard_map/dot_general | solution.py:104
  165.2 2.6 copy-done
  169.1 1.2 reduce.13
  171.0 14.9 %all-to-all-start.2 = ((bf16[32,2,768]{2,1,0:T(2,128)(2,1)}), bf16[32,2,768]{2,1,0:T(2,128)(2,1)S(1)}, u32[]{:S(2)}, u32[]{:S(2)}) async-start(bf16[32,2,768]{2,1,0:T(2,128)(2,1)} %reshape.601), calls=%async_computation.2 | async-start | bytes 196608 | tf_op jit(solution)/shard_map/all_to_all | solution.py:148
  186.5 6.2 %reshape.597 = bf16[2097152]{0:T(1024)(128)(2,1)} reshape(bf16[1,8,262144]{2,1,0:T(8,128)(2,1)} %param.27) | data formatting | bytes 8388608
  192.7 11.2 %reshape.577 = bf16[1,8,4096,64]{3,2,1,0:T(8,128)(2,1)} reshape(bf16[2097152]{0:T(1024)(128)(2,1)} %reshape.597) | data formatting | bytes 8388608 | tf_op jit(solution)/shard_map/reshape | solution.py:159
  203.9 6.1 %reshape.599 = bf16[2097152]{0:T(1024)(128)(2,1)} reshape(bf16[1,8,262144]{2,1,0:T(8,128)(2,1)} %param.28) | data formatting | bytes 8388608
  210.1 11.2 %reshape.578 = bf16[1,8,4096,64]{3,2,1,0:T(8,128)(2,1)} reshape(bf16[2097152]{0:T(1024)(128)(2,1)} %reshape.599) | data formatting | bytes 8388608 | tf_op jit(solution)/shard_map/reshape | solution.py:160
  221.3 6.0 %slice.168 = f32[1024,1536]{1,0:T(8,128)} slice(f32[1025,1536]{1,0:T(8,128)} %copy-done), slice={[0:1024], [0:1536]} | slice | bytes 12582912 | tf_op jit(solution)/shard_map/slice | solution.py:130
  227.3 6.6 %copy.68 = f32[1024,1536]{0,1:T(8,128)} copy(f32[1024,1536]{1,0:T(8,128)} %slice.168) | data formatting | bytes 12582912 | tf_op jit(solution)/shard_map/slice | solution.py:130
  233.9 9.2 %reshape.573 = f32[2,512,8,3,64]{1,0,4,3,2:T(2,128)} reshape(f32[1024,1536]{0,1:T(8,128)} %copy.68) | data formatting | bytes 12582912 | tf_op jit(solution)/shard_map/reshape | solution.py:130
  243.5 18.5 %while.40 = (s32[]{:T(128)}, f32[1,8,4096]{2,1,0:T(8,128)S(1)}, s32[1]{0:T(128)}, bf16[1,8,4096,64]{3,2,1,0:T(8,128)(2,1)}, bf16[1,8,64]{2,1,0:T(8,128)(2,1)S(1)...) while((s32[]{:T(128)}, f32[1,8,4096]{2,1,0:T(8,128)S(1)}, s32[1]{0:T(128)}, ...), condition=%wide.region_9.10_spmd, body=%wide.region_8.9_spmd.sunk | while | flops 533510 | bytes 1099939 | solution.py:176
  243.5 1.6 fusion.106
  245.8 1.6 fusion.106
  248.1 1.6 fusion.106
  250.4 1.6 fusion.106
  252.8 1.6 fusion.106
  255.1 1.6 fusion.106
  257.4 1.6 fusion.106
  259.7 1.6 fusion.106
  262.6 12.2 %while.41 = (s32[]{:T(128)}, f32[1,8,64]{2,1,0:T(8,128)S(1)}, bf16[1,8,4096]{2,1,0:T(8,128)(2,1)S(1)}, bf16[1,8,4096,64]{3,2,1,0:T(8,128)(2,1)}, s32[]{:T(128)}, /*index=5*/s32[]{:T(128)}, s32[]{:T(128)}, s32[]{:T(128)}) while((s32[]{:T(128)}, f32[1,8,64]{2,1,0:T(8,128)S(1)}, bf16[1,8,4096]{2,1,0:T(8,128)(2,1)S(1)}, ...), condition=%wide.region_13.14_spmd, body=%wide.region_12.13_spmd.sunk | while | flops 524806 | bytes 1081491 | solution.py:196
  262.6 1.5 fusion.109
  264.1 1.5 fusion.109
  265.7 1.5 fusion.109
  267.2 1.5 fusion.109
  268.7 1.5 fusion.109
  270.3 1.5 fusion.109
  271.8 1.5 fusion.109
  273.3 1.5 fusion.109
  276.3 9.4 %all-to-all-start.3 = ((bf16[32,2,256]{2,1,0:T(2,128)(2,1)}), bf16[32,2,256]{2,1,0:T(2,128)(2,1)}, u32[]{:S(2)}, u32[]{:S(2)}) async-start(bf16[32,2,256]{2,1,0:T(2,128)(2,1)} %reshape.603), calls=%async_computation.3 | async-start | bytes 65536 | tf_op jit(solution)/shard_map/all_to_all | solution.py:198
  285.8 53.7 %while.42 = (s32[]{:T(128)}, bf16[2,512,512]{2,1,0:T(8,128)(2,1)}, f32[2,512,8,3,64]{1,0,4,3,2:T(2,128)}, s32[2]{0:T(128)}, s32[]{:T(128)}) while((s32[]{:T(128)}, bf16[2,512,512]{2,1,0:T(8,128)(2,1)}, f32[2,512,8,3,64]{1,0,4,3,2:T(2,128)}, s32[2]{0:T(128)}, s32[]{:T(128)}) %tuple.118), condition=%wide.region_5.6_spmd.clone.clone, body=%wide.region_2.5_spmd.clone.clone.sunk | while | flops 554444288 | bytes 41063644 | solution.py:131
  286.0 1.2 dynamic_slice.66
  288.0 6.1 %constant_dynamic-slice_fusion.2 = f32[1,512,8,3,64]{1,0,4,3,2:T(1,128)S(1)} fusion(f32[2,512,8,3,64]{1,0,4,3,2:T(2,128)} %get-tuple-element.548, s32[]{:T(128)S(6)} %copy.137), kind=kLoop, calls=%fused_computation.50.clone.1 | loop fusion | bytes 6291460 | tf_op jit(solution)/shard_map/while/body/jit(dynamic_index_in_dim)/dynamic_slice | solution.py:131
  297.4 8.3 %fusion.112 = (f32[8,512]{1,0:T(8,128)}, f32[8,512,512]{1,2,0:T(8,128)}) fusion(pred[512,512]{0,1:T(8,128)(4,1)S(1)} %fusion.111, bf16[512,8,32]{0,2,1:T(8,128)(2,1)} %slice.261, bf16[512,8,16]{0,2,1:T(8,128)(2,1)} %get-tuple-element.479, bf16[512,8,16]{0,2,1:T(8,128)(2,1)} %get-tuple-element.480, bf16[512,8,32]{0,2,1:T(8,128)(2,1)} %slice.262, ...), kind=kOutput, calls=%fused_computation.144.clone.1 | convolution fusion | flops 279970304 | bytes 9715712 | tf_op jit(solution)/shard_map/while/body/eval_jaxpr/sub | solution.py:125
  305.6 5.0 %fusion.113 = bf16[8,64,512]{2,1,0:T(8,128)(2,1)} fusion(f32[8,512,512]{1,2,0:T(8,128)} %get-tuple-element.483, f32[8,512]{1,0:T(8,128)} %get-tuple-element.484, f32[512,8,3,64]{0,3,1,2:T(8,128)S(1)} %bitcast.131), kind=kOutput, calls=%fused_computation.28.clone.1 | convolution fusion | flops 272891904 | bytes 9453568 | tf_op jit(solution)/shard_map/while/body/eval_jaxpr/hqk,khd->qhd/dot_general | solution.py:127
  310.7 1.3 copy.120
  312.8 1.2 dynamic_slice.66
  314.7 6.1 %constant_dynamic-slice_fusion.2 = f32[1,512,8,3,64]{1,0,4,3,2:T(1,128)S(1)} fusion(f32[2,512,8,3,64]{1,0,4,3,2:T(2,128)} %get-tuple-element.548, s32[]{:T(128)S(6)} %copy.137), kind=kLoop, calls=%fused_computation.50.clone.1 | loop fusion | bytes 6291460 | tf_op jit(solution)/shard_map/while/body/jit(dynamic_index_in_dim)/dynamic_slice | solution.py:131
  324.1 8.3 %fusion.112 = (f32[8,512]{1,0:T(8,128)}, f32[8,512,512]{1,2,0:T(8,128)}) fusion(pred[512,512]{0,1:T(8,128)(4,1)S(1)} %fusion.111, bf16[512,8,32]{0,2,1:T(8,128)(2,1)} %slice.261, bf16[512,8,16]{0,2,1:T(8,128)(2,1)} %get-tuple-element.479, bf16[512,8,16]{0,2,1:T(8,128)(2,1)} %get-tuple-element.480, bf16[512,8,32]{0,2,1:T(8,128)(2,1)} %slice.262, ...), kind=kOutput, calls=%fused_computation.144.clone.1 | convolution fusion | flops 279970304 | bytes 9715712 | tf_op jit(solution)/shard_map/while/body/eval_jaxpr/sub | solution.py:125
  332.4 5.0 %fusion.113 = bf16[8,64,512]{2,1,0:T(8,128)(2,1)} fusion(f32[8,512,512]{1,2,0:T(8,128)} %get-tuple-element.483, f32[8,512]{1,0:T(8,128)} %get-tuple-element.484, f32[512,8,3,64]{0,3,1,2:T(8,128)S(1)} %bitcast.131), kind=kOutput, calls=%fused_computation.28.clone.1 | convolution fusion | flops 272891904 | bytes 9453568 | tf_op jit(solution)/shard_map/while/body/eval_jaxpr/hqk,khd->qhd/dot_general | solution.py:127
  337.4 1.3 copy.120
  341.1 14.1 %copy.80 = bf16[32,4,16,4096]{3,2,0,1:T(8,128)(2,1)} copy(bf16[32,4,16,4096]{3,2,1,0:T(8,128)(2,1)} %bitcast.133) | data formatting | bytes 33554432 | tf_op jit(solution)/shard_map/reshape | solution.py:46
  355.2 28.5 %fusion.44 = f32[1025,2048]{1,0:T(8,128)} fusion(bf16[2048,4096]{1,0:T(8,128)(2,1)} %bitcast.134, f32[1025,2048]{1,0:T(8,128)} %bitcast.137, f32[2048]{0:T(1024)S(1)} %copy-done.7, f32[2048]{0:T(1024)S(1)} %copy-done.9, f32[1025]{0:T(1024)S(1)} %add_rsqrt_fusion, f32[1025]{0:T(1024)S(1)} %broadcast_multiply_fusion), kind=kOutput, calls=%fused_computation.72 | convolution fusion | flops 17226035200 | bytes 33595400 | tf_op jit(solution)/shard_map/dot_general | solution.py:108
  383.8 8.5 %fusion.50 = bf16[1025,2048]{1,0:T(8,128)(2,1)} fusion(f32[1025,2048]{1,0:T(8,128)} %fusion.44, bf16[2048,2048]{1,0:T(8,128)(2,1)} %bitcast.139, bf16[1,512]{1,0:T(2,128)(2,1)S(1)} %convert_element_type.269, bf16[1024,512]{1,0:T(8,128)(2,1)S(1)} %bitcast.153), kind=kOutput, calls=%fused_computation.76 | convolution fusion | flops 2155878400 | bytes 15799296 | tf_op jit(solution)/shard_map/dot_general | solution.py:205
  392.3 49.0 %reduce-scatter.2.cloned.1.call-done = bf16[1025,512]{1,0:T(8,128)(2,1)} async-done(((bf16[1025,2048]{1,0:T(8,128)(2,1)}), bf16[1025,512]{1,0:T(8,128)(2,1)}) %reduce-scatter.2.cloned.1.call-update) | async-done | bytes 1049616 | tf_op jit(solution)/shard_map/reduce_scatter | solution.py:208
  441.3 1.5 convert_element_type.274
  442.9 1.3 fusion.59
  (144 shorter events, 25.0 us)
Async XLA Ops:
  7.2 27.2 %copy-start.3 = (bf16[1,512]{1,0:T(2,128)(2,1)S(1)}, bf16[1,512]{1,0:T(2,128)(2,1)}, u32[]{:S(2)}) copy-start(bf16[1,512]{1,0:T(2,128)(2,1)} %param.20) | copy-start | bytes 3076
  7.2 27.2 %copy-start.1 = (bf16[1024,512]{1,0:T(8,128)(2,1)S(1)}, bf16[1024,512]{1,0:T(8,128)(2,1)}, u32[]{:S(2)}) copy-start(bf16[1024,512]{1,0:T(8,128)(2,1)} %param.19) | copy-start | bytes 3145732
  7.2 138.0 %all-gather.3.cloned.1.call-start = ((), (), s32[]{:S(2)}) async-start(), calls=%async_computation.6 | async-start | bytes 8650752 | tf_op jit(solution)/shard_map/all_gather | solution.py:79
  19.2 321.9 %all-gather.5.cloned.1.call-start = ((), (), s32[]{:S(2)}) async-start(), calls=%async_computation.7 | async-start | bytes 17301504 | tf_op jit(solution)/shard_map/all_gather | solution.py:79
  34.4 8.8 %copy-start.11 = (s32[32]{0:T(128)S(1)}, s32[32]{0:T(128)}, u32[]{:S(2)}) copy-start(s32[32]{0:T(128)} %param.31) | copy-start | bytes 388
  34.4 9.5 %copy-start.10 = (s32[32]{0:T(128)S(1)}, s32[32]{0:T(128)}, u32[]{:S(2)}) copy-start(s32[32]{0:T(128)} %param.30) | copy-start | bytes 388
  36.7 70.1 %all-to-all-start = ((bf16[4,1025,512]{2,1,0:T(8,128)(2,1)}), bf16[4,1025,512]{2,1,0:T(8,128)(2,1)}, u32[]{:S(2)}, u32[]{:S(2)}) async-start(bf16[4,1025,512]{2,1,0:T(8,128)(2,1)} %broadcast_in_dim.108), calls=%async_computation | async-start | bytes 8454144 | tf_op jit(solution)/shard_map/all_to_all | solution.py:93
  145.2 8.3 %copy-start.6 = (f32[2048]{0:T(1024)S(1)}, f32[2048]{0:T(1024)}, u32[]{:S(2)}) copy-start(f32[2048]{0:T(1024)} %param.22) | copy-start | bytes 24580
  145.2 8.3 %copy-start.8 = (f32[2048]{0:T(1024)S(1)}, f32[2048]{0:T(1024)}, u32[]{:S(2)}) copy-start(f32[2048]{0:T(1024)} %param.21) | copy-start | bytes 24580
  165.2 2.6 copy-start
  171.0 72.1 %all-to-all-start.2 = ((bf16[32,2,768]{2,1,0:T(2,128)(2,1)}), bf16[32,2,768]{2,1,0:T(2,128)(2,1)S(1)}, u32[]{:S(2)}, u32[]{:S(2)}) async-start(bf16[32,2,768]{2,1,0:T(2,128)(2,1)} %reshape.601), calls=%async_computation.2 | async-start | bytes 196608 | tf_op jit(solution)/shard_map/all_to_all | solution.py:148
  276.3 63.1 %all-to-all-start.3 = ((bf16[32,2,256]{2,1,0:T(2,128)(2,1)}), bf16[32,2,256]{2,1,0:T(2,128)(2,1)}, u32[]{:S(2)}, u32[]{:S(2)}) async-start(bf16[32,2,256]{2,1,0:T(2,128)(2,1)} %reshape.603), calls=%async_computation.3 | async-start | bytes 65536 | tf_op jit(solution)/shard_map/all_to_all | solution.py:198
  285.7 155.6 %reduce-scatter.2.cloned.1.call-start = ((), (), s32[]{:S(2)}) async-start(), calls=%async_computation.8 | async-start | bytes 5283840 | tf_op jit(solution)/shard_map/reduce_scatter | solution.py:208
  341.1 14.1 %copy-start.7 = (f32[2048]{0:T(1024)S(1)}, f32[2048]{0:T(1024)}, u32[]{:S(2)}) copy-start(f32[2048]{0:T(1024)} %param.22) | copy-start | bytes 24580
  341.1 14.1 %copy-start.9 = (f32[2048]{0:T(1024)S(1)}, f32[2048]{0:T(1024)}, u32[]{:S(2)}) copy-start(f32[2048]{0:T(1024)} %param.21) | copy-start | bytes 24580
  355.2 28.6 %copy-start.5 = (bf16[2,512,512]{2,1,0:T(8,128)(2,1)S(1)}, bf16[2,512,512]{2,1,0:T(8,128)(2,1)}, u32[]{:S(2)}) copy-start(bf16[2,512,512]{2,1,0:T(8,128)(2,1)} %get-tuple-element.270) | copy-start | bytes 3145732
  383.8 59.1 %copy-start.2 = (bf16[1024,512]{1,0:T(8,128)(2,1)S(1)}, bf16[1024,512]{1,0:T(8,128)(2,1)}, u32[]{:S(2)}) copy-start(bf16[1024,512]{1,0:T(8,128)(2,1)} %param.19) | copy-start | bytes 3145732
  392.3 51.9 %copy-start.4 = (bf16[1,512]{1,0:T(2,128)(2,1)S(1)}, bf16[1,512]{1,0:T(2,128)(2,1)}, u32[]{:S(2)}) copy-start(bf16[1,512]{1,0:T(2,128)(2,1)} %param.20) | copy-start | bytes 3076
Sparse Core Ops, SparseCore 0:
  19.3 124.9 all-gather.2
  147.4 157.5 all-gather.4
  392.4 48.8 reduce-scatter.1

commit v2 on v1

--- a/solution.py
+++ b/solution.py
@@ -7,7 +7,6 @@
 ROT = 32
 PLEN = 512
 CTX = 4096
-KEY_BLOCK = 512
 
 
 NEG = -1e30
@@ -36,16 +35,6 @@
             vectors[..., ROT:],
         ],
         axis=-1,
-    )
-
-
-def restore_rows(block, row_count, col_count):
-    width = block.shape[1]
-    shard_rows = block.shape[0] // (row_count * col_count)
-    return (
-        block.reshape(col_count, row_count, shard_rows, width)
-        .transpose(1, 0, 2, 3)
-        .reshape(row_count * col_count * shard_rows, width)
     )
 
 
@@ -77,21 +66,55 @@
         swapped = lax.all_to_all(joined, "row", split_axis=1, concat_axis=0, tiled=True)
         flat = swapped.reshape(swapped.shape[0], swapped.shape[2])
         gathered = lax.all_gather(flat, "col", axis=0, tiled=True)
-        restored = restore_rows(gathered, row_count, col_count)
         pieces = []
         offset = 0
         for w in weights:
             width = w.shape[1] // row_count
-            pieces.append(restored[:, offset:offset + width])
+            pieces.append(gathered[:, offset:offset + width])
             offset += width
         return pieces
+
+    def to_gathered(values):
+        lead = values.shape[:-1]
+        return (
+            values.reshape(lead + (row_count, col_count, -1))
+            .swapaxes(-3, -2)
+            .reshape(lead + (-1,))
+        )
+
+    def from_gathered(values):
+        lead = values.shape[:-1]
+        return (
+            values.reshape(lead + (col_count, row_count, -1))
+            .swapaxes(-3, -2)
+            .reshape(lead + (-1,))
+        )
 
     w_project, w_dense = regroup((project_weight, dense_weight))
     w_expand, w_reduce = regroup((expand_weight, reduce_weight))
     local_joined = jnp.concatenate([prompt_tokens, decode_tokens], axis=0)
-    spread = jnp.broadcast_to(local_joined[None], (row_count,) + local_joined.shape)
-    swapped_rows = lax.all_to_all(spread, "row", split_axis=0, concat_axis=0, tiled=True)
-    joined = swapped_rows.transpose(1, 0, 2).reshape(local_joined.shape[0], -1)
+    row_index = lax.axis_index("row")
+    shifted = [local_joined] + [
+        lax.ppermute(
+            local_joined, "row", [(j, (j + k) % row_count) for j in range(row_count)]
+        )
+        for k in range(1, row_count)
+    ]
+    relative = jnp.stack(shifted, axis=0)
+    blocks = jnp.stack(
+        [
+            lax.dynamic_index_in_dim(relative, (row_index - r) % row_count, 0, keepdims=False)
+            for r in range(row_count)
+        ],
+        axis=0,
+    )
+    joined = (
+        blocks.reshape(row_count, local_joined.shape[0], col_count, -1)
+        .transpose(1, 2, 0, 3)
+        .reshape(local_joined.shape[0], -1)
+    )
+    norm_gain = to_gathered(norm_gain)
+    norm_bias = to_gathered(norm_bias)
     prompt_full = joined[: prompt_tokens.shape[0]]
     decode_full = joined[prompt_tokens.shape[0]:]
     rows_prompt = prompt_full.shape[0]
@@ -158,23 +181,12 @@
     local_ages = lax.dynamic_slice_in_dim(cache_ages, first_slot, slot_local)
     keys_local = key_cache.reshape(slot_local, heads_local, CTX, HD)
     values_local = value_cache.reshape(slot_local, heads_local, CTX, HD)
-    block_count = CTX // KEY_BLOCK
-
-    def score_block(step, held):
-        start = step * KEY_BLOCK
-        keys_block = lax.dynamic_slice_in_dim(keys_local, start, KEY_BLOCK, 2)
-        block_scores = (
-            jnp.einsum("shd,shtd->sht", query, keys_block, preferred_element_type=jnp.float32)
-            * scale
-        )
-        key_places = start + jnp.arange(KEY_BLOCK, dtype=jnp.int32)
-        block_scores = jnp.where(
-            key_places[None, None, :] < local_ages[:, None, None], block_scores, NEG
-        )
-        return lax.dynamic_update_slice_in_dim(held, block_scores, start, 2)
-
-    cache_scores = lax.fori_loop(
-        0, block_count, score_block, jnp.full((slot_local, heads_local, CTX), NEG, jnp.float32)
+    cache_scores = (
+        jnp.einsum("shd,shtd->sht", query, keys_local, preferred_element_type=jnp.float32) * scale
+    )
+    key_places = jnp.arange(CTX, dtype=jnp.int32)
+    cache_scores = jnp.where(
+        key_places[None, None, :] < local_ages[:, None, None], cache_scores, NEG
     )
     own_score = jnp.sum(query.astype(jnp.float32) * own_key.astype(jnp.float32), axis=-1) * scale
     decode_top = jnp.maximum(jnp.max(cache_scores, axis=-1), own_score)
@@ -184,16 +196,10 @@
     cache_probs = (cache_raised / decode_total[:, :, None]).astype(half_float)
     own_prob = (own_raised / decode_total).astype(half_float)
 
-    def value_block(step, running):
-        start = step * KEY_BLOCK
-        probs_block = lax.dynamic_slice_in_dim(cache_probs, start, KEY_BLOCK, 2)
-        values_block = lax.dynamic_slice_in_dim(values_local, start, KEY_BLOCK, 2)
-        return running + jnp.einsum(
-            "sht,shtd->shd", probs_block, values_block, preferred_element_type=jnp.float32
-        )
-
     start_value = own_prob.astype(jnp.float32)[:, :, None] * own_value.astype(jnp.float32)
-    decode_sum = lax.fori_loop(0, block_count, value_block, start_value)
+    decode_sum = start_value + jnp.einsum(
+        "sht,shtd->shd", cache_probs, values_local, preferred_element_type=jnp.float32
+    )
     decode_mixed = decode_sum.astype(half_float).reshape(slot_local, heads_local * HD)
     returned = lax.all_to_all(
         jnp.broadcast_to(decode_mixed, (col_count,) + decode_mixed.shape[1:]),
@@ -206,7 +212,7 @@
         mixed_all, w_dense, (((1,), (1,)), ((), ())), preferred_element_type=jnp.float32
     )
     summed = lax.psum_scatter(
-        (attn_part + mlp_part).astype(half_float), "row", scatter_dimension=1, tiled=True
+        from_gathered(attn_part + mlp_part).astype(half_float), "row", scatter_dimension=1, tiled=True
     ).astype(jnp.float32)
     prompt_result = prompt_tokens.astype(jnp.float32) + summed[:rows_prompt]
     decode_result = decode_tokens.astype(jnp.float32) + summed[rows_prompt:]

time: 457 us -> 410 us (0.90)
  local copies, waits for them, and re-layouts: 141 us -> 112 us
  matrix products: 101 us -> 85 us
  waiting for transfers between devices: 110 us -> 124 us
  starting transfers between devices: 30.8 us -> 18.4 us
    all_gather x2, waiting for transfers between devices: 0.03 us -> 61.5 us  [regroup(): gathered = lax.all_gather(flat, 'col', axis=0, tiled=True)]
    all_to_all x1 -> x0, waiting for transfers between devices: 61 us -> none  [on_device(): lax.all_to_all(spread, 'row', split_axis=0, concat_axis=0, tiled=True)]
    reshape x4 -> x2, local copies, waits for them, and re-layouts: 44.8 us -> 0.15 us  [to_gathered(): values.reshape(lead + (row_count, col_count, -1)).swapaxes(-3, -2)]
    another operation x8 -> x2, local copies, waits for them, and re-layouts: 0.07 us -> 22.3 us
    convert_element_type x1, local copies, waits for them, and re-layouts: 19.4 us -> 1.25 us  [layer_norm(): values = rows.astype(jnp.float32)]
    dot_general x16 -> x2, matrix products: 24.6 us -> 10.3 us  [the longest x1 5.7 us: on_device(): jnp.einsum('shd,shtd->sht', query, keys_local, preferred_element_type=jnp...]
    ppermute x0 -> x3, waiting for transfers between devices: none -> 14.3 us  [on_device(): lax.ppermute(local_joined, 'row', [(j, (j + k) % row_count) for j in rang...]
    convert_element_type x0 -> x2, local copies, waits for them, and re-layouts: none -> 11.3 us  [on_device(): from_gathered(attn_part + mlp_part).astype(half_float)]
  transfers between devices with their start and end apart: 6 -> 8, of which waited for: 2 -> 4; matrix products, arithmetic and copies ran while one was open for 47% -> 41% of each run, Pallas kernels for 0% -> 0%
where the time goes in v2:
time: 410 us; the launch traced here: 404 us
  waiting for transfers between devices  124 us (30%)
  local copies, waits for them, and re-layouts  112 us (27%)
  matrix products  85 us (21%)
  other arithmetic  27.6 us (7%)
  blocking collectives  21.4 us (5%)
  starting transfers between devices  18.4 us (4%)
  between operations  15.2 us (4%)
    all_gather x2, waiting for transfers between devices, regroup(): gathered = lax.all_gather(flat, 'col', axis=0, tiled=True)  61.5 us
    reduce_scatter x1, waiting for transfers between devices, on_device(): lax.psum_scatter(from_gathered(attn_part + mlp_part).astype(half_float),...  48.4 us
    dot_general x1, matrix products, on_device(): lax.dot_general(hidden, w_reduce, (((1,), (1,)), ((), ())), preferred_ele...  28 us
    another operation x2, local copies, waits for them, and re-layouts  22.3 us
    all_to_all x2, blocking collectives, regroup(): lax.all_to_all(joined, 'row', split_axis=1, concat_axis=0, tiled=True)  21.4 us
    unnamed x42, local copies, waits for them, and re-layouts  20.3 us
    sub x2, matrix products, prompt_block(): raised = jnp.exp(scores - top)  16.3 us
    dynamic_slice x6, local copies, waits for them, and re-layouts, on_device(): lax.map(prompt_block, (prompt_blocks, prompt_lengths))  14.3 us
  transfers between devices with their start and end apart: 8, of which 4 were waited for; matrix products, arithmetic and copies ran while one was open for 41% of the time, Pallas kernels for 0%

profile of v2, /device:TPU:1, one launch (start us, length us, event | category | flops | bytes accessed | tf_op | source)
XLA Modules:
  0.0 404.4 jit_solution(2755625738567779040)
XLA Ops:
  7.2 1.1 convert_element_type.264
  8.5 0.9 convert_element_type.265
  9.8 9.5 %all_to_all.48 = bf16[16,4,2048]{2,0,1:T(8,128)(2,1)} all-to-all(bf16[16,4,2048]{2,0,1:T(8,128)(2,1)S(1)} %copy.136), channel_id=1, replica_groups=mesh['row'=4,'col'=32] {'row'}, dimensions={1} | all-to-all | bytes 524288 | tf_op jit(solution)/shard_map/all_to_all | solution.py:66
  19.3 1.1 convert_element_type.280
  21.5 11.9 %all_to_all.49 = bf16[16,4,4096]{2,0,1:T(8,128)(2,1)} all-to-all(bf16[16,4,4096]{2,0,1:T(8,128)(2,1)S(1)} %copy.147), channel_id=1, replica_groups=mesh['row'=4,'col'=32] {'row'}, dimensions={1} | all-to-all | bytes 1048576 | tf_op jit(solution)/shard_map/all_to_all | solution.py:66
  34.4 1.4 copy.127
  35.7 1.0 collective-permute-start
  36.7 1.4 collective-permute-start.1
  38.9 1.3 dynamic_slice.37
  40.2 1.2 dynamic_slice.38
  41.4 2.0 fusion.79
  44.0 6.2 %reshape.557 = bf16[2097152]{0:T(1024)(128)(2,1)} reshape(bf16[1,8,262144]{2,1,0:T(8,128)(2,1)} %param.23) | data formatting | bytes 8388608
  50.2 11.2 %reshape.536 = bf16[8,4096,64]{2,1,0:T(8,128)(2,1)} reshape(bf16[2097152]{0:T(1024)(128)(2,1)} %reshape.557) | data formatting | bytes 8388608 | tf_op jit(solution)/shard_map/reshape.17
  61.4 6.1 %reshape.555 = bf16[2097152]{0:T(1024)(128)(2,1)} reshape(bf16[1,8,262144]{2,1,0:T(8,128)(2,1)} %param.24) | data formatting | bytes 8388608
  67.4 11.1 %reshape.537 = bf16[8,4096,64]{2,1,0:T(8,128)(2,1)} reshape(bf16[2097152]{0:T(1024)(128)(2,1)} %reshape.555) | data formatting | bytes 8388608 | tf_op jit(solution)/shard_map/reshape.43
  78.6 1.7 copy.128
  80.3 14.3 %collective-permute-done.1 = bf16[1025,512]{1,0:T(8,128)(2,1)} collective-permute-done((bf16[1025,512]{1,0:T(8,128)(2,1)}, bf16[1025,512]{1,0:T(8,128)(2,1)}, u32[]{:S(2)}, u32[]{:S(2)}) %collective-permute-start.1) | collective-permute-done | bytes 1049632 | tf_op jit(solution)/shard_map/ppermute | solution.py:98
  94.5 2.4 copy.130
  96.9 2.4 copy.132
  99.2 2.1 pad_maximum_fusion.12
  101.7 1.7 maximum_convert_fusion
  103.9 1.2 copy.133
  105.1 2.7 fusion.92
  107.9 1.0 multiply_reduce_fusion
  108.9 3.6 fusion.26
  112.6 24.9 %all-gather.3.cloned.1.call-done = bf16[2048,2048]{1,0:T(8,128)(2,1)} async-done(((bf16[64,2048]{1,0:T(8,128)(2,1)}), bf16[2048,2048]{1,0:T(8,128)(2,1)}) %all-gather.3.cloned.1.call-update) | async-done | bytes 8388624 | tf_op jit(solution)/shard_map/all_gather | solution.py:68
  137.4 10.8 %fusion.44 = f32[1025,1536]{1,0:T(8,128)S(1)} fusion(bf16[1025,2048]{0,1:T(8,128)(2,1)} %fusion.26, bf16[2048,2048]{1,0:T(8,128)(2,1)} %all-gather.3.cloned.1.call-done), kind=kOutput, calls=%fused_computation.61 | convolution fusion | flops 6448742400 | bytes 17307648 | tf_op jit(solution)/shard_map/dot_general | solution.py:127
  148.3 2.7 copy-done.6
  152.3 1.2 reduce.17
  154.1 6.4 %all-to-all-start.1 = ((bf16[32,2,768]{2,1,0:T(2,128)(2,1)}), bf16[32,2,768]{2,1,0:T(2,128)(2,1)S(1)}, u32[]{:S(2)}, u32[]{:S(2)}) async-start(bf16[32,2,768]{2,1,0:T(2,128)(2,1)} %reshape.559), calls=%async_computation.1 | async-start | bytes 196608 | tf_op jit(solution)/shard_map/all_to_all | solution.py:171
  161.1 6.0 %slice.168 = f32[1024,1536]{1,0:T(8,128)} slice(f32[1025,1536]{1,0:T(8,128)} %copy-done.6), slice={[0:1024], [0:1536]} | slice | bytes 12582912 | tf_op jit(solution)/shard_map/slice | solution.py:153
  167.0 6.6 %copy.137 = f32[1024,1536]{0,1:T(8,128)} copy(f32[1024,1536]{1,0:T(8,128)} %slice.168) | data formatting | bytes 12582912 | tf_op jit(solution)/shard_map/slice | solution.py:153
  173.6 9.5 %reshape.531 = f32[2,512,8,3,64]{1,0,4,3,2:T(2,128)} reshape(f32[1024,1536]{0,1:T(8,128)} %copy.137) | data formatting | bytes 12582912 | tf_op jit(solution)/shard_map/reshape | solution.py:153
  183.6 5.7 %fusion.67 = f32[8,1,4096]{2,1,0:T(1,128)S(1)} fusion(bf16[8,4096,64]{2,1,0:T(8,128)(2,1)} %reshape.536, bf16[1,8,3,64]{3,2,1,0:T(4,128)(2,1)S(1)} %reshape.534), kind=kOutput, calls=%fused_computation.101 | convolution fusion | flops 4194304 | bytes 4329472 | tf_op jit(solution)/shard_map/shd,shtd->sht/dot_general | solution.py:185
  189.9 4.6 %fusion.56 = f32[8,1,64]{2,1,0:T(1,128)S(1)} fusion(bf16[8,4096,64]{2,1,0:T(8,128)(2,1)} %reshape.537, bf16[8,4096,1]{1,0,2:T(8,128)(2,1)S(1)} %fusion.62), kind=kOutput, calls=%fused_computation.81 | convolution fusion | flops 4194304 | bytes 4261888 | tf_op jit(solution)/shard_map/sht,shtd->shd/dot_general | solution.py:200
  194.8 0.8 reduce.18
  196.2 9.3 %all-to-all-start.2 = ((bf16[32,2,256]{2,1,0:T(2,128)(2,1)}), bf16[32,2,256]{2,1,0:T(2,128)(2,1)}, u32[]{:S(2)}, u32[]{:S(2)}) async-start(bf16[32,2,256]{2,1,0:T(2,128)(2,1)} %reshape.561), calls=%async_computation.2 | async-start | bytes 65536 | tf_op jit(solution)/shard_map/all_to_all | solution.py:204
  205.6 52.5 %while.14 = (s32[]{:T(128)}, bf16[2,512,512]{2,1,0:T(8,128)(2,1)}, f32[2,512,8,3,64]{1,0,4,3,2:T(2,128)}, s32[2]{0:T(128)S(1)}, s32[]{:T(128)}) while((s32[]{:T(128)}, bf16[2,512,512]{2,1,0:T(8,128)(2,1)}, f32[2,512,8,3,64]{1,0,4,3,2:T(2,128)}, s32[2]{0:T(128)S(1)}, s32[]{:T(128)}) %tuple.82), condition=%wide.region_5.6_spmd.clone.clone, body=%wide.region_2.5_spmd.clone.clone.sunk | while | flops 554444288 | bytes 41064144 | solution.py:154
  206.0 6.1 %constant_dynamic-slice_fusion.6 = f32[1,512,8,3,64]{1,0,4,3,2:T(1,128)S(1)} fusion(f32[2,512,8,3,64]{1,0,4,3,2:T(2,128)} %get-tuple-element.263, s32[]{:T(128)} %get-tuple-element.256), kind=kLoop, calls=%fused_computation.34.clone.1 | loop fusion | bytes 6291460 | tf_op jit(solution)/shard_map/while/body/jit(dynamic_index_in_dim)/dynamic_slice | solution.py:154
  213.0 0.9 subtract_convert_fusion.5
  215.9 0.8 fusion.104
  216.8 8.2 %fusion.105 = (f32[8,512]{1,0:T(8,128)}, f32[8,512,512]{1,2,0:T(8,128)}) fusion(pred[512,512]{0,1:T(8,128)(4,1)} %fusion.104, bf16[512,8,32]{0,2,1:T(8,128)(2,1)S(1)} %slice.266, bf16[512,8,16]{0,2,1:T(8,128)(2,1)} %get-tuple-element.245, bf16[512,8,16]{0,2,1:T(8,128)(2,1)} %get-tuple-element.246, bf16[512,8,32]{0,2,1:T(8,128)(2,1)} %slice.267, ...), kind=kOutput, calls=%fused_computation.145.clone.1 | convolution fusion | flops 279970304 | bytes 9715712 | tf_op jit(solution)/shard_map/while/body/eval_jaxpr/sub | solution.py:148
  224.9 5.0 %fusion.106 = bf16[8,64,512]{2,1,0:T(8,128)(2,1)} fusion(f32[8,512,512]{1,2,0:T(8,128)} %get-tuple-element.249, f32[8,512]{1,0:T(8,128)} %get-tuple-element.250, f32[512,8,3,64]{0,3,1,2:T(8,128)S(1)} %bitcast.121), kind=kOutput, calls=%fused_computation.12.clone.1 | convolution fusion | flops 272891904 | bytes 9453568 | tf_op jit(solution)/shard_map/while/body/eval_jaxpr/hqk,khd->qhd/dot_general | solution.py:150
  230.0 1.3 copy.189
  231.3 0.8 constant_dynamic-update-slice_fusion.2
  232.1 6.1 %constant_dynamic-slice_fusion.6 = f32[1,512,8,3,64]{1,0,4,3,2:T(1,128)S(1)} fusion(f32[2,512,8,3,64]{1,0,4,3,2:T(2,128)} %get-tuple-element.263, s32[]{:T(128)} %get-tuple-element.256), kind=kLoop, calls=%fused_computation.34.clone.1 | loop fusion | bytes 6291460 | tf_op jit(solution)/shard_map/while/body/jit(dynamic_index_in_dim)/dynamic_slice | solution.py:154
  239.1 0.9 subtract_convert_fusion.5
  240.0 0.7 slice.267
  242.0 0.8 fusion.104
  242.8 8.2 %fusion.105 = (f32[8,512]{1,0:T(8,128)}, f32[8,512,512]{1,2,0:T(8,128)}) fusion(pred[512,512]{0,1:T(8,128)(4,1)} %fusion.104, bf16[512,8,32]{0,2,1:T(8,128)(2,1)S(1)} %slice.266, bf16[512,8,16]{0,2,1:T(8,128)(2,1)} %get-tuple-element.245, bf16[512,8,16]{0,2,1:T(8,128)(2,1)} %get-tuple-element.246, bf16[512,8,32]{0,2,1:T(8,128)(2,1)} %slice.267, ...), kind=kOutput, calls=%fused_computation.145.clone.1 | convolution fusion | flops 279970304 | bytes 9715712 | tf_op jit(solution)/shard_map/while/body/eval_jaxpr/sub | solution.py:148
  251.0 5.0 %fusion.106 = bf16[8,64,512]{2,1,0:T(8,128)(2,1)} fusion(f32[8,512,512]{1,2,0:T(8,128)} %get-tuple-element.249, f32[8,512]{1,0:T(8,128)} %get-tuple-element.250, f32[512,8,3,64]{0,3,1,2:T(8,128)S(1)} %bitcast.121), kind=kOutput, calls=%fused_computation.12.clone.1 | convolution fusion | flops 272891904 | bytes 9453568 | tf_op jit(solution)/shard_map/while/body/eval_jaxpr/hqk,khd->qhd/dot_general | solution.py:150
  256.0 1.3 copy.189
  257.3 0.8 constant_dynamic-update-slice_fusion.2
  258.1 0.8 reshape.562
  258.9 0.8 fusion.63
  259.7 36.6 %all-gather.5.cloned.1.call-done = bf16[2048,4096]{1,0:T(8,128)(2,1)} async-done(((bf16[64,4096]{1,0:T(8,128)(2,1)}), bf16[2048,4096]{1,0:T(8,128)(2,1)}) %all-gather.5.cloned.1.call-update) | async-done | bytes 16777232 | tf_op jit(solution)/shard_map/all_gather | solution.py:68
  296.4 28.0 %fusion.35 = f32[1025,2048]{1,0:T(8,128)} fusion(bf16[2048,4096]{1,0:T(8,128)(2,1)} %all-gather.5.cloned.1.call-done, bf16[1025,2048]{0,1:T(8,128)(2,1)} %fusion.26), kind=kOutput, calls=%fused_computation.56 | convolution fusion | flops 17215539200 | bytes 29372416 | tf_op jit(solution)/shard_map/dot_general | solution.py:131
  324.4 8.5 %fusion.41 = bf16[1025,2048]{1,0:T(8,128)(2,1)} fusion(f32[1025,2048]{1,0:T(8,128)} %fusion.35, bf16[2048,2048]{1,0:T(8,128)(2,1)} %all-gather.3.cloned.1.call-done, bf16[1,512]{1,0:T(2,128)(2,1)S(1)} %convert_element_type.279, bf16[1024,512]{1,0:T(8,128)(2,1)S(1)} %bitcast.142), kind=kOutput, calls=%fused_computation.60 | convolution fusion | flops 2155878400 | bytes 15799296 | tf_op jit(solution)/shard_map/dot_general | solution.py:211
  332.9 6.4 %copy.148 = bf16[1025,2048]{0,1:T(8,128)(2,1)} copy(bf16[1025,2048]{1,0:T(8,128)(2,1)} %fusion.41) | data formatting | bytes 8396800 | tf_op jit(solution)/shard_map/convert_element_type | solution.py:215
  339.3 4.9 %copy.149 = bf16[1025,4,32,16]{0,3,2,1:T(8,128)(2,1)} copy(bf16[1025,4,32,16]{0,3,1,2:T(8,128)(2,1)} %bitcast.125) | data formatting | bytes 8396800 | tf_op jit(solution)/shard_map/convert_element_type | solution.py:215
  344.2 48.4 %reduce-scatter.2.cloned.1.call-done = bf16[1025,512]{0,1:T(8,128)(2,1)} async-done(((bf16[1025,2048]{0,1:T(8,128)(2,1)}), bf16[1025,512]{0,1:T(8,128)(2,1)}) %reduce-scatter.2.cloned.1.call-update) | async-done | bytes 1049616 | tf_op jit(solution)/shard_map/reduce_scatter | solution.py:214
  392.6 1.4 convert_element_type.287
  394.4 1.3 copy.152
  395.7 0.9 slice.180
  (124 shorter events, 14.7 us)
Async XLA Ops:
  7.2 13.4 %copy-start.8 = (f32[16,8192]{1,0:T(8,128)S(1)}, f32[16,8192]{1,0:T(8,128)}, u32[]{:S(2)}) copy-start(f32[16,8192]{1,0:T(8,128)} %param.22) | copy-start | bytes 1572868
  7.2 26.2 %copy-start.7 = (bf16[1024,512]{1,0:T(8,128)(2,1)S(1)}, bf16[1024,512]{1,0:T(8,128)(2,1)}, u32[]{:S(2)}) copy-start(bf16[1024,512]{1,0:T(8,128)(2,1)} %param.15) | copy-start | bytes 3145732
  7.2 130.3 %all-gather.3.cloned.1.call-start = ((), (), s32[]{:S(2)}) async-start(), calls=%async_computation.5 | async-start | bytes 8650752 | tf_op jit(solution)/shard_map/all_gather | solution.py:68
  9.8 24.2 %copy-start.9 = (bf16[1,512]{1,0:T(2,128)(2,1)S(1)}, bf16[1,512]{1,0:T(2,128)(2,1)}, u32[]{:S(2)}) copy-start(bf16[1,512]{1,0:T(2,128)(2,1)} %param.16) | copy-start | bytes 3076
  19.3 277.1 %all-gather.5.cloned.1.call-start = ((), (), s32[]{:S(2)}) async-start(), calls=%async_computation.6 | async-start | bytes 17301504 | tf_op jit(solution)/shard_map/all_gather | solution.py:68
  21.4 16.9 %copy-start.11 = (f32[2048]{0:T(1024)S(1)}, f32[2048]{0:T(1024)}, u32[]{:S(2)}) copy-start(f32[2048]{0:T(1024)} %param.18) | copy-start | bytes 24580
  33.4 5.2 %copy-start.12 = (f32[2048]{0:T(1024)S(1)}, f32[2048]{0:T(1024)}, u32[]{:S(2)}) copy-start(f32[2048]{0:T(1024)} %param.17) | copy-start | bytes 24580
  34.0 16.2 %copy-start.4 = (bf16[1024,512]{0,1:T(8,128)(2,1)}, bf16[1024,512]{0,1:T(8,128)(2,1)S(1)}, u32[]{:S(2)}) copy-start(bf16[1024,512]{0,1:T(8,128)(2,1)S(1)} %copy.124) | copy-start | bytes 3145732
  35.7 42.8 %collective-permute-start = (bf16[1025,512]{1,0:T(8,128)(2,1)}, bf16[1025,512]{1,0:T(8,128)(2,1)}, u32[]{:S(2)}, u32[]{:S(2)}) collective-permute-start(bf16[1025,512]{1,0:T(8,128)(2,1)} %copy.127), channel_id=1, source_target_pairs={{0,32},{32,64},{64,96},{96,0},{1,33},{33,65},{65,97},{97,1},{2,34}... | collective-permute-start | bytes 3148808 | tf_op jit(solution)/shard_map/ppermute | solution.py:98
  36.7 57.8 %collective-permute-start.1 = (bf16[1025,512]{1,0:T(8,128)(2,1)}, bf16[1025,512]{1,0:T(8,128)(2,1)}, u32[]{:S(2)}, u32[]{:S(2)}) collective-permute-start(bf16[1025,512]{1,0:T(8,128)(2,1)} %copy.127), channel_id=1, source_target_pairs={{0,64},{32,96},{64,0},{96,32},{1,65},{33,97},{65,1},{97,33},{2,66}... | collective-permute-start | bytes 3148808 | tf_op jit(solution)/shard_map/ppermute | solution.py:98
  38.1 58.7 %collective-permute-start.2 = (bf16[1025,512]{1,0:T(8,128)(2,1)}, bf16[1025,512]{1,0:T(8,128)(2,1)}, u32[]{:S(2)}, u32[]{:S(2)}) collective-permute-start(bf16[1025,512]{1,0:T(8,128)(2,1)} %copy.127), channel_id=1, source_target_pairs={{0,96},{32,0},{64,32},{96,64},{1,97},{33,1},{65,33},{97,65},{2,98}... | collective-permute-start | bytes 3148808 | tf_op jit(solution)/shard_map/ppermute | solution.py:98
  101.7 1.7 copy-start
  101.7 1.7 copy-start.1
  101.7 1.8 copy-start.2
  101.7 2.1 copy-start.3
  148.3 2.7 copy-start.6
  154.1 29.0 %all-to-all-start.1 = ((bf16[32,2,768]{2,1,0:T(2,128)(2,1)}), bf16[32,2,768]{2,1,0:T(2,128)(2,1)S(1)}, u32[]{:S(2)}, u32[]{:S(2)}) async-start(bf16[32,2,768]{2,1,0:T(2,128)(2,1)} %reshape.559), calls=%async_computation.1 | async-start | bytes 196608 | tf_op jit(solution)/shard_map/all_to_all | solution.py:171
  173.6 9.6 %copy-start.14 = (s32[32]{0:T(128)S(1)}, s32[32]{0:T(128)}, u32[]{:S(2)}) copy-start(s32[32]{0:T(128)} %param.27) | copy-start | bytes 388
  189.9 15.7 %copy-start.15 = (s32[2]{0:T(128)S(1)}, s32[2]{0:T(128)}, u32[]{:S(2)}) copy-start(s32[2]{0:T(128)} %param.25) | copy-start | bytes 28
  196.2 61.9 %all-to-all-start.2 = ((bf16[32,2,256]{2,1,0:T(2,128)(2,1)}), bf16[32,2,256]{2,1,0:T(2,128)(2,1)}, u32[]{:S(2)}, u32[]{:S(2)}) async-start(bf16[32,2,256]{2,1,0:T(2,128)(2,1)} %reshape.561), calls=%async_computation.2 | async-start | bytes 65536 | tf_op jit(solution)/shard_map/all_to_all | solution.py:204
  205.5 187.1 %reduce-scatter.2.cloned.1.call-start = ((), (), s32[]{:S(2)}) async-start(), calls=%async_computation.7 | async-start | bytes 5898240 | tf_op jit(solution)/shard_map/reduce_scatter | solution.py:214
  259.7 64.7 %copy-start.13 = (bf16[2,512,512]{2,1,0:T(8,128)(2,1)S(1)}, bf16[2,512,512]{2,1,0:T(8,128)(2,1)}, u32[]{:S(2)}) copy-start(bf16[2,512,512]{2,1,0:T(8,128)(2,1)} %get-tuple-element.97) | copy-start | bytes 3145732
  344.2 49.8 %copy-start.5 = (bf16[1024,512]{0,1:T(8,128)(2,1)S(1)}, bf16[1024,512]{0,1:T(8,128)(2,1)}, u32[]{:S(2)}) copy-start(bf16[1024,512]{0,1:T(8,128)(2,1)} %copy-done.4) | copy-start | bytes 3145732
  344.2 52.5 %copy-start.10 = (bf16[1,512]{1,0:T(2,128)(2,1)S(1)}, bf16[1,512]{1,0:T(2,128)(2,1)}, u32[]{:S(2)}) copy-start(bf16[1,512]{1,0:T(2,128)(2,1)} %param.16) | copy-start | bytes 3076
Sparse Core Ops, SparseCore 0:
  19.4 117.9 all-gather.2
  140.5 155.8 all-gather.4
  344.3 48.2 reduce-scatter.1

commit v3 on v2

--- a/solution.py
+++ b/solution.py
@@ -10,6 +10,7 @@
 
 
 NEG = -1e30
+COL = ("col_y", "col_z", "col_x")
 
 
 def layer_norm(rows, gain, bias):
@@ -55,7 +56,7 @@
 ):
     half_float = jnp.bfloat16
     row_count = lax.axis_size("row")
-    col_count = lax.axis_size("col")
+    col_count = lax.axis_size(COL)
 
     def by_row_group(weight):
         local_rows, width = weight.shape
@@ -65,7 +66,8 @@
         joined = jnp.concatenate([by_row_group(w) for w in weights], axis=2)
         swapped = lax.all_to_all(joined, "row", split_axis=1, concat_axis=0, tiled=True)
         flat = swapped.reshape(swapped.shape[0], swapped.shape[2])
-        gathered = lax.all_gather(flat, "col", axis=0, tiled=True)
+        gathered = lax.all_gather(flat, COL[-1], axis=0, tiled=True)
+        gathered = lax.all_gather(gathered, COL[:-1], axis=0, tiled=True)
         pieces = []
         offset = 0
         for w in weights:
@@ -154,7 +156,7 @@
     prompt_mixed = lax.map(prompt_block, (prompt_blocks, prompt_lengths)).reshape(
         rows_prompt, heads_local * HD
     )
-    col_index = lax.axis_index("col")
+    col_index = lax.axis_index(COL)
     first_slot = col_index * slot_local
     local_ids = first_slot + jnp.arange(slot_local, dtype=jnp.int32)
     own_request = lax.dynamic_slice_in_dim(slot_request, first_slot, slot_local)
@@ -170,7 +172,7 @@
     )
     handed = lax.all_to_all(
         jnp.broadcast_to(packed, (col_count,) + packed.shape[1:]),
-        "col", split_axis=0, concat_axis=0, tiled=True,
+        COL, split_axis=0, concat_axis=0, tiled=True,
     )
     chooser = (slot_request[None, :] == local_ids[:, None]).astype(half_float)
     mine = jnp.dot(chooser, handed, preferred_element_type=jnp.float32).astype(half_float)
@@ -203,7 +205,7 @@
     decode_mixed = decode_sum.astype(half_float).reshape(slot_local, heads_local * HD)
     returned = lax.all_to_all(
         jnp.broadcast_to(decode_mixed, (col_count,) + decode_mixed.shape[1:]),
-        "col", split_axis=0, concat_axis=0, tiled=True,
+        COL, split_axis=0, concat_axis=0, tiled=True,
     )
     picker = slot_match.astype(half_float)
     decode_heads = jnp.dot(picker, returned, preferred_element_type=jnp.float32).astype(half_float)
@@ -220,22 +222,26 @@
 
 
 def solution(mesh):
+    col_size = mesh.shape["col"]
+    fine_mesh = jax.sharding.Mesh(
+        mesh.devices.reshape(mesh.shape["row"], 4, col_size // 8, 2), ("row",) + COL
+    )
     in_specs = (
-        P("col", "row"),
-        P("col", "row"),
-        P(),
-        P(),
-        P(("row", "col"), None),
-        P(("row", "col"), None),
-        P(("row", "col"), None),
-        P(("row", "col"), None),
-        P("col", "row", None),
-        P("col", "row", None),
-        P("col"),
-        P(),
-        P(),
-    )
-    out_specs = (P("col", "row"), P("col", "row"))
+        P(COL, "row"),
+        P(COL, "row"),
+        P(),
+        P(),
+        P(("row",) + COL, None),
+        P(("row",) + COL, None),
+        P(("row",) + COL, None),
+        P(("row",) + COL, None),
+        P(COL, "row", None),
+        P(COL, "row", None),
+        P(COL),
+        P(),
+        P(),
+    )
+    out_specs = (P(COL, "row"), P(COL, "row"))
     return jax.shard_map(
-        on_device, mesh=mesh, in_specs=in_specs, out_specs=out_specs, check_vma=False
-    )
+        on_device, mesh=fine_mesh, in_specs=in_specs, out_specs=out_specs, check_vma=False
+    )

time: 410 us -> 370 us (0.902)
  waiting for transfers between devices: 124 us -> 70.6 us
  blocking collectives: 21.4 us -> 34.6 us
    all_gather x2 -> x3, waiting for transfers between devices: 61.5 us -> 14.2 us  [the longest x1 8 us: regroup(): gathered = lax.all_gather(flat, COL[-1], axis=0, tiled=True)]
    all_gather x0 -> x1, blocking collectives: none -> 13.8 us  [regroup(): gathered = lax.all_gather(flat, COL[-1], axis=0, tiled=True)]
    ppermute x3, waiting for transfers between devices: 14.3 us -> 4.19 us  [on_device(): lax.ppermute(local_joined, 'row', [(j, (j + k) % row_count) for j in rang...]
    unnamed x42 -> x44, local copies, waits for them, and re-layouts: 20.3 us -> 20.4 us
  transfers between devices with their start and end apart: 8 -> 9, of which waited for: 4 -> 4; matrix products, arithmetic and copies ran while one was open for 41% -> 45% of each run, Pallas kernels for 0% -> 0%
where the time goes in v3:
time: 370 us; the launch traced here: 364 us
  local copies, waits for them, and re-layouts  113 us (31%)
  matrix products  85.2 us (23%)
  waiting for transfers between devices  70.6 us (19%)
  blocking collectives  34.6 us (9%)
  other arithmetic  26.6 us (7%)
  starting transfers between devices  19 us (5%)
  between operations  15.2 us (4%)
    reduce_scatter x1, waiting for transfers between devices, on_device(): lax.psum_scatter(from_gathered(attn_part + mlp_part).astype(half_float),...  52.2 us
    dot_general x1, matrix products, on_device(): lax.dot_general(hidden, w_reduce, (((1,), (1,)), ((), ())), preferred_ele...  28.1 us
    another operation x2, local copies, waits for them, and re-layouts  22.4 us
    all_to_all x2, blocking collectives, regroup(): lax.all_to_all(joined, 'row', split_axis=1, concat_axis=0, tiled=True)  20.8 us
    unnamed x44, local copies, waits for them, and re-layouts  20.4 us
    sub x2, matrix products, prompt_block(): raised = jnp.exp(scores - top)  16.4 us
    dynamic_slice x6, local copies, waits for them, and re-layouts, on_device(): lax.map(prompt_block, (prompt_blocks, prompt_lengths))  14.5 us
    all_gather x1, blocking collectives, regroup(): gathered = lax.all_gather(flat, COL[-1], axis=0, tiled=True)  13.8 us
  transfers between devices with their start and end apart: 9, of which 4 were waited for; matrix products, arithmetic and copies ran while one was open for 45% of the time, Pallas kernels for 0%

profile of v3, /device:TPU:1, one launch (start us, length us, event | category | flops | bytes accessed | tf_op | source)
XLA Modules:
  0.0 364.3 jit_solution(13441300319603228485)
XLA Ops:
  7.2 1.1 convert_element_type.280
  8.5 1.1 convert_element_type.281
  10.4 12.3 %all_to_all.48 = bf16[16,4,4096]{2,0,1:T(8,128)(2,1)} all-to-all(bf16[16,4,4096]{2,0,1:T(8,128)(2,1)S(1)} %copy.147), channel_id=1, replica_groups=mesh['row'=4,'col_y'=4,'col_z'=4,'col_x'=2] {'row'}, dimensions={1} | all-to-all | bytes 1048576 | tf_op jit(solution)/shard_map/all_to_all | solution.py:67
  23.4 8.4 %all_to_all.49 = bf16[16,4,2048]{2,0,1:T(8,128)(2,1)S(1)} all-to-all(bf16[16,4,2048]{2,0,1:T(8,128)(2,1)S(1)} %copy.136), channel_id=1, replica_groups=mesh['row'=4,'col_y'=4,'col_z'=4,'col_x'=2] {'row'}, dimensions={1} | all-to-all | bytes 524288 | tf_op jit(solution)/shard_map/all_to_all | solution.py:67
  31.8 13.8 %all_gather.12 = bf16[128,2048]{1,0:T(8,128)(2,1)} all-gather(bf16[64,2048]{1,0:T(8,128)(2,1)S(1)} %bitcast.131), channel_id=1, replica_groups=mesh['row'=4,'col_y'=4,'col_z'=4,'col_x'=2] {'col_x'}, dimensions={0}, use_global_device_ids=true | all-gather | bytes 786432 | tf_op jit(solution)/shard_map/all_gather | solution.py:69
  45.7 8.0 %all-gather.6.cloned.1.call-done = bf16[128,4096]{1,0:T(8,128)(2,1)} async-done(((bf16[64,4096]{1,0:T(8,128)(2,1)}), bf16[128,4096]{1,0:T(8,128)(2,1)}) %all-gather.6.cloned.1.call-update) | async-done | bytes 1048592 | tf_op jit(solution)/shard_map/all_gather | solution.py:69
  54.7 1.4 copy.127
  56.1 0.8 collective-permute-start
  56.9 1.0 collective-permute-start.1
  58.7 1.2 dynamic_slice.37
  59.9 1.3 dynamic_slice.38
  61.2 1.9 fusion.79
  63.7 6.2 %reshape.557 = bf16[2097152]{0:T(1024)(128)(2,1)} reshape(bf16[1,8,262144]{2,1,0:T(8,128)(2,1)} %param.23) | data formatting | bytes 8388608
  69.8 11.1 %reshape.536 = bf16[8,4096,64]{2,1,0:T(8,128)(2,1)} reshape(bf16[2097152]{0:T(1024)(128)(2,1)} %reshape.557) | data formatting | bytes 8388608 | tf_op jit(solution)/shard_map/reshape.17
  80.9 6.0 %reshape.555 = bf16[2097152]{0:T(1024)(128)(2,1)} reshape(bf16[1,8,262144]{2,1,0:T(8,128)(2,1)} %param.24) | data formatting | bytes 8388608
  87.0 11.3 %reshape.537 = bf16[8,4096,64]{2,1,0:T(8,128)(2,1)} reshape(bf16[2097152]{0:T(1024)(128)(2,1)} %reshape.555) | data formatting | bytes 8388608 | tf_op jit(solution)/shard_map/reshape.43
  98.3 1.7 copy.128
  100.0 4.2 %collective-permute-done.1 = bf16[1025,512]{1,0:T(8,128)(2,1)} collective-permute-done((bf16[1025,512]{1,0:T(8,128)(2,1)}, bf16[1025,512]{1,0:T(8,128)(2,1)}, u32[]{:S(2)}, u32[]{:S(2)}) %collective-permute-start.1) | collective-permute-done | bytes 1049632 | tf_op jit(solution)/shard_map/ppermute | solution.py:100
  104.2 2.4 copy.130
  106.6 2.4 copy.132
  108.9 2.1 pad_maximum_fusion.12
  111.5 1.7 maximum_convert_fusion
  113.6 1.2 copy.133
  114.9 2.9 fusion.92
  117.8 1.0 multiply_reduce_fusion
  118.8 3.7 %fusion.26 = bf16[1025,2048]{0,1:T(8,128)(2,1)} fusion(f32[1025,32,4,16]{0,3,2,1:T(8,128)S(1)} %copy.133, f32[2048]{0:T(1024)S(1)} %add.131, f32[2048]{0:T(1024)S(1)} %mul.371, f32[1025]{0:T(1024)S(1)} %add_rsqrt_fusion, f32[1025]{0:T(1024)S(1)} %broadcast_multiply_fusion), kind=kLoop, calls=%fused_computation.45 | loop fusion | flops 10496000 | bytes 12619784 | tf_op jit(solution)/shard_map/convert_element_type | solution.py:21
  122.4 6.2 %all-gather.4.cloned.1.call-done = bf16[2048,2048]{1,0:T(8,128)(2,1)} async-done(((bf16[128,2048]{1,0:T(8,128)(2,1)}), bf16[2048,2048]{1,0:T(8,128)(2,1)}) %all-gather.4.cloned.1.call-update) | async-done | bytes 8388624 | tf_op jit(solution)/shard_map/all_gather | solution.py:70
  128.6 10.8 %fusion.44 = f32[1025,1536]{1,0:T(8,128)S(1)} fusion(bf16[1025,2048]{0,1:T(8,128)(2,1)} %fusion.26, bf16[2048,2048]{1,0:T(8,128)(2,1)} %all-gather.4.cloned.1.call-done), kind=kOutput, calls=%fused_computation.61 | convolution fusion | flops 6448742400 | bytes 17307648 | tf_op jit(solution)/shard_map/dot_general | solution.py:129
  139.4 2.8 copy-done.6
  143.6 1.2 reduce.17
  145.4 7.6 %all-to-all-start.1 = ((bf16[32,2,768]{2,1,0:T(2,128)(2,1)}), bf16[32,2,768]{2,1,0:T(2,128)(2,1)S(1)}, u32[]{:S(2)}, u32[]{:S(2)}) async-start(bf16[32,2,768]{2,1,0:T(2,128)(2,1)} %reshape.559), calls=%async_computation.1 | async-start | bytes 196608 | tf_op jit(solution)/shard_map/all_to_all | solution.py:173
  153.7 6.0 %slice.168 = f32[1024,1536]{1,0:T(8,128)} slice(f32[1025,1536]{1,0:T(8,128)} %copy-done.6), slice={[0:1024], [0:1536]} | slice | bytes 12582912 | tf_op jit(solution)/shard_map/slice | solution.py:155
  159.7 6.7 %copy.137 = f32[1024,1536]{0,1:T(8,128)} copy(f32[1024,1536]{1,0:T(8,128)} %slice.168) | data formatting | bytes 12582912 | tf_op jit(solution)/shard_map/slice | solution.py:155
  166.4 9.4 %reshape.531 = f32[2,512,8,3,64]{1,0,4,3,2:T(2,128)} reshape(f32[1024,1536]{0,1:T(8,128)} %copy.137) | data formatting | bytes 12582912 | tf_op jit(solution)/shard_map/reshape | solution.py:155
  176.3 5.6 %fusion.67 = f32[8,1,4096]{2,1,0:T(1,128)S(1)} fusion(bf16[8,4096,64]{2,1,0:T(8,128)(2,1)} %reshape.536, bf16[1,8,3,64]{3,2,1,0:T(4,128)(2,1)S(1)} %reshape.534), kind=kOutput, calls=%fused_computation.101 | convolution fusion | flops 4194304 | bytes 4329472 | tf_op jit(solution)/shard_map/shd,shtd->sht/dot_general | solution.py:187
  182.5 4.7 %fusion.56 = f32[8,1,64]{2,1,0:T(1,128)S(1)} fusion(bf16[8,4096,64]{2,1,0:T(8,128)(2,1)} %reshape.537, bf16[8,4096,1]{1,0,2:T(8,128)(2,1)S(1)} %fusion.62), kind=kOutput, calls=%fused_computation.81 | convolution fusion | flops 4194304 | bytes 4261888 | tf_op jit(solution)/shard_map/sht,shtd->shd/dot_general | solution.py:202
  187.5 0.8 reduce.18
  188.9 9.2 %all-to-all-start.2 = ((bf16[32,2,256]{2,1,0:T(2,128)(2,1)}), bf16[32,2,256]{2,1,0:T(2,128)(2,1)}, u32[]{:S(2)}, u32[]{:S(2)}) async-start(bf16[32,2,256]{2,1,0:T(2,128)(2,1)} %reshape.561), calls=%async_computation.2 | async-start | bytes 65536 | tf_op jit(solution)/shard_map/all_to_all | solution.py:206
  198.2 52.7 %while.14 = (s32[]{:T(128)}, bf16[2,512,512]{2,1,0:T(8,128)(2,1)}, f32[2,512,8,3,64]{1,0,4,3,2:T(2,128)}, s32[2]{0:T(128)S(1)}, s32[]{:T(128)}) while((s32[]{:T(128)}, bf16[2,512,512]{2,1,0:T(8,128)(2,1)}, f32[2,512,8,3,64]{1,0,4,3,2:T(2,128)}, s32[2]{0:T(128)S(1)}, s32[]{:T(128)}) %tuple.84), condition=%wide.region_5.6_spmd.clone.clone, body=%wide.region_2.5_spmd.clone.clone.sunk | while | flops 554444288 | bytes 41064144 | solution.py:156
  198.6 6.3 %constant_dynamic-slice_fusion.6 = f32[1,512,8,3,64]{1,0,4,3,2:T(1,128)S(1)} fusion(f32[2,512,8,3,64]{1,0,4,3,2:T(2,128)} %get-tuple-element.263, s32[]{:T(128)} %get-tuple-element.256), kind=kLoop, calls=%fused_computation.34.clone.1 | loop fusion | bytes 6291460 | tf_op jit(solution)/shard_map/while/body/jit(dynamic_index_in_dim)/dynamic_slice | solution.py:156
  205.9 0.9 subtract_convert_fusion.5
  206.8 0.7 slice.267
  208.7 0.8 fusion.104
  209.5 8.2 %fusion.105 = (f32[8,512]{1,0:T(8,128)}, f32[8,512,512]{1,2,0:T(8,128)}) fusion(pred[512,512]{0,1:T(8,128)(4,1)} %fusion.104, bf16[512,8,32]{0,2,1:T(8,128)(2,1)S(1)} %slice.266, bf16[512,8,16]{0,2,1:T(8,128)(2,1)} %get-tuple-element.245, bf16[512,8,16]{0,2,1:T(8,128)(2,1)} %get-tuple-element.246, bf16[512,8,32]{0,2,1:T(8,128)(2,1)} %slice.267, ...), kind=kOutput, calls=%fused_computation.145.clone.1 | convolution fusion | flops 279970304 | bytes 9715712 | tf_op jit(solution)/shard_map/while/body/eval_jaxpr/sub | solution.py:150
  217.8 5.1 %fusion.106 = bf16[8,64,512]{2,1,0:T(8,128)(2,1)} fusion(f32[8,512,512]{1,2,0:T(8,128)} %get-tuple-element.249, f32[8,512]{1,0:T(8,128)} %get-tuple-element.250, f32[512,8,3,64]{0,3,1,2:T(8,128)S(1)} %bitcast.121), kind=kOutput, calls=%fused_computation.12.clone.1 | convolution fusion | flops 272891904 | bytes 9453568 | tf_op jit(solution)/shard_map/while/body/eval_jaxpr/hqk,khd->qhd/dot_general | solution.py:152
  222.8 1.3 copy.189
  224.1 0.8 constant_dynamic-update-slice_fusion.2
  224.9 6.1 %constant_dynamic-slice_fusion.6 = f32[1,512,8,3,64]{1,0,4,3,2:T(1,128)S(1)} fusion(f32[2,512,8,3,64]{1,0,4,3,2:T(2,128)} %get-tuple-element.263, s32[]{:T(128)} %get-tuple-element.256), kind=kLoop, calls=%fused_computation.34.clone.1 | loop fusion | bytes 6291460 | tf_op jit(solution)/shard_map/while/body/jit(dynamic_index_in_dim)/dynamic_slice | solution.py:156
  231.9 0.9 subtract_convert_fusion.5
  232.9 0.7 slice.267
  234.7 0.8 fusion.104
  235.6 8.2 %fusion.105 = (f32[8,512]{1,0:T(8,128)}, f32[8,512,512]{1,2,0:T(8,128)}) fusion(pred[512,512]{0,1:T(8,128)(4,1)} %fusion.104, bf16[512,8,32]{0,2,1:T(8,128)(2,1)S(1)} %slice.266, bf16[512,8,16]{0,2,1:T(8,128)(2,1)} %get-tuple-element.245, bf16[512,8,16]{0,2,1:T(8,128)(2,1)} %get-tuple-element.246, bf16[512,8,32]{0,2,1:T(8,128)(2,1)} %slice.267, ...), kind=kOutput, calls=%fused_computation.145.clone.1 | convolution fusion | flops 279970304 | bytes 9715712 | tf_op jit(solution)/shard_map/while/body/eval_jaxpr/sub | solution.py:150
  243.8 5.0 %fusion.106 = bf16[8,64,512]{2,1,0:T(8,128)(2,1)} fusion(f32[8,512,512]{1,2,0:T(8,128)} %get-tuple-element.249, f32[8,512]{1,0:T(8,128)} %get-tuple-element.250, f32[512,8,3,64]{0,3,1,2:T(8,128)S(1)} %bitcast.121), kind=kOutput, calls=%fused_computation.12.clone.1 | convolution fusion | flops 272891904 | bytes 9453568 | tf_op jit(solution)/shard_map/while/body/eval_jaxpr/hqk,khd->qhd/dot_general | solution.py:152
  248.8 1.3 copy.189
  250.1 0.8 constant_dynamic-update-slice_fusion.2
  250.9 0.8 reshape.562
  252.4 28.1 %fusion.35 = f32[1025,2048]{1,0:T(8,128)} fusion(bf16[2048,4096]{1,0:T(8,128)(2,1)} %all-gather.8.cloned.1.call-done, bf16[1025,2048]{0,1:T(8,128)(2,1)} %fusion.26), kind=kOutput, calls=%fused_computation.56 | convolution fusion | flops 17215539200 | bytes 29372416 | tf_op jit(solution)/shard_map/dot_general | solution.py:133
  280.5 8.5 %fusion.41 = bf16[1025,2048]{1,0:T(8,128)(2,1)} fusion(f32[1025,2048]{1,0:T(8,128)} %fusion.35, bf16[2048,2048]{1,0:T(8,128)(2,1)} %all-gather.4.cloned.1.call-done, bf16[1,512]{1,0:T(2,128)(2,1)S(1)} %convert_element_type.279, bf16[1024,512]{1,0:T(8,128)(2,1)S(1)} %bitcast.142), kind=kOutput, calls=%fused_computation.60 | convolution fusion | flops 2155878400 | bytes 15799296 | tf_op jit(solution)/shard_map/dot_general | solution.py:213
  289.0 6.4 %copy.148 = bf16[1025,2048]{0,1:T(8,128)(2,1)} copy(bf16[1025,2048]{1,0:T(8,128)(2,1)} %fusion.41) | data formatting | bytes 8396800 | tf_op jit(solution)/shard_map/convert_element_type | solution.py:217
  295.5 4.9 %copy.149 = bf16[1025,4,32,16]{0,3,2,1:T(8,128)(2,1)} copy(bf16[1025,4,32,16]{0,3,1,2:T(8,128)(2,1)} %bitcast.125) | data formatting | bytes 8396800 | tf_op jit(solution)/shard_map/convert_element_type | solution.py:217
  300.4 52.2 %reduce-scatter.2.cloned.1.call-done = bf16[1025,512]{0,1:T(8,128)(2,1)} async-done(((bf16[1025,2048]{0,1:T(8,128)(2,1)}), bf16[1025,512]{0,1:T(8,128)(2,1)}) %reduce-scatter.2.cloned.1.call-update) | async-done | bytes 1049616 | tf_op jit(solution)/shard_map/reduce_scatter | solution.py:216
  352.5 1.4 convert_element_type.287
  354.3 1.3 copy.152
  355.7 0.9 slice.180
  (130 shorter events, 14.7 us)
Async XLA Ops:
  7.2 15.7 %copy-start.8 = (f32[16,6144]{1,0:T(8,128)S(1)}, f32[16,6144]{1,0:T(8,128)}, u32[]{:S(2)}) copy-start(f32[16,6144]{1,0:T(8,128)} %param.19) | copy-start | bytes 1179652
  7.2 15.9 %copy-start.9 = (f32[16,2048]{1,0:T(8,128)S(1)}, f32[16,2048]{1,0:T(8,128)}, u32[]{:S(2)}) copy-start(f32[16,2048]{1,0:T(8,128)} %param.20) | copy-start | bytes 393220
  7.2 46.6 %all-gather.6.cloned.1.call-start = ((), (), s32[]{:S(2)}) async-start(), calls=%async_computation.6 | async-start | bytes 1572864 | tf_op jit(solution)/shard_map/all_gather | solution.py:69
  9.6 44.2 %copy-start.7 = (bf16[1024,512]{1,0:T(8,128)(2,1)S(1)}, bf16[1024,512]{1,0:T(8,128)(2,1)}, u32[]{:S(2)}) copy-start(bf16[1024,512]{1,0:T(8,128)(2,1)} %param.15) | copy-start | bytes 3145732
  10.4 43.9 %copy-start.10 = (bf16[1,512]{1,0:T(2,128)(2,1)S(1)}, bf16[1,512]{1,0:T(2,128)(2,1)}, u32[]{:S(2)}) copy-start(bf16[1,512]{1,0:T(2,128)(2,1)} %param.16) | copy-start | bytes 3076
  22.8 105.8 %all-gather.4.cloned.1.call-start = ((), (), s32[]{:S(2)}) async-start(), calls=%async_computation.5 | async-start | bytes 8912896 | tf_op jit(solution)/shard_map/all_gather | solution.py:70
  45.7 12.5 %copy-start.12 = (f32[2048]{0:T(1024)S(1)}, f32[2048]{0:T(1024)}, u32[]{:S(2)}) copy-start(f32[2048]{0:T(1024)} %param.18) | copy-start | bytes 24580
  45.7 206.7 %all-gather.8.cloned.1.call-start = ((), (), s32[]{:S(2)}) async-start(), calls=%async_computation.7 | async-start | bytes 17825792 | tf_op jit(solution)/shard_map/all_gather | solution.py:70
  53.7 4.7 %copy-start.13 = (f32[2048]{0:T(1024)S(1)}, f32[2048]{0:T(1024)}, u32[]{:S(2)}) copy-start(f32[2048]{0:T(1024)} %param.17) | copy-start | bytes 24580
  54.3 15.5 %copy-start.4 = (bf16[1024,512]{0,1:T(8,128)(2,1)}, bf16[1024,512]{0,1:T(8,128)(2,1)S(1)}, u32[]{:S(2)}) copy-start(bf16[1024,512]{0,1:T(8,128)(2,1)S(1)} %copy.124) | copy-start | bytes 3145732
  56.1 42.2 %collective-permute-start = (bf16[1025,512]{1,0:T(8,128)(2,1)}, bf16[1025,512]{1,0:T(8,128)(2,1)}, u32[]{:S(2)}, u32[]{:S(2)}) collective-permute-start(bf16[1025,512]{1,0:T(8,128)(2,1)} %copy.127), channel_id=1, source_target_pairs={{0,32},{32,64},{64,96},{96,0},{1,33},{33,65},{65,97},{97,1},{2,34}... | collective-permute-start | bytes 3148808 | tf_op jit(solution)/shard_map/ppermute | solution.py:100
  56.9 47.2 %collective-permute-start.1 = (bf16[1025,512]{1,0:T(8,128)(2,1)}, bf16[1025,512]{1,0:T(8,128)(2,1)}, u32[]{:S(2)}, u32[]{:S(2)}) collective-permute-start(bf16[1025,512]{1,0:T(8,128)(2,1)} %copy.127), channel_id=1, source_target_pairs={{0,64},{32,96},{64,0},{96,32},{1,65},{33,97},{65,1},{97,33},{2,66}... | collective-permute-start | bytes 3148808 | tf_op jit(solution)/shard_map/ppermute | solution.py:100
  57.9 48.6 %collective-permute-start.2 = (bf16[1025,512]{1,0:T(8,128)(2,1)}, bf16[1025,512]{1,0:T(8,128)(2,1)}, u32[]{:S(2)}, u32[]{:S(2)}) collective-permute-start(bf16[1025,512]{1,0:T(8,128)(2,1)} %copy.127), channel_id=1, source_target_pairs={{0,96},{32,0},{64,32},{96,64},{1,97},{33,1},{65,33},{97,65},{2,98}... | collective-permute-start | bytes 3148808 | tf_op jit(solution)/shard_map/ppermute | solution.py:100
  111.5 1.7 copy-start
  111.5 1.7 copy-start.1
  111.5 1.8 copy-start.2
  111.5 2.1 copy-start.3
  139.4 2.9 copy-start.6
  145.4 30.4 %all-to-all-start.1 = ((bf16[32,2,768]{2,1,0:T(2,128)(2,1)}), bf16[32,2,768]{2,1,0:T(2,128)(2,1)S(1)}, u32[]{:S(2)}, u32[]{:S(2)}) async-start(bf16[32,2,768]{2,1,0:T(2,128)(2,1)} %reshape.559), calls=%async_computation.1 | async-start | bytes 196608 | tf_op jit(solution)/shard_map/all_to_all | solution.py:173
  166.4 9.5 %copy-start.15 = (s32[32]{0:T(128)S(1)}, s32[32]{0:T(128)}, u32[]{:S(2)}) copy-start(s32[32]{0:T(128)} %param.27) | copy-start | bytes 388
  182.5 15.7 %copy-start.16 = (s32[2]{0:T(128)S(1)}, s32[2]{0:T(128)}, u32[]{:S(2)}) copy-start(s32[2]{0:T(128)} %param.25) | copy-start | bytes 28
  188.9 62.0 %all-to-all-start.2 = ((bf16[32,2,256]{2,1,0:T(2,128)(2,1)}), bf16[32,2,256]{2,1,0:T(2,128)(2,1)}, u32[]{:S(2)}, u32[]{:S(2)}) async-start(bf16[32,2,256]{2,1,0:T(2,128)(2,1)} %reshape.561), calls=%async_computation.2 | async-start | bytes 65536 | tf_op jit(solution)/shard_map/all_to_all | solution.py:206
  198.2 154.4 %reduce-scatter.2.cloned.1.call-start = ((), (), s32[]{:S(2)}) async-start(), calls=%async_computation.8 | async-start | bytes 5898240 | tf_op jit(solution)/shard_map/reduce_scatter | solution.py:216
  252.4 28.2 %copy-start.14 = (bf16[2,512,512]{2,1,0:T(8,128)(2,1)S(1)}, bf16[2,512,512]{2,1,0:T(8,128)(2,1)}, u32[]{:S(2)}) copy-start(bf16[2,512,512]{2,1,0:T(8,128)(2,1)} %get-tuple-element.97) | copy-start | bytes 3145732
  300.4 53.6 %copy-start.5 = (bf16[1024,512]{0,1:T(8,128)(2,1)S(1)}, bf16[1024,512]{0,1:T(8,128)(2,1)}, u32[]{:S(2)}) copy-start(bf16[1024,512]{0,1:T(8,128)(2,1)} %copy-done.4) | copy-start | bytes 3145732
  300.4 56.3 %copy-start.11 = (bf16[1,512]{1,0:T(2,128)(2,1)S(1)}, bf16[1,512]{1,0:T(2,128)(2,1)}, u32[]{:S(2)}) copy-start(bf16[1,512]{1,0:T(2,128)(2,1)} %param.16) | copy-start | bytes 3076
Sparse Core Ops, SparseCore 0:
  22.9 30.7 all-gather.5
  55.9 72.6 all-gather.3
  130.8 112.4 all-gather.7
  300.5 51.9 reduce-scatter.1

commit v4 on v3

--- a/solution.py
+++ b/solution.py
@@ -127,12 +127,6 @@
     scale = HD ** (-0.5)
     normed = layer_norm(joined, norm_gain, norm_bias)
     merged = jnp.dot(normed, w_project, preferred_element_type=jnp.float32)
-    hidden = jax.nn.gelu(
-        jnp.dot(normed, w_expand, preferred_element_type=jnp.float32), approximate=True
-    ).astype(half_float)
-    mlp_part = lax.dot_general(
-        hidden, w_reduce, (((1,), (1,)), ((), ())), preferred_element_type=jnp.float32
-    )
     places = jnp.arange(PLEN, dtype=jnp.int32)
 
     def prompt_block(items):
@@ -213,12 +207,28 @@
     attn_part = lax.dot_general(
         mixed_all, w_dense, (((1,), (1,)), ((), ())), preferred_element_type=jnp.float32
     )
-    summed = lax.psum_scatter(
-        from_gathered(attn_part + mlp_part).astype(half_float), "row", scatter_dimension=1, tiled=True
-    ).astype(jnp.float32)
-    prompt_result = prompt_tokens.astype(jnp.float32) + summed[:rows_prompt]
-    decode_result = decode_tokens.astype(jnp.float32) + summed[rows_prompt:]
-    return (prompt_result.astype(half_float), decode_result.astype(half_float))
+    residual = jnp.concatenate([prompt_tokens, decode_tokens], axis=0)
+    bounds = [0, rows_prompt // 2, normed.shape[0]]
+    outputs = []
+    for low, high in zip(bounds[:-1], bounds[1:]):
+        hidden = jax.nn.gelu(
+            jnp.dot(normed[low:high], w_expand, preferred_element_type=jnp.float32),
+            approximate=True,
+        ).astype(half_float)
+        mlp_part = lax.dot_general(
+            hidden, w_reduce, (((1,), (1,)), ((), ())), preferred_element_type=jnp.float32
+        )
+        summed = lax.psum_scatter(
+            from_gathered(attn_part[low:high] + mlp_part).astype(half_float),
+            "row",
+            scatter_dimension=1,
+            tiled=True,
+        )
+        outputs.append(
+            (residual[low:high].astype(jnp.float32) + summed.astype(jnp.float32)).astype(half_float)
+        )
+    result = jnp.concatenate(outputs, axis=0)
+    return (result[:rows_prompt], result[rows_prompt:])
 
 
 def solution(mesh):

time: 370 us -> 366 us (0.989)
  waiting for transfers between devices: 70.6 us -> 60.9 us
  matrix products: 85.2 us -> 91.3 us
    reduce_scatter x1 -> x2, waiting for transfers between devices: 52.2 us -> 42.7 us  [on_device(): lax.psum_scatter(from_gathered(attn_part[low:high] + mlp_part).astype(hal...]
    dot_general x1 -> x2, matrix products: 28.1 us -> 35.1 us  [on_device(): lax.dot_general(hidden, w_reduce, (((1,), (1,)), ((), ())), preferred_ele...]
    convert_element_type x2 -> x4, local copies, waits for them, and re-layouts: 11.3 us -> 10.6 us  [on_device(): from_gathered(attn_part[low:high] + mlp_part).astype(half_float)]
  transfers between devices with their start and end apart: 9 -> 10, of which waited for: 4 -> 5; matrix products, arithmetic and copies ran while one was open for 45% -> 55% of each run, Pallas kernels for 0% -> 0%
where the time goes in v4:
time: 366 us; the launch traced here: 360 us
  local copies, waits for them, and re-layouts  111 us (30%)
  matrix products  91.3 us (25%)
  waiting for transfers between devices  60.9 us (17%)
  blocking collectives  34.6 us (9%)
  other arithmetic  27.6 us (8%)
  starting transfers between devices  19 us (5%)
  between operations  15.3 us (4%)
    reduce_scatter x2, waiting for transfers between devices, on_device(): lax.psum_scatter(from_gathered(attn_part[low:high] + mlp_part).astype(hal...  42.7 us
    dot_general x2, matrix products, on_device(): lax.dot_general(hidden, w_reduce, (((1,), (1,)), ((), ())), preferred_ele...  35.1 us
    another operation x2, local copies, waits for them, and re-layouts  22.4 us
    all_to_all x2, blocking collectives, regroup(): lax.all_to_all(joined, 'row', split_axis=1, concat_axis=0, tiled=True)  20.8 us
    unnamed x44, local copies, waits for them, and re-layouts  20.4 us
    sub x2, matrix products, prompt_block(): raised = jnp.exp(scores - top)  16.4 us
    dynamic_slice x6, local copies, waits for them, and re-layouts, on_device(): lax.map(prompt_block, (prompt_blocks, prompt_lengths))  14.4 us
    all_gather x1, blocking collectives, regroup(): gathered = lax.all_gather(flat, COL[-1], axis=0, tiled=True)  13.8 us
  transfers between devices with their start and end apart: 10, of which 5 were waited for; matrix products, arithmetic and copies ran while one was open for 55% of the time, Pallas kernels for 0%

profile of v4, /device:TPU:1, one launch (start us, length us, event | category | flops | bytes accessed | tf_op | source)
XLA Modules:
  0.0 360.3 jit_solution(6728552336722932268)
XLA Ops:
  7.2 1.1 convert_element_type.298
  8.5 1.1 convert_element_type.299
  10.4 12.3 %all_to_all.48 = bf16[16,4,4096]{2,0,1:T(8,128)(2,1)} all-to-all(bf16[16,4,4096]{2,0,1:T(8,128)(2,1)S(1)} %copy.148), channel_id=1, replica_groups=mesh['row'=4,'col_y'=4,'col_z'=4,'col_x'=2] {'row'}, dimensions={1} | all-to-all | bytes 1048576 | tf_op jit(solution)/shard_map/all_to_all | solution.py:67
  23.4 8.4 %all_to_all.49 = bf16[16,4,2048]{2,0,1:T(8,128)(2,1)S(1)} all-to-all(bf16[16,4,2048]{2,0,1:T(8,128)(2,1)S(1)} %copy.137), channel_id=1, replica_groups=mesh['row'=4,'col_y'=4,'col_z'=4,'col_x'=2] {'row'}, dimensions={1} | all-to-all | bytes 524288 | tf_op jit(solution)/shard_map/all_to_all | solution.py:67
  31.8 13.8 %all_gather.12 = bf16[128,2048]{1,0:T(8,128)(2,1)} all-gather(bf16[64,2048]{1,0:T(8,128)(2,1)S(1)} %bitcast.136), channel_id=1, replica_groups=mesh['row'=4,'col_y'=4,'col_z'=4,'col_x'=2] {'col_x'}, dimensions={0}, use_global_device_ids=true | all-gather | bytes 786432 | tf_op jit(solution)/shard_map/all_gather | solution.py:69
  45.7 8.0 %all-gather.6.cloned.1.call-done = bf16[128,4096]{1,0:T(8,128)(2,1)} async-done(((bf16[64,4096]{1,0:T(8,128)(2,1)}), bf16[128,4096]{1,0:T(8,128)(2,1)}) %all-gather.6.cloned.1.call-update) | async-done | bytes 1048592 | tf_op jit(solution)/shard_map/all_gather | solution.py:69
  54.7 1.4 copy.128
  56.1 0.8 collective-permute-start
  57.0 1.0 collective-permute-start.1
  58.7 1.3 dynamic_slice.37
  60.0 1.3 dynamic_slice.38
  61.3 2.0 fusion.111
  64.0 6.2 %reshape.561 = bf16[2097152]{0:T(1024)(128)(2,1)} reshape(bf16[1,8,262144]{2,1,0:T(8,128)(2,1)} %param.23) | data formatting | bytes 8388608
  70.1 11.2 %reshape.540 = bf16[8,4096,64]{2,1,0:T(8,128)(2,1)} reshape(bf16[2097152]{0:T(1024)(128)(2,1)} %reshape.561) | data formatting | bytes 8388608 | tf_op jit(solution)/shard_map/reshape.17
  81.3 6.0 %reshape.559 = bf16[2097152]{0:T(1024)(128)(2,1)} reshape(bf16[1,8,262144]{2,1,0:T(8,128)(2,1)} %param.24) | data formatting | bytes 8388608
  87.3 11.3 %reshape.541 = bf16[8,4096,64]{2,1,0:T(8,128)(2,1)} reshape(bf16[2097152]{0:T(1024)(128)(2,1)} %reshape.559) | data formatting | bytes 8388608 | tf_op jit(solution)/shard_map/reshape.23
  98.6 1.7 copy.129
  100.3 3.9 %collective-permute-done.1 = bf16[1025,512]{1,0:T(8,128)(2,1)} collective-permute-done((bf16[1025,512]{1,0:T(8,128)(2,1)}, bf16[1025,512]{1,0:T(8,128)(2,1)}, u32[]{:S(2)}, u32[]{:S(2)}) %collective-permute-start.1) | collective-permute-done | bytes 1049632 | tf_op jit(solution)/shard_map/ppermute | solution.py:100
  104.2 2.4 copy.131
  106.6 2.4 copy.133
  109.0 2.1 pad_maximum_fusion.12
  111.5 1.7 maximum_convert_fusion
  113.6 1.2 copy.134
  114.9 2.9 fusion.128
  117.8 1.0 multiply_reduce_fusion
  118.8 3.7 %fusion.26 = bf16[1025,2048]{0,1:T(8,128)(2,1)} fusion(f32[1025,32,4,16]{0,3,2,1:T(8,128)S(1)} %copy.134, f32[2048]{0:T(1024)S(1)} %add.145, f32[2048]{0:T(1024)S(1)} %mul.392, f32[1025]{0:T(1024)S(1)} %add_rsqrt_fusion, f32[1025]{0:T(1024)S(1)} %broadcast_multiply_fusion), kind=kLoop, calls=%fused_computation.44 | loop fusion | flops 10496000 | bytes 12619784 | tf_op jit(solution)/shard_map/convert_element_type | solution.py:21
  122.5 6.1 %all-gather.4.cloned.1.call-done = bf16[2048,2048]{1,0:T(8,128)(2,1)} async-done(((bf16[128,2048]{1,0:T(8,128)(2,1)}), bf16[2048,2048]{1,0:T(8,128)(2,1)}) %all-gather.4.cloned.1.call-update) | async-done | bytes 8388624 | tf_op jit(solution)/shard_map/all_gather | solution.py:70
  128.6 10.8 %fusion.35 = f32[1025,1536]{1,0:T(8,128)S(1)} fusion(bf16[1025,2048]{0,1:T(8,128)(2,1)} %fusion.26, bf16[2048,2048]{1,0:T(8,128)(2,1)} %all-gather.4.cloned.1.call-done), kind=kOutput, calls=%fused_computation.55 | convolution fusion | flops 6448742400 | bytes 17307648 | tf_op jit(solution)/shard_map/dot_general | solution.py:129
  139.5 2.8 copy-done.6
  143.6 1.2 reduce.17
  145.5 7.6 %all-to-all-start.1 = ((bf16[32,2,768]{2,1,0:T(2,128)(2,1)}), bf16[32,2,768]{2,1,0:T(2,128)(2,1)S(1)}, u32[]{:S(2)}, u32[]{:S(2)}) async-start(bf16[32,2,768]{2,1,0:T(2,128)(2,1)} %reshape.563), calls=%async_computation.1 | async-start | bytes 196608 | tf_op jit(solution)/shard_map/all_to_all | solution.py:167
  153.8 6.0 %slice.193 = f32[1024,1536]{1,0:T(8,128)} slice(f32[1025,1536]{1,0:T(8,128)} %copy-done.6), slice={[0:1024], [0:1536]} | slice | bytes 12582912 | tf_op jit(solution)/shard_map/slice | solution.py:149
  159.8 6.7 %copy.138 = f32[1024,1536]{0,1:T(8,128)} copy(f32[1024,1536]{1,0:T(8,128)} %slice.193) | data formatting | bytes 12582912 | tf_op jit(solution)/shard_map/slice | solution.py:149
  166.5 9.4 %reshape.535 = f32[2,512,8,3,64]{1,0,4,3,2:T(2,128)} reshape(f32[1024,1536]{0,1:T(8,128)} %copy.138) | data formatting | bytes 12582912 | tf_op jit(solution)/shard_map/reshape | solution.py:149
  176.3 5.6 %fusion.99 = f32[8,1,4096]{2,1,0:T(1,128)S(1)} fusion(bf16[8,4096,64]{2,1,0:T(8,128)(2,1)} %reshape.540, bf16[1,8,3,64]{3,2,1,0:T(4,128)(2,1)S(1)} %reshape.538), kind=kOutput, calls=%fused_computation.127 | convolution fusion | flops 4194304 | bytes 4329472 | tf_op jit(solution)/shard_map/shd,shtd->sht/dot_general | solution.py:181
  182.6 4.7 %fusion.88 = f32[8,1,64]{2,1,0:T(1,128)S(1)} fusion(bf16[8,4096,64]{2,1,0:T(8,128)(2,1)} %reshape.541, bf16[8,4096,1]{1,0,2:T(8,128)(2,1)S(1)} %fusion.94), kind=kOutput, calls=%fused_computation.107 | convolution fusion | flops 4194304 | bytes 4261888 | tf_op jit(solution)/shard_map/sht,shtd->shd/dot_general | solution.py:196
  189.0 9.2 %all-to-all-start.2 = ((bf16[32,2,256]{2,1,0:T(2,128)(2,1)}), bf16[32,2,256]{2,1,0:T(2,128)(2,1)}, u32[]{:S(2)}, u32[]{:S(2)}) async-start(bf16[32,2,256]{2,1,0:T(2,128)(2,1)} %reshape.565), calls=%async_computation.2 | async-start | bytes 65536 | tf_op jit(solution)/shard_map/all_to_all | solution.py:200
  198.3 52.8 %while.14 = (s32[]{:T(128)}, bf16[2,512,512]{2,1,0:T(8,128)(2,1)}, f32[2,512,8,3,64]{1,0,4,3,2:T(2,128)}, s32[2]{0:T(128)S(1)}, s32[]{:T(128)}) while((s32[]{:T(128)}, bf16[2,512,512]{2,1,0:T(8,128)(2,1)}, f32[2,512,8,3,64]{1,0,4,3,2:T(2,128)}, s32[2]{0:T(128)S(1)}, s32[]{:T(128)}) %tuple.86), condition=%wide.region_5.6_spmd.clone.clone, body=%wide.region_2.5_spmd.clone.clone.sunk | while | flops 554444288 | bytes 41064144 | solution.py:150
  198.7 6.3 %constant_dynamic-slice_fusion.6 = f32[1,512,8,3,64]{1,0,4,3,2:T(1,128)S(1)} fusion(f32[2,512,8,3,64]{1,0,4,3,2:T(2,128)} %get-tuple-element.263, s32[]{:T(128)} %get-tuple-element.256), kind=kLoop, calls=%fused_computation.34.clone.1 | loop fusion | bytes 6291460 | tf_op jit(solution)/shard_map/while/body/jit(dynamic_index_in_dim)/dynamic_slice | solution.py:150
  206.0 0.9 subtract_convert_fusion.5
  208.8 0.8 fusion.139
  209.6 8.2 %fusion.140 = (f32[8,512]{1,0:T(8,128)}, f32[8,512,512]{1,2,0:T(8,128)}) fusion(pred[512,512]{0,1:T(8,128)(4,1)} %fusion.139, bf16[512,8,32]{0,2,1:T(8,128)(2,1)S(1)} %slice.328, bf16[512,8,16]{0,2,1:T(8,128)(2,1)} %get-tuple-element.245, bf16[512,8,16]{0,2,1:T(8,128)(2,1)} %get-tuple-element.246, bf16[512,8,32]{0,2,1:T(8,128)(2,1)} %slice.329, ...), kind=kOutput, calls=%fused_computation.174.clone.1 | convolution fusion | flops 279970304 | bytes 9715712 | tf_op jit(solution)/shard_map/while/body/eval_jaxpr/sub | solution.py:144
  217.8 5.0 %fusion.141 = bf16[8,64,512]{2,1,0:T(8,128)(2,1)} fusion(f32[8,512,512]{1,2,0:T(8,128)} %get-tuple-element.249, f32[8,512]{1,0:T(8,128)} %get-tuple-element.250, f32[512,8,3,64]{0,3,1,2:T(8,128)S(1)} %bitcast.124), kind=kOutput, calls=%fused_computation.12.clone.1 | convolution fusion | flops 272891904 | bytes 9453568 | tf_op jit(solution)/shard_map/while/body/eval_jaxpr/hqk,khd->qhd/dot_general | solution.py:146
  222.9 1.3 copy.190
  224.2 0.8 constant_dynamic-update-slice_fusion.2
  225.0 6.1 %constant_dynamic-slice_fusion.6 = f32[1,512,8,3,64]{1,0,4,3,2:T(1,128)S(1)} fusion(f32[2,512,8,3,64]{1,0,4,3,2:T(2,128)} %get-tuple-element.263, s32[]{:T(128)} %get-tuple-element.256), kind=kLoop, calls=%fused_computation.34.clone.1 | loop fusion | bytes 6291460 | tf_op jit(solution)/shard_map/while/body/jit(dynamic_index_in_dim)/dynamic_slice | solution.py:150
  232.0 0.9 subtract_convert_fusion.5
  234.8 0.8 fusion.139
  235.6 8.2 %fusion.140 = (f32[8,512]{1,0:T(8,128)}, f32[8,512,512]{1,2,0:T(8,128)}) fusion(pred[512,512]{0,1:T(8,128)(4,1)} %fusion.139, bf16[512,8,32]{0,2,1:T(8,128)(2,1)S(1)} %slice.328, bf16[512,8,16]{0,2,1:T(8,128)(2,1)} %get-tuple-element.245, bf16[512,8,16]{0,2,1:T(8,128)(2,1)} %get-tuple-element.246, bf16[512,8,32]{0,2,1:T(8,128)(2,1)} %slice.329, ...), kind=kOutput, calls=%fused_computation.174.clone.1 | convolution fusion | flops 279970304 | bytes 9715712 | tf_op jit(solution)/shard_map/while/body/eval_jaxpr/sub | solution.py:144
  243.8 5.0 %fusion.141 = bf16[8,64,512]{2,1,0:T(8,128)(2,1)} fusion(f32[8,512,512]{1,2,0:T(8,128)} %get-tuple-element.249, f32[8,512]{1,0:T(8,128)} %get-tuple-element.250, f32[512,8,3,64]{0,3,1,2:T(8,128)S(1)} %bitcast.124), kind=kOutput, calls=%fused_computation.12.clone.1 | convolution fusion | flops 272891904 | bytes 9453568 | tf_op jit(solution)/shard_map/while/body/eval_jaxpr/hqk,khd->qhd/dot_general | solution.py:146
  248.9 1.3 copy.190
  250.1 0.8 constant_dynamic-update-slice_fusion.2
  252.7 7.5 %fusion.77 = f32[1025,2048]{1,0:T(8,128)} fusion(bf16[2048,2048]{1,0:T(8,128)(2,1)} %all-gather.4.cloned.1.call-done, bf16[1,512]{1,0:T(2,128)(2,1)S(1)} %convert_element_type.297, bf16[1024,512]{1,0:T(8,128)(2,1)} %bitcast.147), kind=kOutput, calls=%fused_computation.86 | convolution fusion | flops 2151680000 | bytes 11543552 | tf_op jit(solution)/shard_map/dot_general | solution.py:207
  260.3 18.7 %fusion.54 = bf16[512,2048]{1,0:T(8,128)(2,1)} fusion(f32[1025,2048]{1,0:T(8,128)} %fusion.77, bf16[2048,4096]{1,0:T(8,128)(2,1)} %all-gather.8.cloned.1.call-done, bf16[1025,2048]{0,1:T(8,128)(2,1)} %fusion.26), kind=kOutput, calls=%fused_computation.79 | convolution fusion | flops 8601468928 | bytes 25165824 | tf_op jit(solution)/shard_map/dot_general | solution.py:218
  279.0 2.9 copy.149
  281.8 1.6 copy.150
  283.5 16.4 %fusion.45 = bf16[513,2048]{1,0:T(8,128)(2,1)S(1)} fusion(f32[1025,2048]{1,0:T(8,128)} %fusion.77, bf16[2048,4096]{1,0:T(8,128)(2,1)} %all-gather.8.cloned.1.call-done, bf16[1025,2048]{0,1:T(8,128)(2,1)} %fusion.26), kind=kOutput, calls=%fused_computation.69 | convolution fusion | flops 8618268672 | bytes 25759744 | tf_op jit(solution)/shard_map/dot_general | solution.py:218
  299.9 2.6 copy.151
  302.5 3.6 %copy.152 = bf16[513,4,32,16]{0,3,2,1:T(8,128)(2,1)} copy(bf16[513,4,32,16]{0,3,1,2:T(8,128)(2,1)} %bitcast.129) | data formatting | bytes 4202496 | tf_op jit(solution)/shard_map/convert_element_type | solution.py:222
  306.1 8.1 %reduce-scatter.3.cloned.1.call-done = bf16[512,512]{0,1:T(8,128)(2,1)} async-done(((bf16[512,2048]{0,1:T(8,128)(2,1)}), bf16[512,512]{0,1:T(8,128)(2,1)}) %reduce-scatter.3.cloned.1.call-update) | async-done | bytes 524304 | tf_op jit(solution)/shard_map/reduce_scatter | solution.py:221
  314.2 1.2 add_convert_fusion.3
  315.4 34.6 %reduce-scatter.5.cloned.1.call-done = bf16[513,512]{0,1:T(8,128)(2,1)} async-done(((bf16[513,2048]{0,1:T(8,128)(2,1)}), bf16[513,512]{0,1:T(8,128)(2,1)}) %reduce-scatter.5.cloned.1.call-update) | async-done | bytes 525328 | tf_op jit(solution)/shard_map/reduce_scatter | solution.py:221
  350.1 1.3 add_convert_fusion.2
  351.5 1.3 copy.153
  (134 shorter events, 17.5 us)
Async XLA Ops:
  7.2 15.7 %copy-start.10 = (f32[16,6144]{1,0:T(8,128)S(1)}, f32[16,6144]{1,0:T(8,128)}, u32[]{:S(2)}) copy-start(f32[16,6144]{1,0:T(8,128)} %param.19) | copy-start | bytes 1179652
  7.2 15.9 %copy-start.11 = (f32[16,2048]{1,0:T(8,128)S(1)}, f32[16,2048]{1,0:T(8,128)}, u32[]{:S(2)}) copy-start(f32[16,2048]{1,0:T(8,128)} %param.20) | copy-start | bytes 393220
  7.2 46.6 %all-gather.6.cloned.1.call-start = ((), (), s32[]{:S(2)}) async-start(), calls=%async_computation.7 | async-start | bytes 1572864 | tf_op jit(solution)/shard_map/all_gather | solution.py:69
  9.8 44.0 %copy-start.9 = (bf16[1024,512]{1,0:T(8,128)(2,1)S(1)}, bf16[1024,512]{1,0:T(8,128)(2,1)}, u32[]{:S(2)}) copy-start(bf16[1024,512]{1,0:T(8,128)(2,1)} %param.15) | copy-start | bytes 3145732
  10.4 43.9 %copy-start.14 = (bf16[1,512]{1,0:T(2,128)(2,1)S(1)}, bf16[1,512]{1,0:T(2,128)(2,1)}, u32[]{:S(2)}) copy-start(bf16[1,512]{1,0:T(2,128)(2,1)} %param.16) | copy-start | bytes 3076
  22.8 105.8 %all-gather.4.cloned.1.call-start = ((), (), s32[]{:S(2)}) async-start(), calls=%async_computation.6 | async-start | bytes 8912896 | tf_op jit(solution)/shard_map/all_gather | solution.py:70
  45.7 214.6 %all-gather.8.cloned.1.call-start = ((), (), s32[]{:S(2)}) async-start(), calls=%async_computation.8 | async-start | bytes 17825792 | tf_op jit(solution)/shard_map/all_gather | solution.py:70
  53.8 4.4 %copy-start.12 = (f32[2048]{0:T(1024)S(1)}, f32[2048]{0:T(1024)}, u32[]{:S(2)}) copy-start(f32[2048]{0:T(1024)} %param.18) | copy-start | bytes 24580
  53.8 4.7 %copy-start.13 = (f32[2048]{0:T(1024)S(1)}, f32[2048]{0:T(1024)}, u32[]{:S(2)}) copy-start(f32[2048]{0:T(1024)} %param.17) | copy-start | bytes 24580
  54.4 15.8 %copy-start = (bf16[1024,512]{0,1:T(8,128)(2,1)}, bf16[1024,512]{0,1:T(8,128)(2,1)S(1)}, u32[]{:S(2)}) copy-start(bf16[1024,512]{0,1:T(8,128)(2,1)S(1)} %copy.125) | copy-start | bytes 3145732
  54.6 15.6 %copy-start.7 = (bf16[1,512]{0,1:T(8,128)(2,1)}, bf16[1,512]{0,1:T(8,128)(2,1)S(1)}, u32[]{:S(2)}) copy-start(bf16[1,512]{0,1:T(8,128)(2,1)S(1)} %copy.127) | copy-start | bytes 3076
  56.1 42.5 %collective-permute-start = (bf16[1025,512]{1,0:T(8,128)(2,1)}, bf16[1025,512]{1,0:T(8,128)(2,1)}, u32[]{:S(2)}, u32[]{:S(2)}) collective-permute-start(bf16[1025,512]{1,0:T(8,128)(2,1)} %copy.128), channel_id=1, source_target_pairs={{0,32},{32,64},{64,96},{96,0},{1,33},{33,65},{65,97},{97,1},{2,34}... | collective-permute-start | bytes 3148808 | tf_op jit(solution)/shard_map/ppermute | solution.py:100
  57.0 47.2 %collective-permute-start.1 = (bf16[1025,512]{1,0:T(8,128)(2,1)}, bf16[1025,512]{1,0:T(8,128)(2,1)}, u32[]{:S(2)}, u32[]{:S(2)}) collective-permute-start(bf16[1025,512]{1,0:T(8,128)(2,1)} %copy.128), channel_id=1, source_target_pairs={{0,64},{32,96},{64,0},{96,32},{1,65},{33,97},{65,1},{97,33},{2,66}... | collective-permute-start | bytes 3148808 | tf_op jit(solution)/shard_map/ppermute | solution.py:100
  57.9 48.7 %collective-permute-start.2 = (bf16[1025,512]{1,0:T(8,128)(2,1)}, bf16[1025,512]{1,0:T(8,128)(2,1)}, u32[]{:S(2)}, u32[]{:S(2)}) collective-permute-start(bf16[1025,512]{1,0:T(8,128)(2,1)} %copy.128), channel_id=1, source_target_pairs={{0,96},{32,0},{64,32},{96,64},{1,97},{33,1},{65,33},{97,65},{2,98}... | collective-permute-start | bytes 3148808 | tf_op jit(solution)/shard_map/ppermute | solution.py:100
  111.5 1.7 copy-start.2
  111.5 1.7 copy-start.3
  111.5 1.8 copy-start.4
  111.5 2.1 copy-start.5
  139.5 2.9 copy-start.6
  145.5 30.4 %all-to-all-start.1 = ((bf16[32,2,768]{2,1,0:T(2,128)(2,1)}), bf16[32,2,768]{2,1,0:T(2,128)(2,1)S(1)}, u32[]{:S(2)}, u32[]{:S(2)}) async-start(bf16[32,2,768]{2,1,0:T(2,128)(2,1)} %reshape.563), calls=%async_computation.1 | async-start | bytes 196608 | tf_op jit(solution)/shard_map/all_to_all | solution.py:167
  166.5 9.5 %copy-start.15 = (s32[32]{0:T(128)S(1)}, s32[32]{0:T(128)}, u32[]{:S(2)}) copy-start(s32[32]{0:T(128)} %param.27) | copy-start | bytes 388
  182.6 15.7 %copy-start.16 = (s32[2]{0:T(128)S(1)}, s32[2]{0:T(128)}, u32[]{:S(2)}) copy-start(s32[2]{0:T(128)} %param.25) | copy-start | bytes 28
  189.0 62.1 %all-to-all-start.2 = ((bf16[32,2,256]{2,1,0:T(2,128)(2,1)}), bf16[32,2,256]{2,1,0:T(2,128)(2,1)}, u32[]{:S(2)}, u32[]{:S(2)}) async-start(bf16[32,2,256]{2,1,0:T(2,128)(2,1)} %reshape.565), calls=%async_computation.2 | async-start | bytes 65536 | tf_op jit(solution)/shard_map/all_to_all | solution.py:200
  198.2 116.0 %reduce-scatter.3.cloned.1.call-start = ((), (), s32[]{:S(2)}) async-start(), calls=%async_computation.9 | async-start | bytes 2621440 | tf_op jit(solution)/shard_map/reduce_scatter | solution.py:221
  283.4 66.6 %reduce-scatter.5.cloned.1.call-start = ((), (), s32[]{:S(2)}) async-start(), calls=%async_computation.10 | async-start | bytes 3276800 | tf_op jit(solution)/shard_map/reduce_scatter | solution.py:221
  302.5 11.8 %copy-start.1 = (bf16[1024,512]{0,1:T(8,128)(2,1)S(1)}, bf16[1024,512]{0,1:T(8,128)(2,1)}, u32[]{:S(2)}) copy-start(bf16[1024,512]{0,1:T(8,128)(2,1)} %copy-done) | copy-start | bytes 3145732
  302.5 47.6 %copy-start.8 = (bf16[1,512]{0,1:T(8,128)(2,1)S(1)}, bf16[1,512]{0,1:T(8,128)(2,1)}, u32[]{:S(2)}) copy-start(bf16[1,512]{0,1:T(8,128)(2,1)} %copy-done.7) | copy-start | bytes 3076
Sparse Core Ops, SparseCore 0:
  22.9 30.7 all-gather.5
  55.9 72.6 all-gather.3
  130.8 112.4 all-gather.7
  283.6 30.6 reduce-scatter.2
  316.6 33.4 reduce-scatter.4

commit v5 on v4

--- a/solution.py
+++ b/solution.py
@@ -1,6 +1,10 @@
+import functools
+
 import jax
 import jax.numpy as jnp
 from jax import lax
+from jax.experimental import pallas as pl
+from jax.experimental.pallas import tpu as pltpu
 from jax.sharding import PartitionSpec as P
 
 HD = 64
@@ -37,6 +41,41 @@
         ],
         axis=-1,
     )
+
+
+def attention_kernel(lengths_ref, query_ref, key_ref, value_ref, out_ref, *, heads):
+    length = lengths_ref[pl.program_id(0)]
+    rows = lax.broadcasted_iota(jnp.int32, (PLEN, PLEN), 0)
+    cols = lax.broadcasted_iota(jnp.int32, (PLEN, PLEN), 1)
+    allowed = (cols <= rows) & (cols < length)
+    for head in range(heads):
+        lanes = slice(head * HD, (head + 1) * HD)
+        scores = lax.dot_general(
+            query_ref[:, lanes], key_ref[:, lanes], (((1,), (1,)), ((), ())),
+            preferred_element_type=jnp.float32,
+        ) * (HD ** -0.5)
+        scores = jnp.where(allowed, scores, NEG)
+        top = jnp.max(scores, axis=-1, keepdims=True)
+        raised = jnp.exp(scores - top)
+        probs = (raised / jnp.sum(raised, axis=-1, keepdims=True)).astype(jnp.bfloat16)
+        mixed = jnp.dot(probs, value_ref[:, lanes], preferred_element_type=jnp.float32)
+        out_ref[:, lanes] = mixed.astype(jnp.bfloat16)
+
+
+def prompt_attention(lengths, queries, keys, values, heads, interpret=False):
+    rows, width = queries.shape
+    block = pl.BlockSpec((PLEN, width), lambda p, lengths_ref: (p, 0))
+    return pl.pallas_call(
+        functools.partial(attention_kernel, heads=heads),
+        out_shape=jax.ShapeDtypeStruct((rows, width), jnp.bfloat16),
+        grid_spec=pltpu.PrefetchScalarGridSpec(
+            num_scalar_prefetch=1,
+            grid=(rows // PLEN,),
+            in_specs=[block, block, block],
+            out_specs=block,
+        ),
+        interpret=interpret,
+    )(lengths, queries, keys, values)
 
 
 def on_device(
@@ -127,28 +166,14 @@
     scale = HD ** (-0.5)
     normed = layer_norm(joined, norm_gain, norm_bias)
     merged = jnp.dot(normed, w_project, preferred_element_type=jnp.float32)
-    places = jnp.arange(PLEN, dtype=jnp.int32)
-
-    def prompt_block(items):
-        block, length = items
-        queries = rotary(block[:, :, 0], places).astype(half_float)
-        keys_rot = rotary(block[:, :, 1], places).astype(half_float)
-        values = block[:, :, 2].astype(half_float)
-        scores = (
-            jnp.einsum("qhd,khd->hqk", queries, keys_rot, preferred_element_type=jnp.float32)
-            * scale
-        )
-        allowed = (places[None, :] <= places[:, None]) & (places[None, :] < length)
-        scores = jnp.where(allowed[None], scores, NEG)
-        top = jnp.max(scores, axis=-1, keepdims=True)
-        raised = jnp.exp(scores - top)
-        probs = (raised / jnp.sum(raised, axis=-1, keepdims=True)).astype(half_float)
-        mixed = jnp.einsum("hqk,khd->qhd", probs, values, preferred_element_type=jnp.float32)
-        return mixed.astype(half_float).reshape(PLEN, heads_local * HD)
-
-    prompt_blocks = merged[:rows_prompt].reshape(prompt_count, PLEN, heads_local, 3, HD)
-    prompt_mixed = lax.map(prompt_block, (prompt_blocks, prompt_lengths)).reshape(
-        rows_prompt, heads_local * HD
+    prompt_pieces = merged[:rows_prompt].reshape(rows_prompt, heads_local, 3, HD)
+    places = jnp.arange(rows_prompt, dtype=jnp.int32) % PLEN
+    width = heads_local * HD
+    prompt_queries = rotary(prompt_pieces[:, :, 0], places).astype(half_float).reshape(rows_prompt, width)
+    prompt_keys = rotary(prompt_pieces[:, :, 1], places).astype(half_float).reshape(rows_prompt, width)
+    prompt_values = prompt_pieces[:, :, 2].astype(half_float).reshape(rows_prompt, width)
+    prompt_mixed = prompt_attention(
+        prompt_lengths, prompt_queries, prompt_keys, prompt_values, heads_local
     )
     col_index = lax.axis_index(COL)
     first_slot = col_index * slot_local

time: 366 us -> 345 us (0.943)
  matrix products: 91.3 us -> 65.1 us
  local copies, waits for them, and re-layouts: 111 us -> 88 us
  waiting for transfers between devices: 60.9 us -> 81.7 us
  Pallas kernels: 0 us -> 14 us
  starting transfers between devices: 19 us -> 15.2 us
    all_gather x2, waiting for transfers between devices: 6.14 us -> 26.4 us  [regroup(): gathered = lax.all_gather(gathered, COL[:-1], axis=0, tiled=True)]
    sub x2 -> x0, matrix products: 16.4 us -> none  [prompt_block(): raised = jnp.exp(scores - top)]
    dynamic_slice x6 -> x0, local copies, waits for them, and re-layouts: 14.4 us -> none  [on_device(): lax.map(prompt_block, (prompt_blocks, prompt_lengths))]
    pallas_call x0 -> x1, Pallas kernels: none -> 14 us  [prompt_attention(): pl.pallas_call(functools.partial(attention_kernel, heads=heads), out_shap...]
    dot_general x2 -> x0, matrix products: 10.1 us -> none  [prompt_block(): jnp.einsum('hqk,khd->qhd', probs, values, preferred_element_type=jnp.floa...]
    reshape x1 -> x0, local copies, waits for them, and re-layouts: 9.39 us -> none  [on_device(): merged[:rows_prompt].reshape(prompt_count, PLEN, heads_local, 3, HD)]
    all_to_all x1, waiting for transfers between devices: 0.01 us -> 5.01 us  [on_device(): lax.all_to_all(jnp.broadcast_to(packed, (col_count,) + packed.shape[1:]),...]
    dynamic_update_slice x4 -> x0, local copies, waits for them, and re-layouts: 4.19 us -> none  [on_device(): lax.map(prompt_block, (prompt_blocks, prompt_lengths))]
  transfers between devices with their start and end apart: 10 -> 10, of which waited for: 5 -> 7; matrix products, arithmetic and copies ran while one was open for 55% -> 43% of each run, Pallas kernels for 0% -> 4%
where the time goes in v5:
time: 345 us; the launch traced here: 340 us
  local copies, waits for them, and re-layouts  88 us (26%)
  waiting for transfers between devices  81.7 us (24%)
  matrix products  65.1 us (19%)
  blocking collectives  34.6 us (10%)
  other arithmetic  25.8 us (7%)
  between operations  15.3 us (4%)
  starting transfers between devices  15.2 us (4%)
  Pallas kernels  14 us (4%)
    reduce_scatter x2, waiting for transfers between devices, on_device(): lax.psum_scatter(from_gathered(attn_part[low:high] + mlp_part).astype(hal...  40.1 us
    dot_general x2, matrix products, on_device(): lax.dot_general(hidden, w_reduce, (((1,), (1,)), ((), ())), preferred_ele...  35.1 us
    all_gather x2, waiting for transfers between devices, regroup(): gathered = lax.all_gather(gathered, COL[:-1], axis=0, tiled=True)  26.4 us
    another operation x2, local copies, waits for them, and re-layouts  22.3 us
    all_to_all x2, blocking collectives, regroup(): lax.all_to_all(joined, 'row', split_axis=1, concat_axis=0, tiled=True)  20.7 us
    unnamed x46, local copies, waits for them, and re-layouts  20.4 us
    pallas_call x1, Pallas kernels, prompt_attention(): pl.pallas_call(functools.partial(attention_kernel, heads=heads), out_shap...  14 us
    all_gather x1, blocking collectives, regroup(): gathered = lax.all_gather(flat, COL[-1], axis=0, tiled=True)  13.8 us
  transfers between devices with their start and end apart: 10, of which 7 were waited for; matrix products, arithmetic and copies ran while one was open for 43% of the time, Pallas kernels for 4%

profile of v5, /device:TPU:1, one launch (start us, length us, event | category | flops | bytes accessed | tf_op | source)
XLA Modules:
  0.0 339.7 jit_solution(18441564281328211103)
XLA Ops:
  7.2 1.1 convert_element_type.277
  8.5 1.1 convert_element_type.278
  10.4 12.3 %all_to_all.48 = bf16[16,4,4096]{2,0,1:T(8,128)(2,1)} all-to-all(bf16[16,4,4096]{2,0,1:T(8,128)(2,1)S(1)} %copy.154), channel_id=1, replica_groups=mesh['row'=4,'col_y'=4,'col_z'=4,'col_x'=2] {'row'}, dimensions={1} | all-to-all | bytes 1048576 | tf_op jit(solution)/shard_map/all_to_all | solution.py:106
  23.4 8.4 %all_to_all.49 = bf16[16,4,2048]{2,0,1:T(8,128)(2,1)S(1)} all-to-all(bf16[16,4,2048]{2,0,1:T(8,128)(2,1)S(1)} %copy.141), channel_id=1, replica_groups=mesh['row'=4,'col_y'=4,'col_z'=4,'col_x'=2] {'row'}, dimensions={1} | all-to-all | bytes 524288 | tf_op jit(solution)/shard_map/all_to_all | solution.py:106
  31.8 13.8 %all_gather.12 = bf16[128,2048]{1,0:T(8,128)(2,1)} all-gather(bf16[64,2048]{1,0:T(8,128)(2,1)S(1)} %bitcast.118), channel_id=1, replica_groups=mesh['row'=4,'col_y'=4,'col_z'=4,'col_x'=2] {'col_x'}, dimensions={0}, use_global_device_ids=true | all-gather | bytes 786432 | tf_op jit(solution)/shard_map/all_gather | solution.py:108
  45.7 8.0 %all-gather.6.cloned.1.call-done = bf16[128,4096]{1,0:T(8,128)(2,1)} async-done(((bf16[64,4096]{1,0:T(8,128)(2,1)}), bf16[128,4096]{1,0:T(8,128)(2,1)}) %all-gather.6.cloned.1.call-update) | async-done | bytes 1048592 | tf_op jit(solution)/shard_map/all_gather | solution.py:108
  54.7 1.4 copy.132
  56.1 0.8 collective-permute-start
  56.9 1.0 collective-permute-start.1
  58.4 0.8 reshape.470
  59.2 0.7 mul.332
  59.9 1.2 dynamic_slice.23
  61.8 1.3 fusion.92
  63.7 6.2 %reshape.500 = bf16[2097152]{0:T(1024)(128)(2,1)} reshape(bf16[1,8,262144]{2,1,0:T(8,128)(2,1)} %param.21) | data formatting | bytes 8388608
  69.9 11.1 %reshape.479 = bf16[8,4096,64]{2,1,0:T(8,128)(2,1)} reshape(bf16[2097152]{0:T(1024)(128)(2,1)} %reshape.500) | data formatting | bytes 8388608 | tf_op jit(solution)/shard_map/reshape.15
  81.0 6.0 %reshape.498 = bf16[2097152]{0:T(1024)(128)(2,1)} reshape(bf16[1,8,262144]{2,1,0:T(8,128)(2,1)} %param.22) | data formatting | bytes 8388608
  87.0 11.3 %reshape.480 = bf16[8,4096,64]{2,1,0:T(8,128)(2,1)} reshape(bf16[2097152]{0:T(1024)(128)(2,1)} %reshape.498) | data formatting | bytes 8388608 | tf_op jit(solution)/shard_map/reshape.21
  99.5 1.0 multiply_cosine_fusion
  100.4 1.7 copy.133
  102.1 2.1 collective-permute-done.1
  104.2 2.4 copy.135
  106.6 2.4 copy.137
  108.9 2.1 pad_maximum_fusion
  111.5 1.7 maximum_convert_fusion
  113.6 1.2 copy.138
  114.9 2.9 fusion.107
  117.8 1.0 multiply_reduce_fusion
  118.8 3.7 %fusion.3 = bf16[1025,2048]{0,1:T(8,128)(2,1)} fusion(f32[1025,32,4,16]{0,3,2,1:T(8,128)S(1)} %copy.138, f32[2048]{0:T(1024)S(1)} %add.157, f32[2048]{0:T(1024)S(1)} %copy-done.12, f32[1025]{0:T(1024)S(1)} %add_rsqrt_fusion, f32[1025]{0:T(1024)S(1)} %broadcast_multiply_fusion), kind=kLoop, calls=%fused_computation.4 | loop fusion | flops 10496000 | bytes 12619784 | tf_op jit(solution)/shard_map/convert_element_type | solution.py:25
  122.5 6.1 %all-gather.4.cloned.1.call-done = bf16[2048,2048]{1,0:T(8,128)(2,1)} async-done(((bf16[128,2048]{1,0:T(8,128)(2,1)}), bf16[2048,2048]{1,0:T(8,128)(2,1)}) %all-gather.4.cloned.1.call-update) | async-done | bytes 8388624 | tf_op jit(solution)/shard_map/all_gather | solution.py:109
  128.6 10.9 %fusion.12 = f32[1025,1536]{1,0:T(8,128)S(1)} fusion(bf16[1025,2048]{0,1:T(8,128)(2,1)} %fusion.3, bf16[2048,2048]{1,0:T(8,128)(2,1)} %all-gather.4.cloned.1.call-done), kind=kOutput, calls=%fused_computation.15 | convolution fusion | flops 6448742400 | bytes 17307648 | tf_op jit(solution)/shard_map/dot_general | solution.py:168
  139.5 2.9 copy-done.6
  142.4 3.1 slice.148
  145.5 6.7 %copy.142 = f32[1024,1536]{0,1:T(8,128)} copy(f32[1024,1536]{1,0:T(8,128)} %slice.148) | data formatting | bytes 12582912 | tf_op jit(solution)/shard_map/slice | solution.py:169
  152.2 0.8 slice_reduce_fusion
  154.3 1.2 reduce.17
  156.2 7.7 %all-to-all-start.1 = ((bf16[32,2,768]{2,1,0:T(2,128)(2,1)}), bf16[32,2,768]{2,1,0:T(2,128)(2,1)S(1)}, u32[]{:S(2)}, u32[]{:S(2)}) async-start(bf16[32,2,768]{2,1,0:T(2,128)(2,1)} %reshape.502), calls=%async_computation.1 | async-start | bytes 196608 | tf_op jit(solution)/shard_map/all_to_all | solution.py:192
  163.9 2.5 slice_bitcast_fusion
  166.5 1.2 subtract_convert_fusion
  167.8 5.0 %all-to-all-done.1 = bf16[32,2,768]{2,1,0:T(2,128)(2,1)S(1)} async-done(((bf16[32,2,768]{2,1,0:T(2,128)(2,1)}), bf16[32,2,768]{2,1,0:T(2,128)(2,1)S(1)}, u32[]{:S(2)}, u32[]{:S(2)}) %all-to-all-start.1) | async-done | bytes 98336 | tf_op jit(solution)/shard_map/all_to_all | solution.py:192
  173.3 5.6 %fusion.77 = f32[8,1,4096]{2,1,0:T(1,128)S(1)} fusion(bf16[8,4096,64]{2,1,0:T(8,128)(2,1)} %reshape.479, bf16[1,8,3,64]{3,2,1,0:T(4,128)(2,1)S(1)} %reshape.477), kind=kOutput, calls=%fused_computation.102 | convolution fusion | flops 4194304 | bytes 4329472 | tf_op jit(solution)/shard_map/shd,shtd->sht/dot_general | solution.py:206
  179.5 4.8 %fusion.65 = f32[8,1,64]{2,1,0:T(1,128)S(1)} fusion(bf16[8,4096,64]{2,1,0:T(8,128)(2,1)} %reshape.480, bf16[8,4096,1]{1,0,2:T(8,128)(2,1)S(1)} %fusion.71), kind=kOutput, calls=%fused_computation.78 | convolution fusion | flops 4194304 | bytes 4261888 | tf_op jit(solution)/shard_map/sht,shtd->shd/dot_general | solution.py:221
  184.6 0.8 reduce.18
  186.0 5.3 %all-to-all-start.2 = ((bf16[32,2,256]{2,1,0:T(2,128)(2,1)}), bf16[32,2,256]{2,1,0:T(2,128)(2,1)}, u32[]{:S(2)}, u32[]{:S(2)}) async-start(bf16[32,2,256]{2,1,0:T(2,128)(2,1)} %reshape.504), calls=%async_computation.2 | async-start | bytes 65536 | tf_op jit(solution)/shard_map/all_to_all | solution.py:225
  191.3 1.4 pad_maximum_fusion.3
  192.7 1.8 slice.274
  194.6 1.5 copy.144.query_ref
  196.1 1.3 copy.145.key_ref
  197.4 1.3 copy.146.value_ref
  198.7 14.0 %shard_map.140 = bf16[1024,512]{1,0:T(8,128)(2,1)} custom-call(s32[2]{0:T(128)} %lengths_ref.1, bf16[1024,512]{1,0:T(8,128)(2,1)} %copy.144.query_ref, bf16[1024,512]{1,0:T(8,128)(2,1)} %copy.145.key_ref, bf16[1024,512]{1,0:T(8,128)(2,1)} %copy.146.value_ref), custom_call_target="tpu_custom_call" | custom-call | tf_op jit(solution)/shard_map/pallas_call | solution.py:68
  212.7 0.8 reshape.505
  213.5 0.8 fusion.72
  214.3 7.7 %fusion.54 = f32[1025,2048]{1,0:T(8,128)} fusion(bf16[2048,2048]{1,0:T(8,128)(2,1)} %all-gather.4.cloned.1.call-done, bf16[1,512]{1,0:T(2,128)(2,1)S(1)} %convert_element_type.276, bf16[1024,512]{1,0:T(8,128)(2,1)} %shard_map.140), kind=kOutput, calls=%fused_computation.46 | convolution fusion | flops 2151680000 | bytes 11543552 | tf_op jit(solution)/shard_map/dot_general | solution.py:232
  222.0 20.3 %all-gather.8.cloned.1.call-done = bf16[2048,4096]{1,0:T(8,128)(2,1)} async-done(((bf16[128,4096]{1,0:T(8,128)(2,1)}), bf16[2048,4096]{1,0:T(8,128)(2,1)}) %all-gather.8.cloned.1.call-update) | async-done | bytes 16777232 | tf_op jit(solution)/shard_map/all_gather | solution.py:109
  242.3 18.7 %fusion.31 = bf16[512,2048]{1,0:T(8,128)(2,1)} fusion(f32[1025,2048]{1,0:T(8,128)} %fusion.54, bf16[2048,4096]{1,0:T(8,128)(2,1)} %all-gather.8.cloned.1.call-done, bf16[1025,2048]{0,1:T(8,128)(2,1)} %fusion.3), kind=kOutput, calls=%fused_computation.39 | convolution fusion | flops 8601468928 | bytes 25165824 | tf_op jit(solution)/shard_map/dot_general | solution.py:243
  261.0 2.9 copy.155
  263.9 1.6 copy.156
  265.6 16.4 %fusion.22 = bf16[513,2048]{1,0:T(8,128)(2,1)S(1)} fusion(f32[1025,2048]{1,0:T(8,128)} %fusion.54, bf16[2048,4096]{1,0:T(8,128)(2,1)} %all-gather.8.cloned.1.call-done, bf16[1025,2048]{0,1:T(8,128)(2,1)} %fusion.3), kind=kOutput, calls=%fused_computation.29 | convolution fusion | flops 8618268672 | bytes 25759744 | tf_op jit(solution)/shard_map/dot_general | solution.py:243
  282.0 2.6 copy.157
  284.6 3.6 %copy.158 = bf16[513,4,32,16]{0,3,2,1:T(8,128)(2,1)} copy(bf16[513,4,32,16]{0,3,1,2:T(8,128)(2,1)} %bitcast.108) | data formatting | bytes 4202496 | tf_op jit(solution)/shard_map/convert_element_type | solution.py:247
  288.2 5.4 %reduce-scatter.3.cloned.1.call-done = bf16[512,512]{0,1:T(8,128)(2,1)} async-done(((bf16[512,2048]{0,1:T(8,128)(2,1)}), bf16[512,512]{0,1:T(8,128)(2,1)}) %reduce-scatter.3.cloned.1.call-update) | async-done | bytes 524304 | tf_op jit(solution)/shard_map/reduce_scatter | solution.py:246
  293.6 1.2 add_convert_fusion.1
  294.8 34.7 %reduce-scatter.5.cloned.1.call-done = bf16[513,512]{0,1:T(8,128)(2,1)} async-done(((bf16[513,2048]{0,1:T(8,128)(2,1)}), bf16[513,512]{0,1:T(8,128)(2,1)}) %reduce-scatter.5.cloned.1.call-update) | async-done | bytes 525328 | tf_op jit(solution)/shard_map/reduce_scatter | solution.py:246
  329.5 1.3 add_convert_fusion
  330.9 1.3 copy.159
  (114 shorter events, 10.5 us)
Async XLA Ops:
  7.2 15.7 %copy-start.8 = (f32[16,6144]{1,0:T(8,128)S(1)}, f32[16,6144]{1,0:T(8,128)}, u32[]{:S(2)}) copy-start(f32[16,6144]{1,0:T(8,128)} %param.17) | copy-start | bytes 1179652
  7.2 15.8 %copy-start.11 = (f32[16,2048]{1,0:T(8,128)S(1)}, f32[16,2048]{1,0:T(8,128)}, u32[]{:S(2)}) copy-start(f32[16,2048]{1,0:T(8,128)} %param.18) | copy-start | bytes 393220
  7.2 46.6 %all-gather.6.cloned.1.call-start = ((), (), s32[]{:S(2)}) async-start(), calls=%async_computation.7 | async-start | bytes 1572864 | tf_op jit(solution)/shard_map/all_gather | solution.py:108
  9.8 44.0 %copy-start.7 = (bf16[1024,512]{1,0:T(8,128)(2,1)S(1)}, bf16[1024,512]{1,0:T(8,128)(2,1)}, u32[]{:S(2)}) copy-start(bf16[1024,512]{1,0:T(8,128)(2,1)} %param.13) | copy-start | bytes 3145732
  10.4 43.9 %copy-start.14 = (bf16[1,512]{1,0:T(2,128)(2,1)S(1)}, bf16[1,512]{1,0:T(2,128)(2,1)}, u32[]{:S(2)}) copy-start(bf16[1,512]{1,0:T(2,128)(2,1)} %param.14) | copy-start | bytes 3076
  22.8 105.8 %all-gather.4.cloned.1.call-start = ((), (), s32[]{:S(2)}) async-start(), calls=%async_computation.6 | async-start | bytes 8912896 | tf_op jit(solution)/shard_map/all_gather | solution.py:109
  45.7 196.6 %all-gather.8.cloned.1.call-start = ((), (), s32[]{:S(2)}) async-start(), calls=%async_computation.8 | async-start | bytes 17825792 | tf_op jit(solution)/shard_map/all_gather | solution.py:109
  53.8 4.4 %copy-start.13 = (f32[2048]{0:T(1024)S(1)}, f32[2048]{0:T(1024)}, u32[]{:S(2)}) copy-start(f32[2048]{0:T(1024)} %param.16) | copy-start | bytes 24580
  53.8 7.4 %copy-start.16 = (s32[32]{0:T(128)S(1)}, s32[32]{0:T(128)}, u32[]{:S(2)}) copy-start(s32[32]{0:T(128)} %param.24) | copy-start | bytes 388
  54.3 15.6 %copy-start = (bf16[1024,512]{0,1:T(8,128)(2,1)}, bf16[1024,512]{0,1:T(8,128)(2,1)S(1)}, u32[]{:S(2)}) copy-start(bf16[1024,512]{0,1:T(8,128)(2,1)S(1)} %copy.129) | copy-start | bytes 3145732
  56.1 44.3 %collective-permute-start = (bf16[1025,512]{1,0:T(8,128)(2,1)}, bf16[1025,512]{1,0:T(8,128)(2,1)}, u32[]{:S(2)}, u32[]{:S(2)}) collective-permute-start(bf16[1025,512]{1,0:T(8,128)(2,1)} %copy.132), channel_id=1, source_target_pairs={{0,32},{32,64},{64,96},{96,0},{1,33},{33,65},{65,97},{97,1},{2,34}... | collective-permute-start | bytes 3148808 | tf_op jit(solution)/shard_map/ppermute | solution.py:139
  56.9 47.2 %collective-permute-start.1 = (bf16[1025,512]{1,0:T(8,128)(2,1)}, bf16[1025,512]{1,0:T(8,128)(2,1)}, u32[]{:S(2)}, u32[]{:S(2)}) collective-permute-start(bf16[1025,512]{1,0:T(8,128)(2,1)} %copy.132), channel_id=1, source_target_pairs={{0,64},{32,96},{64,0},{96,32},{1,65},{33,97},{65,1},{97,33},{2,66}... | collective-permute-start | bytes 3148808 | tf_op jit(solution)/shard_map/ppermute | solution.py:139
  57.9 48.6 %collective-permute-start.2 = (bf16[1025,512]{1,0:T(8,128)(2,1)}, bf16[1025,512]{1,0:T(8,128)(2,1)}, u32[]{:S(2)}, u32[]{:S(2)}) collective-permute-start(bf16[1025,512]{1,0:T(8,128)(2,1)} %copy.132), channel_id=1, source_target_pairs={{0,96},{32,0},{64,32},{96,64},{1,97},{33,1},{65,33},{97,65},{2,98}... | collective-permute-start | bytes 3148808 | tf_op jit(solution)/shard_map/ppermute | solution.py:139
  111.5 1.7 copy-start.2
  111.5 1.7 copy-start.3
  111.5 1.8 copy-start.4
  111.5 2.1 copy-start.5
  117.8 1.0 copy-start.12
  139.5 2.9 copy-start.6
  145.5 7.7 %copy-start.15 = (f32[16]{0:T(128)S(1)}, f32[16]{0:T(128)}, u32[]{:S(2)}) copy-start(f32[16]{0:T(128)} %get-tuple-element.39) | copy-start | bytes 196
  156.2 10.3 %copy-start.9 = (f32[1024,16]{0,1:T(8,128)S(1)}, f32[1024,16]{0,1:T(8,128)}, u32[]{:S(2)}) copy-start(f32[1024,16]{0,1:T(8,128)} %get-tuple-element.32) | copy-start | bytes 196612
  156.2 10.3 %copy-start.10 = (f32[1024,16]{0,1:T(8,128)S(1)}, f32[1024,16]{0,1:T(8,128)}, u32[]{:S(2)}) copy-start(f32[1024,16]{0,1:T(8,128)} %get-tuple-element.33) | copy-start | bytes 196612
  156.2 16.6 %all-to-all-start.1 = ((bf16[32,2,768]{2,1,0:T(2,128)(2,1)}), bf16[32,2,768]{2,1,0:T(2,128)(2,1)S(1)}, u32[]{:S(2)}, u32[]{:S(2)}) async-start(bf16[32,2,768]{2,1,0:T(2,128)(2,1)} %reshape.502), calls=%async_computation.1 | async-start | bytes 196608 | tf_op jit(solution)/shard_map/all_to_all | solution.py:192
  166.5 6.4 %copy-start.17 = (s32[32]{0:T(128)S(1)}, s32[32]{0:T(128)}, u32[]{:S(2)}) copy-start(s32[32]{0:T(128)} %param.25) | copy-start | bytes 388
  186.0 26.7 %all-to-all-start.2 = ((bf16[32,2,256]{2,1,0:T(2,128)(2,1)}), bf16[32,2,256]{2,1,0:T(2,128)(2,1)}, u32[]{:S(2)}, u32[]{:S(2)}) async-start(bf16[32,2,256]{2,1,0:T(2,128)(2,1)} %reshape.504), calls=%async_computation.2 | async-start | bytes 65536 | tf_op jit(solution)/shard_map/all_to_all | solution.py:225
  191.3 102.3 %reduce-scatter.3.cloned.1.call-start = ((), (), s32[]{:S(2)}) async-start(), calls=%async_computation.9 | async-start | bytes 2621440 | tf_op jit(solution)/shard_map/reduce_scatter | solution.py:246
  265.5 64.0 %reduce-scatter.5.cloned.1.call-start = ((), (), s32[]{:S(2)}) async-start(), calls=%async_computation.10 | async-start | bytes 3276800 | tf_op jit(solution)/shard_map/reduce_scatter | solution.py:246
  284.6 9.0 %copy-start.1 = (bf16[1024,512]{0,1:T(8,128)(2,1)S(1)}, bf16[1024,512]{0,1:T(8,128)(2,1)}, u32[]{:S(2)}) copy-start(bf16[1024,512]{0,1:T(8,128)(2,1)} %copy-done) | copy-start | bytes 3145732
Sparse Core Ops, SparseCore 0:
  22.9 30.7 all-gather.5
  55.9 72.6 all-gather.3
  130.7 111.4 all-gather.7
  265.6 27.9 reduce-scatter.2
  296.0 33.4 reduce-scatter.4

commit v6 on v5

--- a/solution.py
+++ b/solution.py
@@ -105,8 +105,12 @@
         joined = jnp.concatenate([by_row_group(w) for w in weights], axis=2)
         swapped = lax.all_to_all(joined, "row", split_axis=1, concat_axis=0, tiled=True)
         flat = swapped.reshape(swapped.shape[0], swapped.shape[2])
-        gathered = lax.all_gather(flat, COL[-1], axis=0, tiled=True)
-        gathered = lax.all_gather(gathered, COL[:-1], axis=0, tiled=True)
+        partner = lax.ppermute(flat, COL[-1], [(0, 1), (1, 0)])
+        first = lax.axis_index(COL[-1]) == 0
+        paired = jnp.concatenate(
+            [jnp.where(first, flat, partner), jnp.where(first, partner, flat)], axis=0
+        )
+        gathered = lax.all_gather(paired, COL[:-1], axis=0, tiled=True)
         pieces = []
         offset = 0
         for w in weights:
@@ -233,7 +237,7 @@
         mixed_all, w_dense, (((1,), (1,)), ((), ())), preferred_element_type=jnp.float32
     )
     residual = jnp.concatenate([prompt_tokens, decode_tokens], axis=0)
-    bounds = [0, rows_prompt // 2, normed.shape[0]]
+    bounds = [0, rows_prompt // 4, rows_prompt // 2, 3 * rows_prompt // 4, normed.shape[0]]
     outputs = []
     for low, high in zip(bounds[:-1], bounds[1:]):
         hidden = jax.nn.gelu(

time: 345 us -> 348 us (level)
  blocking collectives: 34.6 us -> 21.4 us
  matrix products: 65.1 us -> 77.2 us
  starting transfers between devices: 15.2 us -> 24.5 us
  waiting for transfers between devices: 81.7 us -> 76.8 us
    all_gather x3 -> x2, waiting for transfers between devices: 34.5 us -> 0.01 us  [regroup(): gathered = lax.all_gather(paired, COL[:-1], axis=0, tiled=True)]
    ppermute x0 -> x2, waiting for transfers between devices: none -> 17 us  [regroup(): partner = lax.ppermute(flat, COL[-1], [(0, 1), (1, 0)])]
    all_gather x1 -> x0, blocking collectives: 13.8 us -> none  [regroup(): gathered = lax.all_gather(flat, COL[-1], axis=0, tiled=True)]
    reduce_scatter x2 -> x4, waiting for transfers between devices: 40.1 us -> 52.8 us  [on_device(): lax.psum_scatter(from_gathered(attn_part[low:high] + mlp_part).astype(hal...]
    dot_general x2 -> x4, matrix products: 35.1 us -> 47.5 us  [on_device(): lax.dot_general(hidden, w_reduce, (((1,), (1,)), ((), ())), preferred_ele...]
    ppermute x0 -> x2, starting transfers between devices: none -> 5.14 us  [regroup(): partner = lax.ppermute(flat, COL[-1], [(0, 1), (1, 0)])]
    convert_element_type x4 -> x8, local copies, waits for them, and re-layouts: 10.7 us -> 7.94 us  [on_device(): from_gathered(attn_part[low:high] + mlp_part).astype(half_float)]
  transfers between devices with their start and end apart: 10 -> 13, of which waited for: 7 -> 7; matrix products, arithmetic and copies ran while one was open for 43% -> 49% of each run, Pallas kernels for 4% -> 4%
where the time goes in v6:
time: 348 us; the launch traced here: 342 us
  local copies, waits for them, and re-layouts  85.5 us (25%)
  matrix products  77.2 us (22%)
  waiting for transfers between devices  76.8 us (22%)
  other arithmetic  27.5 us (8%)
  starting transfers between devices  24.5 us (7%)
  blocking collectives  21.4 us (6%)
  between operations  15.6 us (4%)
  Pallas kernels  13.9 us (4%)
    reduce_scatter x4, waiting for transfers between devices, on_device(): lax.psum_scatter(from_gathered(attn_part[low:high] + mlp_part).astype(hal...  52.8 us
    dot_general x4, matrix products, on_device(): lax.dot_general(hidden, w_reduce, (((1,), (1,)), ((), ())), preferred_ele...  47.5 us
    another operation x2, local copies, waits for them, and re-layouts  22.3 us
    all_to_all x2, blocking collectives, regroup(): lax.all_to_all(joined, 'row', split_axis=1, concat_axis=0, tiled=True)  21.4 us
    unnamed x46, local copies, waits for them, and re-layouts  20.4 us
    ppermute x2, waiting for transfers between devices, regroup(): partner = lax.ppermute(flat, COL[-1], [(0, 1), (1, 0)])  17 us
    pallas_call x1, Pallas kernels, prompt_attention(): pl.pallas_call(functools.partial(attention_kernel, heads=heads), out_shap...  13.9 us
    dot_general x1, matrix products, on_device(): merged = jnp.dot(normed, w_project, preferred_element_type=jnp.float32)  10.8 us
  transfers between devices with their start and end apart: 13, of which 7 were waited for; matrix products, arithmetic and copies ran while one was open for 49% of the time, Pallas kernels for 4%

profile of v6, /device:TPU:1, one launch (start us, length us, event | category | flops | bytes accessed | tf_op | source)
XLA Modules:
  0.0 342.5 jit_solution(9099536999480571085)
XLA Ops:
  7.2 1.0 convert_element_type.306
  8.4 0.9 convert_element_type.307
  9.6 9.2 %all_to_all.48 = bf16[16,4,2048]{2,0,1:T(8,128)(2,1)S(1)} all-to-all(bf16[16,4,2048]{2,0,1:T(8,128)(2,1)S(1)} %copy.167), channel_id=1, replica_groups=mesh['row'=4,'col_y'=4,'col_z'=4,'col_x'=2] {'row'}, dimensions={1} | all-to-all | bytes 524288 | tf_op jit(solution)/shard_map/all_to_all | solution.py:106
  18.8 2.6 collective-permute-start.3
  21.4 5.7 %collective-permute-done.3 = bf16[64,2048]{1,0:T(8,128)(2,1)S(1)} collective-permute-done((bf16[64,2048]{1,0:T(8,128)(2,1)S(1)}, bf16[64,2048]{1,0:T(8,128)(2,1)S(1)}, u32[]{:S(2)}, u32[]{:S(2)}) %collective-permute-start.3) | collective-permute-done | bytes 262176 | tf_op jit(solution)/shard_map/ppermute | solution.py:108
  27.2 0.8 pad_maximum_fusion.8
  29.2 12.2 %all_to_all.49 = bf16[16,4,4096]{2,0,1:T(8,128)(2,1)S(1)} all-to-all(bf16[16,4,4096]{2,0,1:T(8,128)(2,1)S(1)} %copy.180), channel_id=1, replica_groups=mesh['row'=4,'col_y'=4,'col_z'=4,'col_x'=2] {'row'}, dimensions={1} | all-to-all | bytes 1048576 | tf_op jit(solution)/shard_map/all_to_all | solution.py:106
  41.3 2.6 collective-permute-start.4
  43.9 11.3 %collective-permute-done.4 = bf16[64,4096]{1,0:T(8,128)(2,1)S(1)} collective-permute-done((bf16[64,4096]{1,0:T(8,128)(2,1)S(1)}, bf16[64,4096]{1,0:T(8,128)(2,1)S(1)}, u32[]{:S(2)}, u32[]{:S(2)}) %collective-permute-start.4) | collective-permute-done | bytes 524320 | tf_op jit(solution)/shard_map/ppermute | solution.py:108
  55.3 1.1 pad_maximum_fusion.7
  57.4 1.4 copy.158
  58.8 2.4 collective-permute-start
  61.1 1.0 collective-permute-start.1
  64.4 1.2 dynamic_slice.23
  66.3 1.2 fusion.160
  68.1 6.1 %reshape.508 = bf16[2097152]{0:T(1024)(128)(2,1)} reshape(bf16[1,8,262144]{2,1,0:T(8,128)(2,1)} %param.21) | data formatting | bytes 8388608
  74.3 11.2 %reshape.487 = bf16[8,4096,64]{2,1,0:T(8,128)(2,1)} reshape(bf16[2097152]{0:T(1024)(128)(2,1)} %reshape.508) | data formatting | bytes 8388608 | tf_op jit(solution)/shard_map/reshape.15
  85.4 6.2 %reshape.506 = bf16[2097152]{0:T(1024)(128)(2,1)} reshape(bf16[1,8,262144]{2,1,0:T(8,128)(2,1)} %param.22) | data formatting | bytes 8388608
  91.6 11.1 %reshape.488 = bf16[8,4096,64]{2,1,0:T(8,128)(2,1)} reshape(bf16[2097152]{0:T(1024)(128)(2,1)} %reshape.506) | data formatting | bytes 8388608 | tf_op jit(solution)/shard_map/reshape.21
  104.0 1.0 multiply_cosine_fusion
  104.9 1.7 copy.159
  106.6 1.5 collective-permute-done.1
  108.1 2.4 copy.161
  110.5 2.4 copy.163
  112.8 2.1 pad_maximum_fusion
  115.3 1.7 maximum_convert_fusion
  117.5 1.2 copy.164
  118.7 2.7 fusion.183
  121.5 1.0 multiply_reduce_fusion
  122.5 3.6 %fusion.3 = bf16[1025,2048]{0,1:T(8,128)(2,1)} fusion(f32[1025,32,4,16]{0,3,2,1:T(8,128)S(1)} %copy.164, f32[2048]{0:T(1024)S(1)} %add.182, f32[2048]{0:T(1024)S(1)} %copy-done.12, f32[1025]{0:T(1024)S(1)} %add_rsqrt_fusion, f32[1025]{0:T(1024)S(1)} %broadcast_multiply_fusion), kind=kLoop, calls=%fused_computation.4 | loop fusion | flops 10496000 | bytes 12619784 | tf_op jit(solution)/shard_map/convert_element_type | solution.py:25
  126.2 10.8 %fusion.4 = f32[1025,1536]{1,0:T(8,128)S(1)} fusion(bf16[1025,2048]{0,1:T(8,128)(2,1)} %fusion.3, bf16[2048,2048]{1,0:T(8,128)(2,1)} %all-gather.3.cloned.1.call-done), kind=kOutput, calls=%fused_computation.6 | convolution fusion | flops 6448742400 | bytes 17307648 | tf_op jit(solution)/shard_map/dot_general | solution.py:172
  137.0 2.7 copy-done.6
  139.7 3.1 slice.172
  142.8 7.2 %copy.168 = f32[1024,1536]{0,1:T(8,128)} copy(f32[1024,1536]{1,0:T(8,128)} %slice.172) | data formatting | bytes 12582912 | tf_op jit(solution)/shard_map/slice | solution.py:173
  152.1 1.2 reduce.17
  154.0 10.3 %all-to-all-start.1 = ((bf16[32,2,768]{2,1,0:T(2,128)(2,1)}), bf16[32,2,768]{2,1,0:T(2,128)(2,1)S(1)}, u32[]{:S(2)}, u32[]{:S(2)}) async-start(bf16[32,2,768]{2,1,0:T(2,128)(2,1)} %reshape.510), calls=%async_computation.1 | async-start | bytes 196608 | tf_op jit(solution)/shard_map/all_to_all | solution.py:196
  164.2 2.6 slice_bitcast_fusion
  166.8 1.2 subtract_convert_fusion
  168.2 5.4 %all-to-all-done.1 = bf16[32,2,768]{2,1,0:T(2,128)(2,1)S(1)} async-done(((bf16[32,2,768]{2,1,0:T(2,128)(2,1)}), bf16[32,2,768]{2,1,0:T(2,128)(2,1)S(1)}, u32[]{:S(2)}, u32[]{:S(2)}) %all-to-all-start.1) | async-done | bytes 98336 | tf_op jit(solution)/shard_map/all_to_all | solution.py:196
  174.0 5.7 %fusion.145 = f32[8,1,4096]{2,1,0:T(1,128)S(1)} fusion(bf16[8,4096,64]{2,1,0:T(8,128)(2,1)} %reshape.487, bf16[1,8,3,64]{3,2,1,0:T(4,128)(2,1)S(1)} %reshape.485), kind=kOutput, calls=%fused_computation.152 | convolution fusion | flops 4194304 | bytes 4329472 | tf_op jit(solution)/shard_map/shd,shtd->sht/dot_general | solution.py:210
  180.4 4.6 %fusion.133 = f32[8,1,64]{2,1,0:T(1,128)S(1)} fusion(bf16[8,4096,64]{2,1,0:T(8,128)(2,1)} %reshape.488, bf16[8,4096,1]{1,0,2:T(8,128)(2,1)S(1)} %fusion.139), kind=kOutput, calls=%fused_computation.128 | convolution fusion | flops 4194304 | bytes 4261888 | tf_op jit(solution)/shard_map/sht,shtd->shd/dot_general | solution.py:225
  186.7 4.5 %all-to-all-start.2 = ((bf16[32,2,256]{2,1,0:T(2,128)(2,1)}), bf16[32,2,256]{2,1,0:T(2,128)(2,1)}, u32[]{:S(2)}, u32[]{:S(2)}) async-start(bf16[32,2,256]{2,1,0:T(2,128)(2,1)} %reshape.512), calls=%async_computation.2 | async-start | bytes 65536 | tf_op jit(solution)/shard_map/all_to_all | solution.py:229
  191.2 1.4 pad_maximum_fusion.5
  192.6 1.8 slice.344
  194.4 1.5 copy.170.query_ref
  195.9 1.3 copy.171.key_ref
  197.2 1.3 copy.172.value_ref
  198.6 13.9 %shard_map.140 = bf16[1024,512]{1,0:T(8,128)(2,1)} custom-call(s32[2]{0:T(128)} %lengths_ref.1, bf16[1024,512]{1,0:T(8,128)(2,1)} %copy.170.query_ref, bf16[1024,512]{1,0:T(8,128)(2,1)} %copy.171.key_ref, bf16[1024,512]{1,0:T(8,128)(2,1)} %copy.172.value_ref), custom_call_target="tpu_custom_call" | custom-call | tf_op jit(solution)/shard_map/pallas_call | solution.py:68
  214.1 7.6 %fusion.102 = f32[1025,2048]{1,0:T(8,128)} fusion(bf16[2048,2048]{1,0:T(8,128)(2,1)} %all-gather.3.cloned.1.call-done, bf16[1,512]{1,0:T(2,128)(2,1)S(1)} %convert_element_type.324, bf16[1024,512]{1,0:T(8,128)(2,1)} %shard_map.140), kind=kOutput, calls=%fused_computation.70 | convolution fusion | flops 2151680000 | bytes 11543552 | tf_op jit(solution)/shard_map/dot_general | solution.py:236
  221.6 11.4 %fusion.40 = bf16[256,2048]{1,0:T(8,128)(2,1)S(1)} fusion(bf16[2048,4096]{1,0:T(8,128)(2,1)} %all-gather.5.cloned.1.call-done, f32[1025,2048]{1,0:T(8,128)} %fusion.102, bf16[1025,2048]{0,1:T(8,128)(2,1)} %fusion.3), kind=kOutput, calls=%fused_computation.36 | convolution fusion | flops 4300734464 | bytes 20971520 | tf_op jit(solution)/shard_map/dot_general | solution.py:247
  233.6 1.1 copy.185
  235.2 11.4 %fusion.37 = bf16[256,2048]{1,0:T(8,128)(2,1)S(1)} fusion(bf16[2048,4096]{1,0:T(8,128)(2,1)} %all-gather.5.cloned.1.call-done, f32[1025,2048]{1,0:T(8,128)} %fusion.102, bf16[1025,2048]{0,1:T(8,128)(2,1)} %fusion.3), kind=kOutput, calls=%fused_computation.35 | convolution fusion | flops 4300734464 | bytes 20971520 | tf_op jit(solution)/shard_map/dot_general | solution.py:247
  247.1 1.1 copy.188
  248.3 11.6 %fusion.43 = bf16[256,2048]{1,0:T(8,128)(2,1)S(1)} fusion(bf16[2048,4096]{1,0:T(8,128)(2,1)} %all-gather.5.cloned.1.call-done, f32[1025,2048]{1,0:T(8,128)} %fusion.102, bf16[1025,2048]{0,1:T(8,128)(2,1)} %fusion.3), kind=kOutput, calls=%fused_computation.37 | convolution fusion | flops 4300734464 | bytes 20971520 | tf_op jit(solution)/shard_map/dot_general | solution.py:247
  260.4 1.1 copy.182
  261.7 13.1 %fusion.34 = bf16[257,2048]{1,0:T(8,128)(2,1)} fusion(bf16[2048,4096]{1,0:T(8,128)(2,1)} %all-gather.5.cloned.1.call-done, f32[1025,2048]{1,0:T(8,128)} %fusion.102, bf16[1025,2048]{0,1:T(8,128)(2,1)} %fusion.3), kind=kOutput, calls=%fused_computation.34 | convolution fusion | flops 4317534208 | bytes 21565440 | tf_op jit(solution)/shard_map/dot_general | solution.py:247
  274.8 1.8 copy.189
  276.6 1.3 copy.190
  278.0 2.6 reduce-scatter.9.cloned.1.call-done
  280.6 24.2 %reduce-scatter.5.cloned.1.call-done = bf16[256,512]{0,1:T(8,128)(2,1)} async-done(((bf16[256,2048]{0,1:T(8,128)(2,1)}), bf16[256,512]{0,1:T(8,128)(2,1)}) %reduce-scatter.5.cloned.1.call-update) | async-done | bytes 262160 | tf_op jit(solution)/shard_map/reduce_scatter | solution.py:250
  304.8 1.3 add_convert_fusion.3
  306.1 26.0 %reduce-scatter.11.cloned.1.call-done = bf16[257,512]{0,1:T(8,128)(2,1)} async-done(((bf16[257,2048]{0,1:T(8,128)(2,1)}), bf16[257,512]{0,1:T(8,128)(2,1)}) %reduce-scatter.11.cloned.1.call-update) | async-done | bytes 263184 | tf_op jit(solution)/shard_map/reduce_scatter | solution.py:250
  332.1 1.1 add_convert_fusion
  333.4 1.3 copy.191
  (130 shorter events, 18.0 us)
Async XLA Ops:
  7.2 119.0 %all-gather.3.cloned.1.call-start = ((), (), s32[]{:S(2)}) async-start(), calls=%async_computation.8 | async-start | bytes 8912896 | tf_op jit(solution)/shard_map/all_gather | solution.py:113
  9.3 18.8 %copy-start.8 = (f32[16,8192]{1,0:T(8,128)S(1)}, f32[16,8192]{1,0:T(8,128)}, u32[]{:S(2)}) copy-start(f32[16,8192]{1,0:T(8,128)} %param.19) | copy-start | bytes 1572868
  9.6 18.7 %copy-start.9 = (f32[16,8192]{1,0:T(8,128)S(1)}, f32[16,8192]{1,0:T(8,128)}, u32[]{:S(2)}) copy-start(f32[16,8192]{1,0:T(8,128)} %param.20) | copy-start | bytes 1572868
  18.8 8.3 %collective-permute-start.3 = (bf16[64,2048]{1,0:T(8,128)(2,1)S(1)}, bf16[64,2048]{1,0:T(8,128)(2,1)S(1)}, u32[]{:S(2)}, u32[]{:S(2)}) collective-permute-start(bf16[64,2048]{1,0:T(8,128)(2,1)S(1)} %bitcast.134), channel_id=1, source_target_pairs={{0,1},{1,0},{2,3},{3,2},{4,5},{5,4},{6,7},{7,6},{8,9},{9,8},{10,11... | collective-permute-start | bytes 786440 | tf_op jit(solution)/shard_map/ppermute | solution.py:108
  28.0 193.6 %all-gather.5.cloned.1.call-start = ((), (), s32[]{:S(2)}) async-start(), calls=%async_computation.9 | async-start | bytes 17825792 | tf_op jit(solution)/shard_map/all_gather | solution.py:113
  41.3 15.1 %copy-start.7 = (bf16[1024,512]{1,0:T(8,128)(2,1)S(1)}, bf16[1024,512]{1,0:T(8,128)(2,1)}, u32[]{:S(2)}) copy-start(bf16[1024,512]{1,0:T(8,128)(2,1)} %param.13) | copy-start | bytes 3145732
  41.3 13.9 %collective-permute-start.4 = (bf16[64,4096]{1,0:T(8,128)(2,1)S(1)}, bf16[64,4096]{1,0:T(8,128)(2,1)S(1)}, u32[]{:S(2)}, u32[]{:S(2)}) collective-permute-start(bf16[64,4096]{1,0:T(8,128)(2,1)S(1)} %bitcast.133), channel_id=1, source_target_pairs={{0,1},{1,0},{2,3},{3,2},{4,5},{5,4},{6,7},{7,6},{8,9},{9,8},{10,11... | collective-permute-start | bytes 1572872 | tf_op jit(solution)/shard_map/ppermute | solution.py:108
  55.3 1.7 copy-start.14
  57.0 1.8 copy-start
  57.2 5.5 %copy-start.13 = (f32[2048]{0:T(1024)S(1)}, f32[2048]{0:T(1024)}, u32[]{:S(2)}) copy-start(f32[2048]{0:T(1024)} %param.16) | copy-start | bytes 24580
  57.4 8.3 %copy-start.16 = (s32[32]{0:T(128)S(1)}, s32[32]{0:T(128)}, u32[]{:S(2)}) copy-start(s32[32]{0:T(128)} %param.24) | copy-start | bytes 388
  58.8 46.2 %collective-permute-start = (bf16[1025,512]{1,0:T(8,128)(2,1)}, bf16[1025,512]{1,0:T(8,128)(2,1)}, u32[]{:S(2)}, u32[]{:S(2)}) collective-permute-start(bf16[1025,512]{1,0:T(8,128)(2,1)} %copy.158), channel_id=1, source_target_pairs={{0,32},{32,64},{64,96},{96,0},{1,33},{33,65},{65,97},{97,1},{2,34}... | collective-permute-start | bytes 3148808 | tf_op jit(solution)/shard_map/ppermute | solution.py:143
  61.1 47.0 %collective-permute-start.1 = (bf16[1025,512]{1,0:T(8,128)(2,1)}, bf16[1025,512]{1,0:T(8,128)(2,1)}, u32[]{:S(2)}, u32[]{:S(2)}) collective-permute-start(bf16[1025,512]{1,0:T(8,128)(2,1)} %copy.158), channel_id=1, source_target_pairs={{0,64},{32,96},{64,0},{96,32},{1,65},{33,97},{65,1},{97,33},{2,66}... | collective-permute-start | bytes 3148808 | tf_op jit(solution)/shard_map/ppermute | solution.py:143
  62.1 48.4 %collective-permute-start.2 = (bf16[1025,512]{1,0:T(8,128)(2,1)}, bf16[1025,512]{1,0:T(8,128)(2,1)}, u32[]{:S(2)}, u32[]{:S(2)}) collective-permute-start(bf16[1025,512]{1,0:T(8,128)(2,1)} %copy.158), channel_id=1, source_target_pairs={{0,96},{32,0},{64,32},{96,64},{1,97},{33,1},{65,33},{97,65},{2,98}... | collective-permute-start | bytes 3148808 | tf_op jit(solution)/shard_map/ppermute | solution.py:143
  115.3 1.7 copy-start.2
  115.3 1.7 copy-start.3
  115.3 1.8 copy-start.4
  115.3 2.1 copy-start.5
  121.5 1.0 copy-start.12
  137.0 2.7 copy-start.6
  142.8 8.1 %copy-start.15 = (f32[16]{0:T(128)S(1)}, f32[16]{0:T(128)}, u32[]{:S(2)}) copy-start(f32[16]{0:T(128)} %get-tuple-element.46) | copy-start | bytes 196
  154.0 19.6 %all-to-all-start.1 = ((bf16[32,2,768]{2,1,0:T(2,128)(2,1)}), bf16[32,2,768]{2,1,0:T(2,128)(2,1)S(1)}, u32[]{:S(2)}, u32[]{:S(2)}) async-start(bf16[32,2,768]{2,1,0:T(2,128)(2,1)} %reshape.510), calls=%async_computation.1 | async-start | bytes 196608 | tf_op jit(solution)/shard_map/all_to_all | solution.py:196
  164.2 2.6 copy-start.10
  164.2 2.6 copy-start.11
  166.8 6.8 %copy-start.17 = (s32[32]{0:T(128)S(1)}, s32[32]{0:T(128)}, u32[]{:S(2)}) copy-start(s32[32]{0:T(128)} %param.25) | copy-start | bytes 388
  186.7 25.8 %all-to-all-start.2 = ((bf16[32,2,256]{2,1,0:T(2,128)(2,1)}), bf16[32,2,256]{2,1,0:T(2,128)(2,1)}, u32[]{:S(2)}, u32[]{:S(2)}) async-start(bf16[32,2,256]{2,1,0:T(2,128)(2,1)} %reshape.512), calls=%async_computation.2 | async-start | bytes 65536 | tf_op jit(solution)/shard_map/all_to_all | solution.py:229
  191.2 86.9 %reduce-scatter.7.cloned.1.call-start = ((), (), s32[]{:S(2)}) async-start(), calls=%async_computation.11 | async-start | bytes 1310720 | tf_op jit(solution)/shard_map/reduce_scatter | solution.py:250
  234.7 45.9 %reduce-scatter.9.cloned.1.call-start = ((), (), s32[]{:S(2)}) async-start(), calls=%async_computation.12 | async-start | bytes 1310720 | tf_op jit(solution)/shard_map/reduce_scatter | solution.py:250
  248.2 56.6 %reduce-scatter.5.cloned.1.call-start = ((), (), s32[]{:S(2)}) async-start(), calls=%async_computation.10 | async-start | bytes 1310720 | tf_op jit(solution)/shard_map/reduce_scatter | solution.py:250
  261.5 70.6 %reduce-scatter.11.cloned.1.call-start = ((), (), s32[]{:S(2)}) async-start(), calls=%async_computation.13 | async-start | bytes 1966080 | tf_op jit(solution)/shard_map/reduce_scatter | solution.py:250
  276.6 28.2 %copy-start.1 = (bf16[1024,512]{0,1:T(8,128)(2,1)S(1)}, bf16[1024,512]{0,1:T(8,128)(2,1)}, u32[]{:S(2)}) copy-start(bf16[1024,512]{0,1:T(8,128)(2,1)} %copy-done) | copy-start | bytes 3145732
Sparse Core Ops, SparseCore 0:
  28.1 74.3 all-gather.2
  105.3 112.4 all-gather.4
  234.8 21.9 reduce-scatter.6
  259.2 21.3 reduce-scatter.8
  283.4 21.3 reduce-scatter.4
  307.2 24.8 reduce-scatter.10

commit v7 on v6

--- a/solution.py
+++ b/solution.py
@@ -15,6 +15,7 @@
 
 NEG = -1e30
 COL = ("col_y", "col_z", "col_x")
+ROW = ("row_x", "row_core")
 
 
 def layer_norm(rows, gain, bias):
@@ -94,7 +95,7 @@
     slot_request,
 ):
     half_float = jnp.bfloat16
-    row_count = lax.axis_size("row")
+    row_count = lax.axis_size(ROW)
     col_count = lax.axis_size(COL)
 
     def by_row_group(weight):
@@ -103,7 +104,7 @@
 
     def regroup(weights):
         joined = jnp.concatenate([by_row_group(w) for w in weights], axis=2)
-        swapped = lax.all_to_all(joined, "row", split_axis=1, concat_axis=0, tiled=True)
+        swapped = lax.all_to_all(joined, ROW, split_axis=1, concat_axis=0, tiled=True)
         flat = swapped.reshape(swapped.shape[0], swapped.shape[2])
         partner = lax.ppermute(flat, COL[-1], [(0, 1), (1, 0)])
         first = lax.axis_index(COL[-1]) == 0
@@ -138,10 +139,10 @@
     w_project, w_dense = regroup((project_weight, dense_weight))
     w_expand, w_reduce = regroup((expand_weight, reduce_weight))
     local_joined = jnp.concatenate([prompt_tokens, decode_tokens], axis=0)
-    row_index = lax.axis_index("row")
+    row_index = lax.axis_index(ROW)
     shifted = [local_joined] + [
         lax.ppermute(
-            local_joined, "row", [(j, (j + k) % row_count) for j in range(row_count)]
+            local_joined, ROW, [(j, (j + k) % row_count) for j in range(row_count)]
         )
         for k in range(1, row_count)
     ]
@@ -237,7 +238,7 @@
         mixed_all, w_dense, (((1,), (1,)), ((), ())), preferred_element_type=jnp.float32
     )
     residual = jnp.concatenate([prompt_tokens, decode_tokens], axis=0)
-    bounds = [0, rows_prompt // 4, rows_prompt // 2, 3 * rows_prompt // 4, normed.shape[0]]
+    bounds = [0, rows_prompt // 2, normed.shape[0]]
     outputs = []
     for low, high in zip(bounds[:-1], bounds[1:]):
         hidden = jax.nn.gelu(
@@ -247,12 +248,12 @@
         mlp_part = lax.dot_general(
             hidden, w_reduce, (((1,), (1,)), ((), ())), preferred_element_type=jnp.float32
         )
-        summed = lax.psum_scatter(
-            from_gathered(attn_part[low:high] + mlp_part).astype(half_float),
-            "row",
-            scatter_dimension=1,
-            tiled=True,
-        )
+        chunk = (attn_part[low:high] + mlp_part).astype(half_float)
+        chunk = chunk.reshape(high - low, col_count, 2, row_count // 2, -1)
+        chunk = chunk.transpose(3, 2, 0, 1, 4).reshape(row_count // 2, 2, high - low, -1)
+        chunk = lax.psum_scatter(chunk, ROW[1], scatter_dimension=0, tiled=True)
+        chunk = lax.psum_scatter(chunk, ROW[0], scatter_dimension=1, tiled=True)
+        summed = chunk.reshape(high - low, -1)
         outputs.append(
             (residual[low:high].astype(jnp.float32) + summed.astype(jnp.float32)).astype(half_float)
         )
@@ -263,24 +264,24 @@
 def solution(mesh):
     col_size = mesh.shape["col"]
     fine_mesh = jax.sharding.Mesh(
-        mesh.devices.reshape(mesh.shape["row"], 4, col_size // 8, 2), ("row",) + COL
+        mesh.devices.reshape(mesh.shape["row"] // 2, 2, 4, col_size // 8, 2), ROW + COL
     )
     in_specs = (
-        P(COL, "row"),
-        P(COL, "row"),
-        P(),
-        P(),
-        P(("row",) + COL, None),
-        P(("row",) + COL, None),
-        P(("row",) + COL, None),
-        P(("row",) + COL, None),
-        P(COL, "row", None),
-        P(COL, "row", None),
+        P(COL, ROW),
+        P(COL, ROW),
+        P(),
+        P(),
+        P(ROW + COL, None),
+        P(ROW + COL, None),
+        P(ROW + COL, None),
+        P(ROW + COL, None),
+        P(COL, ROW, None),
+        P(COL, ROW, None),
         P(COL),
         P(),
         P(),
     )
-    out_specs = (P(COL, "row"), P(COL, "row"))
+    out_specs = (P(COL, ROW), P(COL, ROW))
     return jax.shard_map(
         on_device, mesh=fine_mesh, in_specs=in_specs, out_specs=out_specs, check_vma=False
     )

time: 348 us -> 353 us (1.014)
  waiting for transfers between devices: 76.8 us -> 91.8 us
  matrix products: 77.2 us -> 64.9 us
    reduce_scatter x4, waiting for transfers between devices: 52.8 us -> 67.5 us  [the longest x2 53.8 us: on_device(): chunk = lax.psum_scatter(chunk, ROW[0], scatter_dimension=1, tiled=True)]
    dot_general x4 -> x2, matrix products: 47.5 us -> 35.2 us  [on_device(): lax.dot_general(hidden, w_reduce, (((1,), (1,)), ((), ())), preferred_ele...]
    transpose x0 -> x2, local copies, waits for them, and re-layouts: none -> 5.16 us  [on_device(): chunk.transpose(3, 2, 0, 1, 4).reshape(row_count // 2, 2, high - low, -1)]
    convert_element_type x8 -> x2, local copies, waits for them, and re-layouts: 7.94 us -> 5.43 us  [on_device(): chunk = (attn_part[low:high] + mlp_part).astype(half_float)]
  transfers between devices with their start and end apart: 13 -> 13, of which waited for: 7 -> 7; matrix products, arithmetic and copies ran while one was open for 49% -> 42% of each run, Pallas kernels for 4% -> 4%
where the time goes in v7:
time: 353 us; the launch traced here: 348 us
  waiting for transfers between devices  91.8 us (26%)
  local copies, waits for them, and re-layouts  87.8 us (25%)
  matrix products  64.9 us (18%)
  other arithmetic  27.7 us (8%)
  starting transfers between devices  24.7 us (7%)
  blocking collectives  21.2 us (6%)
  between operations  15.7 us (4%)
  Pallas kernels  13.9 us (4%)
    reduce_scatter x2, waiting for transfers between devices, on_device(): chunk = lax.psum_scatter(chunk, ROW[0], scatter_dimension=1, tiled=True)  53.8 us
    dot_general x2, matrix products, on_device(): lax.dot_general(hidden, w_reduce, (((1,), (1,)), ((), ())), preferred_ele...  35.2 us
    another operation x2, local copies, waits for them, and re-layouts  22.2 us
    all_to_all x2, blocking collectives, regroup(): lax.all_to_all(joined, ROW, split_axis=1, concat_axis=0, tiled=True)  21.2 us
    unnamed x46, local copies, waits for them, and re-layouts  20.4 us
    ppermute x2, waiting for transfers between devices, regroup(): partner = lax.ppermute(flat, COL[-1], [(0, 1), (1, 0)])  17 us
    pallas_call x1, Pallas kernels, prompt_attention(): pl.pallas_call(functools.partial(attention_kernel, heads=heads), out_shap...  13.9 us
    reduce_scatter x2, waiting for transfers between devices, on_device(): chunk = lax.psum_scatter(chunk, ROW[1], scatter_dimension=0, tiled=True)  13.7 us
  transfers between devices with their start and end apart: 13, of which 7 were waited for; matrix products, arithmetic and copies ran while one was open for 42% of the time, Pallas kernels for 4%

profile of v7, /device:TPU:1, one launch (start us, length us, event | category | flops | bytes accessed | tf_op | source)
XLA Modules:
  0.0 347.8 jit_solution(12490978963372992516)
XLA Ops:
  7.2 1.1 convert_element_type.246
  8.5 0.9 convert_element_type.247
  9.7 9.1 %all_to_all.48 = bf16[16,4,2048]{2,0,1:T(8,128)(2,1)S(1)} all-to-all(bf16[16,4,2048]{2,0,1:T(8,128)(2,1)S(1)} %copy.141), channel_id=1, replica_groups=mesh['row_x'=2,'row_core'=2,'col_y'=4,'col_z'=4,'col_x'=2] {'row_x','row..., dimensions={1} | all-to-all | bytes 524288 | tf_op jit(solution)/shard_map/all_to_all | solution.py:107
  18.8 2.6 collective-permute-start.3
  21.4 5.7 %collective-permute-done.3 = bf16[64,2048]{1,0:T(8,128)(2,1)S(1)} collective-permute-done((bf16[64,2048]{1,0:T(8,128)(2,1)S(1)}, bf16[64,2048]{1,0:T(8,128)(2,1)S(1)}, u32[]{:S(2)}, u32[]{:S(2)}) %collective-permute-start.3) | collective-permute-done | bytes 262176 | tf_op jit(solution)/shard_map/ppermute | solution.py:109
  27.1 0.8 pad_maximum_fusion.6
  29.1 12.2 %all_to_all.49 = bf16[16,4,4096]{2,0,1:T(8,128)(2,1)S(1)} all-to-all(bf16[16,4,4096]{2,0,1:T(8,128)(2,1)S(1)} %copy.154), channel_id=1, replica_groups=mesh['row_x'=2,'row_core'=2,'col_y'=4,'col_z'=4,'col_x'=2] {'row_x','row..., dimensions={1} | all-to-all | bytes 1048576 | tf_op jit(solution)/shard_map/all_to_all | solution.py:107
  41.3 2.6 collective-permute-start.4
  43.9 11.3 %collective-permute-done.4 = bf16[64,4096]{1,0:T(8,128)(2,1)S(1)} collective-permute-done((bf16[64,4096]{1,0:T(8,128)(2,1)S(1)}, bf16[64,4096]{1,0:T(8,128)(2,1)S(1)}, u32[]{:S(2)}, u32[]{:S(2)}) %collective-permute-start.4) | collective-permute-done | bytes 524320 | tf_op jit(solution)/shard_map/ppermute | solution.py:109
  55.3 1.1 pad_maximum_fusion.5
  57.4 1.4 copy.132
  58.8 2.4 collective-permute-start
  61.1 1.0 collective-permute-start.1
  64.1 1.2 dynamic_slice.23
  65.9 1.3 fusion.94
  67.8 6.2 %reshape.516 = bf16[2097152]{0:T(1024)(128)(2,1)} reshape(bf16[1,8,262144]{2,1,0:T(8,128)(2,1)} %param.21) | data formatting | bytes 8388608
  74.0 11.2 %reshape.489 = bf16[8,4096,64]{2,1,0:T(8,128)(2,1)} reshape(bf16[2097152]{0:T(1024)(128)(2,1)} %reshape.516) | data formatting | bytes 8388608 | tf_op jit(solution)/shard_map/reshape.15
  85.2 6.1 %reshape.514 = bf16[2097152]{0:T(1024)(128)(2,1)} reshape(bf16[1,8,262144]{2,1,0:T(8,128)(2,1)} %param.22) | data formatting | bytes 8388608
  91.3 11.1 %reshape.490 = bf16[8,4096,64]{2,1,0:T(8,128)(2,1)} reshape(bf16[2097152]{0:T(1024)(128)(2,1)} %reshape.514) | data formatting | bytes 8388608 | tf_op jit(solution)/shard_map/reshape.21
  103.5 1.0 multiply_cosine_fusion
  104.5 1.7 copy.133
  106.2 1.9 collective-permute-done.1
  108.1 2.4 copy.135
  110.4 2.4 copy.137
  112.8 2.3 pad_maximum_fusion
  115.5 1.7 maximum_convert_fusion
  117.6 1.2 copy.138
  118.9 2.7 fusion.109
  121.6 1.0 multiply_reduce_fusion
  122.7 3.7 %fusion.3 = bf16[1025,2048]{0,1:T(8,128)(2,1)} fusion(f32[1025,32,4,16]{0,3,2,1:T(8,128)S(1)} %copy.138, f32[2048]{0:T(1024)S(1)} %add.165, f32[2048]{0:T(1024)S(1)} %copy-done.12, f32[1025]{0:T(1024)S(1)} %add_rsqrt_fusion, f32[1025]{0:T(1024)S(1)} %broadcast_multiply_fusion), kind=kLoop, calls=%fused_computation.4 | loop fusion | flops 10496000 | bytes 12619784 | tf_op jit(solution)/shard_map/convert_element_type | solution.py:26
  126.3 11.1 %fusion.12 = f32[1025,1536]{1,0:T(8,128)S(1)} fusion(bf16[1025,2048]{0,1:T(8,128)(2,1)} %fusion.3, bf16[2048,2048]{1,0:T(8,128)(2,1)} %all-gather.3.cloned.1.call-done), kind=kOutput, calls=%fused_computation.15 | convolution fusion | flops 6448742400 | bytes 17307648 | tf_op jit(solution)/shard_map/dot_general | solution.py:173
  137.4 2.7 copy-done.6
  140.2 3.1 slice.148
  143.2 6.8 %copy.142 = f32[1024,1536]{0,1:T(8,128)} copy(f32[1024,1536]{1,0:T(8,128)} %slice.148) | data formatting | bytes 12582912 | tf_op jit(solution)/shard_map/slice | solution.py:174
  150.0 0.8 slice_reduce_fusion
  152.2 1.2 reduce.17
  154.0 10.7 %all-to-all-start.1 = ((bf16[32,2,768]{2,1,0:T(2,128)(2,1)}), bf16[32,2,768]{2,1,0:T(2,128)(2,1)S(1)}, u32[]{:S(2)}, u32[]{:S(2)}) async-start(bf16[32,2,768]{2,1,0:T(2,128)(2,1)} %reshape.518), calls=%async_computation.1 | async-start | bytes 196608 | tf_op jit(solution)/shard_map/all_to_all | solution.py:197
  164.8 2.7 slice_bitcast_fusion
  167.5 1.2 subtract_convert_fusion
  168.8 4.8 %all-to-all-done.1 = bf16[32,2,768]{2,1,0:T(2,128)(2,1)S(1)} async-done(((bf16[32,2,768]{2,1,0:T(2,128)(2,1)}), bf16[32,2,768]{2,1,0:T(2,128)(2,1)S(1)}, u32[]{:S(2)}, u32[]{:S(2)}) %all-to-all-start.1) | async-done | bytes 98336 | tf_op jit(solution)/shard_map/all_to_all | solution.py:197
  174.1 5.6 %fusion.79 = f32[8,1,4096]{2,1,0:T(1,128)S(1)} fusion(bf16[8,4096,64]{2,1,0:T(8,128)(2,1)} %reshape.489, bf16[1,8,3,64]{3,2,1,0:T(4,128)(2,1)S(1)} %reshape.487), kind=kOutput, calls=%fused_computation.110 | convolution fusion | flops 4194304 | bytes 4329472 | tf_op jit(solution)/shard_map/shd,shtd->sht/dot_general | solution.py:211
  180.4 4.6 %fusion.67 = f32[8,1,64]{2,1,0:T(1,128)S(1)} fusion(bf16[8,4096,64]{2,1,0:T(8,128)(2,1)} %reshape.490, bf16[8,4096,1]{1,0,2:T(8,128)(2,1)S(1)} %fusion.73), kind=kOutput, calls=%fused_computation.86 | convolution fusion | flops 4194304 | bytes 4261888 | tf_op jit(solution)/shard_map/sht,shtd->shd/dot_general | solution.py:226
  185.1 0.8 reduce.18
  186.6 5.1 %all-to-all-start.2 = ((bf16[32,2,256]{2,1,0:T(2,128)(2,1)}), bf16[32,2,256]{2,1,0:T(2,128)(2,1)}, u32[]{:S(2)}, u32[]{:S(2)}) async-start(bf16[32,2,256]{2,1,0:T(2,128)(2,1)} %reshape.520), calls=%async_computation.2 | async-start | bytes 65536 | tf_op jit(solution)/shard_map/all_to_all | solution.py:230
  191.8 1.4 pad_maximum_fusion.3
  193.1 1.8 slice.274
  194.9 1.5 copy.144.query_ref
  196.4 1.3 copy.145.key_ref
  197.7 1.3 copy.146.value_ref
  199.1 13.9 %shard_map.140 = bf16[1024,512]{1,0:T(8,128)(2,1)} custom-call(s32[2]{0:T(128)} %lengths_ref.1, bf16[1024,512]{1,0:T(8,128)(2,1)} %copy.144.query_ref, bf16[1024,512]{1,0:T(8,128)(2,1)} %copy.145.key_ref, bf16[1024,512]{1,0:T(8,128)(2,1)} %copy.146.value_ref), custom_call_target="tpu_custom_call" | custom-call | tf_op jit(solution)/shard_map/pallas_call | solution.py:69
  213.0 0.8 reshape.521
  214.5 7.6 %fusion.54 = f32[1025,2048]{1,0:T(8,128)} fusion(bf16[2048,2048]{1,0:T(8,128)(2,1)} %all-gather.3.cloned.1.call-done, bf16[1,512]{1,0:T(2,128)(2,1)S(1)} %convert_element_type.264, bf16[1024,512]{1,0:T(8,128)(2,1)} %shard_map.140), kind=kOutput, calls=%fused_computation.46 | convolution fusion | flops 2151680000 | bytes 11543552 | tf_op jit(solution)/shard_map/dot_general | solution.py:237
  222.1 18.7 %fusion.31 = bf16[512,2048]{1,0:T(8,128)(2,1)} fusion(f32[1025,2048]{1,0:T(8,128)} %fusion.54, bf16[2048,4096]{1,0:T(8,128)(2,1)} %all-gather.5.cloned.1.call-done, bf16[1025,2048]{0,1:T(8,128)(2,1)} %fusion.3), kind=kOutput, calls=%fused_computation.39 | convolution fusion | flops 8601468928 | bytes 25165824 | tf_op jit(solution)/shard_map/dot_general | solution.py:248
  240.8 2.9 copy.155
  243.7 1.6 copy.156
  245.4 16.4 %fusion.22 = bf16[513,2048]{1,0:T(8,128)(2,1)S(1)} fusion(f32[1025,2048]{1,0:T(8,128)} %fusion.54, bf16[2048,4096]{1,0:T(8,128)(2,1)} %all-gather.5.cloned.1.call-done, bf16[1025,2048]{0,1:T(8,128)(2,1)} %fusion.3), kind=kOutput, calls=%fused_computation.29 | convolution fusion | flops 8618268672 | bytes 25759744 | tf_op jit(solution)/shard_map/dot_general | solution.py:248
  261.8 2.6 copy.157
  264.4 3.6 %copy.158 = bf16[2,2,513,32,16]{2,4,3,1,0:T(8,128)(2,1)} copy(bf16[2,2,513,32,16]{2,4,0,1,3:T(8,128)(2,1)} %bitcast.118) | data formatting | bytes 4202496 | tf_op jit(solution)/shard_map/transpose | solution.py:253
  268.6 13.7 %reduce-scatter.9.cloned.1.call-done = bf16[1,2,513,512]{2,3,1,0:T(8,128)(2,1)} async-done(((bf16[2,2,513,512]{2,3,1,0:T(8,128)(2,1)}), bf16[1,2,513,512]{2,3,1,0:T(8,128)(2,1)}) %reduce-scatter.9.cloned.1.call-update) | async-done | bytes 1050640 | tf_op jit(solution)/shard_map/reduce_scatter | solution.py:254
  282.3 26.0 %reduce-scatter.7.cloned.1.call-done = bf16[1,1,512,512]{2,3,1,0:T(8,128)(2,1)} async-done(((bf16[1,2,512,512]{2,3,1,0:T(8,128)(2,1)}), bf16[1,1,512,512]{2,3,1,0:T(8,128)(2,1)}) %reduce-scatter.7.cloned.1.call-update) | async-done | bytes 524304 | tf_op jit(solution)/shard_map/reduce_scatter | solution.py:255
  308.3 1.2 fusion.64
  309.5 27.8 %reduce-scatter.11.cloned.1.call-done = bf16[1,1,513,512]{2,3,1,0:T(8,128)(2,1)} async-done(((bf16[1,2,513,512]{2,3,1,0:T(8,128)(2,1)}), bf16[1,1,513,512]{2,3,1,0:T(8,128)(2,1)}) %reduce-scatter.11.cloned.1.call-update) | async-done | bytes 525328 | tf_op jit(solution)/shard_map/reduce_scatter | solution.py:255
  337.3 1.3 fusion.60
  338.7 1.3 copy.159
  (124 shorter events, 13.4 us)
Async XLA Ops:
  7.2 20.9 %copy-start.8 = (f32[16,8192]{1,0:T(8,128)S(1)}, f32[16,8192]{1,0:T(8,128)}, u32[]{:S(2)}) copy-start(f32[16,8192]{1,0:T(8,128)} %param.19) | copy-start | bytes 1572868
  7.2 21.1 %copy-start.9 = (f32[16,8192]{1,0:T(8,128)S(1)}, f32[16,8192]{1,0:T(8,128)}, u32[]{:S(2)}) copy-start(f32[16,8192]{1,0:T(8,128)} %param.20) | copy-start | bytes 1572868
  7.2 119.2 %all-gather.3.cloned.1.call-start = ((), (), s32[]{:S(2)}) async-start(), calls=%async_computation.8 | async-start | bytes 8912896 | tf_op jit(solution)/shard_map/all_gather | solution.py:114
  18.8 8.3 %collective-permute-start.3 = (bf16[64,2048]{1,0:T(8,128)(2,1)S(1)}, bf16[64,2048]{1,0:T(8,128)(2,1)S(1)}, u32[]{:S(2)}, u32[]{:S(2)}) collective-permute-start(bf16[64,2048]{1,0:T(8,128)(2,1)S(1)} %bitcast.128), channel_id=1, source_target_pairs={{0,1},{1,0},{2,3},{3,2},{4,5},{5,4},{6,7},{7,6},{8,9},{9,8},{10,11... | collective-permute-start | bytes 786440 | tf_op jit(solution)/shard_map/ppermute | solution.py:109
  28.0 194.1 %all-gather.5.cloned.1.call-start = ((), (), s32[]{:S(2)}) async-start(), calls=%async_computation.9 | async-start | bytes 17825792 | tf_op jit(solution)/shard_map/all_gather | solution.py:114
  28.5 27.9 %copy-start.7 = (bf16[1024,512]{1,0:T(8,128)(2,1)S(1)}, bf16[1024,512]{1,0:T(8,128)(2,1)}, u32[]{:S(2)}) copy-start(bf16[1024,512]{1,0:T(8,128)(2,1)} %param.13) | copy-start | bytes 3145732
  29.1 27.9 %copy-start.14 = (bf16[1,512]{1,0:T(2,128)(2,1)S(1)}, bf16[1,512]{1,0:T(2,128)(2,1)}, u32[]{:S(2)}) copy-start(bf16[1,512]{1,0:T(2,128)(2,1)} %param.14) | copy-start | bytes 3076
  41.3 13.9 %collective-permute-start.4 = (bf16[64,4096]{1,0:T(8,128)(2,1)S(1)}, bf16[64,4096]{1,0:T(8,128)(2,1)S(1)}, u32[]{:S(2)}, u32[]{:S(2)}) collective-permute-start(bf16[64,4096]{1,0:T(8,128)(2,1)S(1)} %bitcast.127), channel_id=1, source_target_pairs={{0,1},{1,0},{2,3},{3,2},{4,5},{5,4},{6,7},{7,6},{8,9},{9,8},{10,11... | collective-permute-start | bytes 1572872 | tf_op jit(solution)/shard_map/ppermute | solution.py:109
  56.4 5.9 %copy-start.13 = (f32[2048]{0:T(1024)S(1)}, f32[2048]{0:T(1024)}, u32[]{:S(2)}) copy-start(f32[2048]{0:T(1024)} %param.16) | copy-start | bytes 24580
  56.4 8.9 %copy-start.16 = (s32[32]{0:T(128)S(1)}, s32[32]{0:T(128)}, u32[]{:S(2)}) copy-start(s32[32]{0:T(128)} %param.24) | copy-start | bytes 388
  57.0 17.0 %copy-start = (bf16[1024,512]{0,1:T(8,128)(2,1)}, bf16[1024,512]{0,1:T(8,128)(2,1)S(1)}, u32[]{:S(2)}) copy-start(bf16[1024,512]{0,1:T(8,128)(2,1)S(1)} %copy.129) | copy-start | bytes 3145732
  58.8 45.7 %collective-permute-start = (bf16[1025,512]{1,0:T(8,128)(2,1)}, bf16[1025,512]{1,0:T(8,128)(2,1)}, u32[]{:S(2)}, u32[]{:S(2)}) collective-permute-start(bf16[1025,512]{1,0:T(8,128)(2,1)} %copy.132), channel_id=1, source_target_pairs={{0,32},{32,64},{64,96},{96,0},{1,33},{33,65},{65,97},{97,1},{2,34}... | collective-permute-start | bytes 3148808 | tf_op jit(solution)/shard_map/ppermute | solution.py:144
  61.1 47.0 %collective-permute-start.1 = (bf16[1025,512]{1,0:T(8,128)(2,1)}, bf16[1025,512]{1,0:T(8,128)(2,1)}, u32[]{:S(2)}, u32[]{:S(2)}) collective-permute-start(bf16[1025,512]{1,0:T(8,128)(2,1)} %copy.132), channel_id=1, source_target_pairs={{0,64},{32,96},{64,0},{96,32},{1,65},{33,97},{65,1},{97,33},{2,66}... | collective-permute-start | bytes 3148808 | tf_op jit(solution)/shard_map/ppermute | solution.py:144
  62.1 48.4 %collective-permute-start.2 = (bf16[1025,512]{1,0:T(8,128)(2,1)}, bf16[1025,512]{1,0:T(8,128)(2,1)}, u32[]{:S(2)}, u32[]{:S(2)}) collective-permute-start(bf16[1025,512]{1,0:T(8,128)(2,1)} %copy.132), channel_id=1, source_target_pairs={{0,96},{32,0},{64,32},{96,64},{1,97},{33,1},{65,33},{97,65},{2,98}... | collective-permute-start | bytes 3148808 | tf_op jit(solution)/shard_map/ppermute | solution.py:144
  115.5 1.7 copy-start.2
  115.5 1.7 copy-start.3
  115.5 1.8 copy-start.4
  115.5 2.1 copy-start.5
  121.6 1.0 copy-start.12
  137.4 2.7 copy-start.6
  143.2 7.8 %copy-start.15 = (f32[16]{0:T(128)S(1)}, f32[16]{0:T(128)}, u32[]{:S(2)}) copy-start(f32[16]{0:T(128)} %get-tuple-element.43) | copy-start | bytes 196
  154.0 19.6 %all-to-all-start.1 = ((bf16[32,2,768]{2,1,0:T(2,128)(2,1)}), bf16[32,2,768]{2,1,0:T(2,128)(2,1)S(1)}, u32[]{:S(2)}, u32[]{:S(2)}) async-start(bf16[32,2,768]{2,1,0:T(2,128)(2,1)} %reshape.518), calls=%async_computation.1 | async-start | bytes 196608 | tf_op jit(solution)/shard_map/all_to_all | solution.py:197
  164.7 2.7 copy-start.10
  164.7 2.7 copy-start.11
  167.5 6.3 %copy-start.17 = (s32[32]{0:T(128)S(1)}, s32[32]{0:T(128)}, u32[]{:S(2)}) copy-start(s32[32]{0:T(128)} %param.25) | copy-start | bytes 388
  186.6 26.4 %all-to-all-start.2 = ((bf16[32,2,256]{2,1,0:T(2,128)(2,1)}), bf16[32,2,256]{2,1,0:T(2,128)(2,1)}, u32[]{:S(2)}, u32[]{:S(2)}) async-start(bf16[32,2,256]{2,1,0:T(2,128)(2,1)} %reshape.520), calls=%async_computation.2 | async-start | bytes 65536 | tf_op jit(solution)/shard_map/all_to_all | solution.py:230
  191.7 76.3 %reduce-scatter.5.cloned.1.call-start = ((), (), s32[]{:S(2)}) async-start(), calls=%async_computation.10 | async-start | bytes 3145728 | tf_op jit(solution)/shard_map/reduce_scatter | solution.py:254
  245.3 36.9 %reduce-scatter.9.cloned.1.call-start = ((), (), s32[]{:S(2)}) async-start(), calls=%async_computation.12 | async-start | bytes 3932160 | tf_op jit(solution)/shard_map/reduce_scatter | solution.py:254
  264.4 43.9 %copy-start.1 = (bf16[1024,512]{0,1:T(8,128)(2,1)S(1)}, bf16[1024,512]{0,1:T(8,128)(2,1)}, u32[]{:S(2)}) copy-start(bf16[1024,512]{0,1:T(8,128)(2,1)} %copy-done) | copy-start | bytes 3145732
  268.0 40.3 %reduce-scatter.7.cloned.1.call-start = ((), (), s32[]{:S(2)}) async-start(), calls=%async_computation.11 | async-start | bytes 1572864 | tf_op jit(solution)/shard_map/reduce_scatter | solution.py:255
  268.6 68.7 %reduce-scatter.11.cloned.1.call-start = ((), (), s32[]{:S(2)}) async-start(), calls=%async_computation.13 | async-start | bytes 1966080 | tf_op jit(solution)/shard_map/reduce_scatter | solution.py:255
Sparse Core Ops, SparseCore 0:
  28.1 74.3 all-gather.2
  104.6 112.3 all-gather.4
  245.5 13.5 reduce-scatter.4
  268.1 14.1 reduce-scatter.8
  284.5 23.7 reduce-scatter.6
  310.6 26.6 reduce-scatter.10
